TPU v7x, 32 devices: a whole 2x2x4 slice. The times are simulated.
32 devices in a mesh: dp: 8 (over y, x, core), tensor: 4 (over z).
Axes of the slice: x: 2, y: 2, z: 4, core: 2. Of those that a mesh axis runs over, the one named last changes fastest.
Arguments:
- inputs: bfloat16 [16384, 768], P(('dp', 'tensor')), may hold values from -6 to 6
- prefix: int32 [16], P('dp'), may hold values from 102 to 512, as said below
- cotangent: bfloat16 [16384, 768], P(('dp', 'tensor')), may hold values from -6 to 6
- w_query: bfloat16 [768, 768], P('dp', 'tensor'), may hold values from -0.3125 to 0.3125
- w_key: bfloat16 [768, 768], P('dp', 'tensor'), may hold values from -0.3125 to 0.3125
- w_value: bfloat16 [768, 768], P('dp', 'tensor'), may hold values from -0.21875 to 0.21875
- w_out: bfloat16 [768, 768], P('tensor', 'dp'), may hold values from -0.875 to 0.875
- w_up: bfloat16 [768, 3072], P('dp', 'tensor'), may hold values from -0.21875 to 0.21875
- w_down: bfloat16 [3072, 768], P('tensor', 'dp'), may hold values from -0.109375 to 0.109375
- b_query: bfloat16 [768], replicated, may hold values from -3 to 3
- b_value: bfloat16 [768], replicated, may hold values from -3 to 3
- b_out: bfloat16 [768], replicated, may hold values from -2 to 2
- b_up: bfloat16 [3072], replicated, may hold values from -3 to 3
- b_down: bfloat16 [768], replicated, may hold values from -2 to 2
- gain_one: bfloat16 [768], replicated, may hold values from 0.25 to 1.75
- shift_one: bfloat16 [768], replicated, may hold values from -2 to 2
- gain_two: bfloat16 [768], replicated, may hold values from 0.25 to 1.75
- shift_two: bfloat16 [768], replicated, may hold values from -2 to 2
Outputs:
- output: bfloat16 [16384, 768], P(('dp', 'tensor'))
- grad_input: float32 [16384, 768], P(('dp', 'tensor'))
- grad_w_query: float32 [768, 768], P('dp', 'tensor')
- grad_w_key: float32 [768, 768], P('dp', 'tensor')
- grad_w_value: float32 [768, 768], P('dp', 'tensor')
- grad_w_out: float32 [768, 768], P('tensor', 'dp')
- grad_w_up: float32 [768, 3072], P('dp', 'tensor')
- grad_w_down: float32 [3072, 768], P('tensor', 'dp')
- grad_b_query: float32 [768], replicated
- grad_b_value: float32 [768], replicated
- grad_b_out: float32 [768], replicated
- grad_b_up: float32 [3072], replicated
- grad_b_down: float32 [768], replicated
- grad_gain_one: float32 [768], replicated
- grad_shift_one: float32 [768], replicated
- grad_gain_two: float32 [768], replicated
- grad_shift_two: float32 [768], replicated
Inputs may be any that keep to these rules, and one draw needn't show every extreme that they name: Every draw has a sequence whose prefix is exactly 512.
All inputs are finite; a program needn't handle non-finite values.
Results may differ from a plain program's by a relative error of at most 0.015.
Values may be sent and summed in bfloat16 or wider, within the bound.
No kernel may reach another device: no remote copies, remote signals or barrier semaphores. Data moves between devices by JAX's collectives and lax.ppermute only.
A program may use at most 192 MiB of HBM per device.

v0:
```python
import jax
import jax.numpy as jnp
from jax import lax
from jax.sharding import PartitionSpec as P


HEAD = 64
SEQ_LEN = 1024

norm_eps = 1e-12
masked_score = -1e30


def layer_norm(values, norm_gain, norm_shift):
    center = values - jnp.mean(values, axis=-1, keepdims=True)
    spread = jnp.mean(center * center, axis=-1, keepdims=True)
    return center * lax.rsqrt(spread + norm_eps) * norm_gain + norm_shift


def gelu_exact(values):
    return jax.nn.gelu(values, approximate=False)


def dot_right(first_op, second_op):
    return jnp.dot(first_op, second_op, preferred_element_type=jnp.float32)


def dot_back(first_op, second_op):
    return lax.dot_general(
        first_op, second_op, (((1,), (1,)), ((), ())), preferred_element_type=jnp.float32
    )


def dot_over_rows(first_op, second_op):
    return lax.dot_general(
        first_op, second_op, (((0,), (0,)), ((), ())), preferred_element_type=jnp.float32
    )


AXES = ("dp", "tensor")


def gather_joined(shards, dp, tp):
    r = shards[0].shape[0]
    joined = jnp.concatenate(shards, axis=1)
    full = lax.all_gather(joined, AXES, axis=0, tiled=False).reshape(dp, tp, r, -1)
    out = []
    start = 0
    for piece in shards:
        c = piece.shape[1]
        block = full[:, :, :, start : start + c]
        out.append(block.transpose(0, 2, 1, 3).reshape(dp * r, tp * c))
        start += c
    return out


LINK = jnp.bfloat16


def scatter_rows(grad, axis=0):
    return lax.psum_scatter(grad.astype(LINK), "dp", scatter_dimension=axis, tiled=True)


def scatter_cols_joined(pieces, tp):
    parts = []
    for piece in pieces:
        r, c = piece.shape
        parts.append(piece.reshape(r, tp, c // tp).transpose(1, 0, 2))
    joined = jnp.concatenate(parts, axis=2)
    mine = lax.psum_scatter(joined, "tensor", scatter_dimension=0, tiled=False).astype(jnp.float32)
    out = []
    start = 0
    for piece in pieces:
        c = piece.shape[1] // tp
        out.append(mine[:, start : start + c])
        start += c
    return out


def scores_of(queries, key_rows, qpos, kpos, prefix_len):
    scaling = HEAD ** (-0.5)
    scores = jnp.einsum("qhe,khe->hqk", queries, key_rows, preferred_element_type=jnp.float32) * scaling
    visible = (kpos[None, :] <= qpos[:, None]) | (kpos[None, :] < prefix_len)
    return jnp.where(visible[None], scores, masked_score)


def layer(
    inputs,
    prefix,
    cotangent,
    w_query,
    w_key,
    w_value,
    w_out,
    w_up,
    w_down,
    b_query,
    b_value,
    b_out,
    b_up,
    b_down,
    gain_one,
    shift_one,
    gain_two,
    shift_two,
):
    f32 = jnp.float32
    bf16 = jnp.bfloat16
    dp = lax.axis_size("dp")
    tp = lax.axis_size("tensor")
    t_index = lax.axis_index("tensor")
    rows = inputs.shape[0]
    pieces = SEQ_LEN // rows
    assert pieces == 2
    half = t_index % pieces
    seq_here = (t_index * rows) // SEQ_LEN
    prefix_len = lax.dynamic_index_in_dim(prefix, seq_here, keepdims=False)
    pos_own = half * rows + lax.iota(jnp.int32, rows)
    pos_oth = (1 - half) * rows + lax.iota(jnp.int32, rows)
    to_second = [(t, t + 1) for t in range(0, tp, 2)]
    to_first = [(t + 1, t) for t in range(0, tp, 2)]

    full_query, full_key, full_value, out_t = gather_joined([w_query, w_key, w_value, w_out.T], dp, tp)
    full_out = out_t.T
    full_up, down_t = gather_joined([w_up, w_down.T], dp, tp)
    full_down = down_t.T
    width = full_query.shape[1]
    heads = width // HEAD

    gain_first = gain_one.astype(f32)
    shift_first = shift_one.astype(f32)
    gain_second = gain_two.astype(f32)
    shift_second = shift_two.astype(f32)

    in_rows = inputs.astype(f32)
    normed_one = layer_norm(in_rows, gain_first, shift_first).astype(bf16)
    key_rows = dot_right(normed_one, full_key).astype(bf16)
    value_rows = (dot_right(normed_one, full_value) + b_value.astype(f32)).astype(bf16)
    queries = (dot_right(normed_one, full_query) + b_query.astype(f32)).astype(bf16)
    shape3 = (rows, heads, HEAD)
    q3 = queries.reshape(shape3)
    k3 = key_rows.reshape(shape3)
    v3 = value_rows.reshape(shape3)
    k_oth, v_oth = lax.ppermute((k3, v3), "tensor", to_second)

    s_own = scores_of(q3, k3, pos_own, pos_own, prefix_len)
    s_oth = scores_of(q3, k_oth, pos_own, pos_oth, prefix_len)
    row_top = jnp.maximum(jnp.max(s_own, axis=-1, keepdims=True), jnp.max(s_oth, axis=-1, keepdims=True))
    e_own = jnp.exp(s_own - row_top)
    e_oth = jnp.exp(s_oth - row_top)
    row_total = jnp.sum(e_own, axis=-1, keepdims=True) + jnp.sum(e_oth, axis=-1, keepdims=True)
    p_own = (e_own / row_total).astype(bf16)
    p_oth = (e_oth / row_total).astype(bf16)
    attended = jnp.einsum("hqk,khe->qhe", p_own, v3, preferred_element_type=f32) + jnp.einsum(
        "hqk,khe->qhe", p_oth, v_oth, preferred_element_type=f32
    )
    log_sums = row_top + jnp.log(row_total)
    attended = attended.reshape(rows, width).astype(bf16)
    q_rcv, lse_rcv = lax.ppermute((q3, log_sums), "tensor", to_first)

    middle = in_rows + dot_right(attended, full_out) + b_out.astype(f32)
    normed_two = layer_norm(middle, gain_second, shift_second).astype(bf16)
    pre_act = dot_right(normed_two, full_up) + b_up.astype(f32)
    activated = gelu_exact(pre_act).astype(bf16)
    result = (middle + dot_right(activated, full_down) + b_down.astype(f32)).astype(bf16)

    grad_result = cotangent.astype(f32)
    grad_act = dot_back(cotangent, full_down)
    grad_pre = jax.vjp(gelu_exact, pre_act)[1](grad_act)[0].astype(bf16)
    ffn_grad = lax.dot_general(
        jnp.stack([normed_two, cotangent]),
        jnp.stack([grad_pre, activated]),
        (((1,), (1,)), ((0,), (0,))),
        preferred_element_type=f32,
    )
    grad_norm_two = dot_back(grad_pre, full_up)
    ffn_grad, grad_norm_two = lax.optimization_barrier((ffn_grad, grad_norm_two))
    ffn_rows = scatter_rows(ffn_grad, axis=1)
    up_rows = ffn_rows[0]
    down_rows = ffn_rows[1]
    norm_two_back = jax.vjp(layer_norm, middle, gain_second, shift_second)[1](grad_norm_two)
    grad_middle = grad_result + norm_two_back[0]
    grad_attn_rows = grad_middle.astype(bf16)
    grad_attended = dot_back(grad_attn_rows, full_out).astype(bf16)
    do3 = grad_attended.reshape(shape3)

    scaling = HEAD ** (-0.5)
    prob_own = jnp.exp(s_own - log_sums)
    prob_oth = jnp.exp(s_oth - log_sums)
    dp_own = jnp.einsum("qhe,khe->hqk", do3, v3, preferred_element_type=f32)
    dp_oth = jnp.einsum("qhe,khe->hqk", do3, v_oth, preferred_element_type=f32)
    delta = jnp.sum(prob_own * dp_own, axis=-1, keepdims=True) + jnp.sum(
        prob_oth * dp_oth, axis=-1, keepdims=True
    )
    do_rcv, delta_rcv = lax.ppermute((do3, delta), "tensor", to_first)
    ds_own = (prob_own * (dp_own - delta)).astype(bf16)
    ds_oth = (prob_oth * (dp_oth - delta)).astype(bf16)
    dq = (
        jnp.einsum("hqk,khe->qhe", ds_own, k3, preferred_element_type=f32)
        + jnp.einsum("hqk,khe->qhe", ds_oth, k_oth, preferred_element_type=f32)
    ) * scaling
    dk = jnp.einsum("hqk,qhe->khe", ds_own, q3, preferred_element_type=f32)
    dv = jnp.einsum("hqk,qhe->khe", prob_own.astype(bf16), do3, preferred_element_type=f32)
    s_x = scores_of(q_rcv, k3, pos_oth, pos_own, prefix_len)
    prob_x = jnp.exp(s_x - lse_rcv)
    dp_x = jnp.einsum("qhe,khe->hqk", do_rcv, v3, preferred_element_type=f32)
    ds_x = (prob_x * (dp_x - delta_rcv)).astype(bf16)
    dk = (dk + jnp.einsum("hqk,qhe->khe", ds_x, q_rcv, preferred_element_type=f32)) * scaling
    dv = dv + jnp.einsum("hqk,qhe->khe", prob_x.astype(bf16), do_rcv, preferred_element_type=f32)

    grad_q = dq.reshape(rows, width).astype(bf16)
    grad_k = dk.reshape(rows, width).astype(bf16)
    grad_v = dv.reshape(rows, width).astype(bf16)
    grad_qkv = jnp.concatenate([grad_q, grad_k, grad_v], axis=1)
    attn_grad = jnp.concatenate(
        [dot_over_rows(normed_one, grad_qkv), dot_over_rows(grad_attn_rows, attended)], axis=1
    )
    attn_rows = scatter_rows(attn_grad)
    qkv_rows = attn_rows[:, : 3 * width]
    out_rows = attn_rows[:, 3 * width :]
    grad_norm_one = dot_back(grad_q, full_query) + dot_back(grad_k, full_key) + dot_back(grad_v, full_value)
    norm_one_back = jax.vjp(layer_norm, in_rows, gain_first, shift_first)[1](grad_norm_one)
    grad_input = grad_middle + norm_one_back[0]

    shard_query, shard_key, shard_value, shard_out_t, shard_up, shard_down_t = scatter_cols_joined(
        [qkv_rows[:, :width], qkv_rows[:, width : 2 * width], qkv_rows[:, 2 * width :], out_rows, up_rows, down_rows],
        tp,
    )
    shard_out = shard_out_t.T
    shard_down = shard_down_t.T
    vector_sums = lax.psum(
        (
        jnp.sum(grad_q, axis=0, dtype=f32),
        jnp.sum(grad_v, axis=0, dtype=f32),
        jnp.sum(grad_middle, axis=0),
        jnp.sum(grad_pre, axis=0, dtype=f32),
        jnp.sum(grad_result, axis=0),
        norm_one_back[1],
        norm_one_back[2],
        norm_two_back[1],
        norm_two_back[2],
        ),
        AXES,
    )
    return (
        result,
        grad_input,
        shard_query,
        shard_key,
        shard_value,
        shard_out,
        shard_up,
        shard_down,
    ) + tuple(vector_sums)


def solution(mesh):
    rows_spec = P(("dp", "tensor"), None)
    placed = (
        rows_spec,
        P("dp"),
        rows_spec,
        P("dp", "tensor"),
        P("dp", "tensor"),
        P("dp", "tensor"),
        P("tensor", "dp"),
        P("dp", "tensor"),
        P("tensor", "dp"),
    ) + (P(),) * 9
    return jax.shard_map(
        layer,
        mesh=mesh,
        in_specs=placed,
        out_specs=(
            rows_spec,
            rows_spec,
            P("dp", "tensor"),
            P("dp", "tensor"),
            P("dp", "tensor"),
            P("tensor", "dp"),
            P("dp", "tensor"),
            P("tensor", "dp"),
        )
        + (P(),) * 9,
        check_vma=False,
    )
```

profile of v0, /device:TPU:0, one launch (start us, length us, event | category | flops | bytes accessed | tf_op | source)
XLA Modules:
  0.0 567.9 jit_solution(3087959872192285096)
XLA Ops:
  23.3 54.4 %all-gather.5.cloned.1.call-done = bf16[3072,768]{1,0:T(8,128)(2,1)} async-done(((bf16[96,768]{1,0:T(8,128)(2,1)}), bf16[3072,768]{1,0:T(8,128)(2,1)}) %all-gather.5.cloned.1.call-update) | async-done | bytes 4718608 | tf_op jit(solution)/shard_map/all_gather | solution.py:46
  77.7 7.0 %slice_bitcast_fusion = (bf16[8,96,4,192]{3,1,2,0:T(8,128)(2,1)S(1)}, bf16[8,96,4,192]{3,1,2,0:T(8,128)(2,1)}, bf16[8,96,4,192]{3,1,2,0:T(8,128)(2,1)}, bf16[8,96,4,192]{3,1,2,0:T(8,128)(2,1)}) fusion(bf16[8,4,96,768]{3,2,1,0:T(8,128)(2,1)} %bitcast.157), kind=kLoop, calls=%fused_computation.87 | loop fusion | bytes 9437184 | tf_op jit(solution)/shard_map/transpose | solution.py:52
  86.5 3.9 reshape.381
  99.5 4.2 collective-permute-start
  106.5 3.8 reshape.377
  124.8 5.6 collective-permute-start.1
  133.7 4.6 fusion.4
  138.4 5.5 fusion.1
  145.8 4.4 fusion.32
  150.2 12.0 %collective-permute-done.1 = bf16[512,12,64]{0,2,1:T(8,128)(2,1)S(1)} collective-permute-done((bf16[512,12,64]{0,2,1:T(8,128)(2,1)}, bf16[512,12,64]{0,2,1:T(8,128)(2,1)S(1)}, u32[]{:S(2)}, u32[]{:S(2)}) %collective-permute-start.1) | collective-permute-done | bytes 786464 | tf_op jit(solution)/shard_map/ppermute | solution.py:144
  162.2 5.2 add_convert_fusion.3
  169.9 7.5 %fusion.97 = f32[12,512,512]{1,2,0:T(8,128)} fusion(bf16[512,12,64]{0,2,1:T(8,128)(2,1)} %collective-permute-done.2, bf16[512,12,64]{0,2,1:T(8,128)(2,1)S(1)} %bitcast.154), kind=kOutput, calls=%fused_computation.172 | convolution fusion | flops 402653184 | bytes 14155776 | tf_op jit(solution)/shard_map/qhe,khe->hqk/dot_general | solution.py:82
  177.4 6.7 %fusion.88 = (bf16[8,4,96,768]{3,2,1,0:T(8,128)(2,1)}, bf16[8,4,96,768]{3,2,1,0:T(8,128)(2,1)S(1)}) fusion(bf16[8,4,96,1536]{3,2,1,0:T(8,128)(2,1)} %bitcast.156), kind=kLoop, calls=%fused_computation.163 | loop fusion | bytes 18874368 | tf_op jit(solution)/shard_map/slice | solution.py:51
  184.1 6.0 %copy.112 = bf16[8,4,96,768]{3,1,2,0:T(4,128)(2,1)S(1)} copy(bf16[8,4,96,768]{3,2,1,0:T(8,128)(2,1)} %get-tuple-element.83) | data formatting | bytes 9437184
  191.2 4.1 copy.111
  196.3 18.4 %multiply_convert_fusion.3 = (bf16[512,3072]{1,0:T(8,128)(2,1)S(1)}, f32[512,3072]{1,0:T(8,128)}, f32[512,3072]{1,0:T(8,128)}) fusion(f32[3072]{0:T(1024)S(1)} %convert_element_type.169, bf16[768,3072]{1,0:T(8,128)(2,1)S(1)} %bitcast.164, f32[512,768]{1,0:T(8,128)S(1)} %get-tuple-element.110, f32[768]{0:T(1024)S(1)} %convert_element_type.167, ...), kind=kOutput, calls=%fused_computation.37 | convolution fusion | flops 2521694208 | bytes 22042624 | tf_op jit(solution)/shard_map/dot_general | solution.py:25
  214.7 9.4 %convert_reduce_fusion = (f32[3072]{0:T(1024)}, bf16[512,3072]{1,0:T(8,128)(2,1)S(1)}) fusion(f32[512,3072]{1,0:T(8,128)} %get-tuple-element.82, bf16[512,768]{1,0:T(8,128)(2,1)S(1)} %copy-done.19, bf16[768,3072]{1,0:T(8,128)(2,1)S(1)} %bitcast.162, f32[512,3072]{1,0:T(8,128)} %get-tuple-element.111, f32[3072]{0:T(1024)S(1)} %convert_element_type.169), kind=kOutput, calls=%fused_computation.35 | convolution fusion | flops 2442654720 | bytes 21258240 | tf_op jit(solution)/shard_map/dot_general | solution.py:29
  224.1 3.9 fusion.92
  228.0 8.4 %fusion.8 = bf16[2,768,3072]{2,1,0:T(8,128)(2,1)} fusion(bf16[1,512,3072]{2,1,0:T(8,128)(2,1)S(1)} %bitcast.185, bf16[1,512,3072]{2,1,0:T(8,128)(2,1)S(1)} %bitcast.186, bf16[1,512,768]{2,1,0:T(8,128)(2,1)S(1)} %bitcast.176, bf16[1,512,768]{2,1,0:T(8,128)(2,1)S(1)} %copy-done.22), kind=kOutput, calls=%fused_computation.22 | convolution fusion | flops 4835770368 | bytes 17301504 | tf_op jit(solution)/shard_map/dot_general | solution.py:170
  246.9 7.5 %fusion.6 = f32[12,64,512]{2,1,0:T(8,128)} fusion(bf16[512,12,64]{0,2,1:T(8,128)(2,1)S(1)} %bitcast.159, f32[12,512]{1,0:T(8,128)} %get-tuple-element.77, f32[12,512,512]{1,2,0:T(8,128)} %copy-done.1, pred[512,512]{0,1:T(8,128)(4,1)} %copy-done.4), kind=kOutput, calls=%fused_computation.21 | convolution fusion | flops 415236096 | bytes 15228928 | tf_op jit(solution)/shard_map/hqk,qhe->khe/dot_general | solution.py:203
  254.4 6.3 %fusion.93 = f32[12,512,512]{1,2,0:T(8,128)} fusion(bf16[512,12,64]{0,2,1:T(8,128)(2,1)S(1)} %bitcast.160, bf16[512,12,64]{0,2,1:T(8,128)(2,1)S(1)} %bitcast.168), kind=kOutput, calls=%fused_computation.168 | convolution fusion | flops 402653184 | bytes 14155776 | tf_op jit(solution)/shard_map/qhe,khe->hqk/dot_general | solution.py:190
  260.6 20.1 %multiply_reduce_fusion = (f32[12,512]{1,0:T(8,128)S(1)}, f32[12,512]{1,0:T(8,128)S(1)}, f32[12,512,512]{1,2,0:T(8,128)}) fusion(f32[12,512,512]{1,2,0:T(8,128)} %copy-done, f32[12,512]{1,0:T(8,128)} %get-tuple-element.77, pred[512,512]{0,1:T(8,128)(4,1)S(1)} %get-tuple-element.103, f32[12,512,512]{1,2,0:T(8,128)} %fusion.93, f32[12,512,512]{1,2,0:T(8,128)} %copy-done.1, ...), kind=kOutput, calls=%fused_computation.4 | convolution fusion | flops 434098176 | bytes 52502528 | tf_op jit(solution)/shard_map/qhe,khe->hqk/dot_general | solution.py:191
  280.8 10.1 %multiply_convert_fusion.2 = bf16[12,512,512]{1,2,0:T(8,128)(2,1)S(1)} fusion(f32[12,512,512]{1,2,0:T(8,128)} %fusion.93, f32[12,512]{1,0:T(8,128)S(1)} %add.253, f32[12,512]{1,0:T(8,128)} %get-tuple-element.77, f32[12,512,512]{1,2,0:T(8,128)} %copy-done.1, pred[512,512]{0,1:T(8,128)(4,1)} %copy-done.4), kind=kLoop, calls=%fused_computation.3 | loop fusion | flops 18874368 | bytes 31768576 | tf_op jit(solution)/shard_map/convert_element_type | solution.py:196
  292.1 13.3 %convert_reduce_fusion.4 = (f32[12,64]{1,0:T(8,128)S(1)}, bf16[12,64,512]{2,1,0:T(8,128)(2,1)}) fusion(f32[12,64,512]{2,1,0:T(8,128)S(1)} %fusion.94, bf16[512,12,64]{0,2,1:T(8,128)(2,1)} %collective-permute-done, f32[12,512,512]{1,2,0:T(8,128)} %get-tuple-element.112, f32[12,512,512]{1,2,0:T(8,128)} %copy-done, f32[12,512]{1,0:T(8,128)S(1)} %add.253, ...), kind=kOutput, calls=%fused_computation.96 | convolution fusion | flops 423492864 | bytes 28625920 | tf_op jit(solution)/shard_map/hqk,khe->qhe/dot_general | solution.py:200
  305.4 4.5 fusion.96
  313.7 9.4 %convert_reduce_fusion.3 = (f32[12,64]{1,0:T(8,128)}, bf16[12,64,512]{2,1,0:T(8,128)(2,1)}) fusion(f32[12,64,512]{2,1,0:T(8,128)S(1)} %copy-done.49, bf16[512,12,64]{0,2,1:T(8,128)(2,1)} %collective-permute-done.4, f32[12,512,512]{1,2,0:T(8,128)} %fusion.97, f32[12,512]{1,0:T(8,128)} %bitcast.25, pred[512,512]{0,1:T(8,128)(4,1)S(1)} %copy-done.25), kind=kOutput, calls=%fused_computation.95 | convolution fusion | flops 416808192 | bytes 16018432 | tf_op jit(solution)/shard_map/hqk,qhe->khe/dot_general | solution.py:209
  323.1 12.1 %multiply_convert_fusion.6 = bf16[12,64,512]{2,1,0:T(8,128)(2,1)} fusion(f32[12,64,512]{2,1,0:T(8,128)} %fusion.96, bf16[512,12,64]{0,2,1:T(8,128)(2,1)} %collective-permute-done.2, f32[12,512,512]{1,2,0:T(8,128)} %fusion.97, f32[12,512]{1,0:T(8,128)S(1)} %bitcast.184, f32[12,512]{1,0:T(8,128)} %bitcast.25, pred[512,512]{0,1:T(8,128)(4,1)S(1)} %copy-done.25, ...), kind=kOutput, calls=%fused_computation.100 | convolution fusion | flops 825360384 | bytes 17612800 | tf_op jit(solution)/shard_map/hqk,qhe->khe/dot_general | solution.py:208
  335.3 4.0 convolution_convert_fusion
  342.9 64.4 %reduce-scatter.4.cloned.1.call-done = bf16[96,3072]{1,0:T(8,128)(2,1)} async-done(((bf16[768,3072]{1,0:T(8,128)(2,1)}), bf16[96,3072]{1,0:T(8,128)(2,1)}) %reduce-scatter.4.cloned.1.call-update) | async-done | bytes 589840 | tf_op jit(solution)/shard_map/reduce_scatter | solution.py:61
  412.2 75.3 %reduce-scatter.6.cloned.1.call-done = bf16[2,96,3072]{2,1,0:T(8,128)(2,1)} async-done(((bf16[2,768,3072]{2,1,0:T(8,128)(2,1)}), bf16[2,96,3072]{2,1,0:T(8,128)(2,1)}) %reduce-scatter.6.cloned.1.call-update) | async-done | bytes 1179664 | tf_op jit(solution)/shard_map/reduce_scatter | solution.py:61
  502.9 6.1 %add_convert_fusion.1 = bf16[512,768]{1,0:T(8,128)(2,1)} fusion(f32[512,768]{1,0:T(8,128)S(1)} %get-tuple-element.110, bf16[512,3072]{1,0:T(8,128)(2,1)S(1)} %copy-done.46, bf16[768,3072]{1,0:T(8,128)(2,1)} %bitcast.163, f32[768]{0:T(1024)S(1)} %copy-done.44), kind=kOutput, calls=%fused_computation.103 | convolution fusion | flops 2417098752 | bytes 10226688 | tf_op jit(solution)/shard_map/dot_general | solution.py:25
  516.9 40.9 %all-reduce = (f32[768]{0:T(1024)}, f32[768]{0:T(1024)}, f32[768]{0:T(1024)}, f32[3072]{0:T(1024)}, f32[768]{0:T(1024)}, /*index=5*/f32[768]{0:T(1024)}, f32[768]{0:T(1024)}, f32[768]{0:T(1024)}, f32[768]{0:T(1024)}) all-reduce(f32[768]{0:T(1024)S(1)} %copy-done.37, ...), channel_id=1, replica_groups=mesh['dp'=8,'tensor'=4] {'dp','tensor'}, use_global_device_ids=true, to_apply=%region_18.19 | all-reduce | flops 9216 | bytes 73728 | tf_op jit(solution)/shard_map/psum | solution.py:231
  (201 shorter events, 104.2 us)
Async XLA Ops:
  7.2 70.5 %all-gather.5.cloned.1.call-start = ((), (), s32[]{:S(2)}) async-start(), calls=%async_computation.6 | async-start | bytes 4866048 | tf_op jit(solution)/shard_map/all_gather | solution.py:46
  9.8 167.6 %all-gather.7.cloned.1.call-start = ((), (), s32[]{:S(2)}) async-start(), calls=%async_computation.7 | async-start | bytes 9732096 | tf_op jit(solution)/shard_map/all_gather | solution.py:46
  11.6 395.8 %reduce-scatter.4.cloned.1.call-start = ((), (), s32[]{:S(2)}) async-start(), calls=%async_computation.3 | async-start | bytes 5308416 | tf_op jit(solution)/shard_map/reduce_scatter | solution.py:61
  12.3 108.4 %copy-start.26 = (f32[768]{0:T(1024)}, f32[768]{0:T(1024)S(1)}, u32[]{:S(2)}) copy-start(f32[768]{0:T(1024)S(1)} %convert_element_type.152) | copy-start | bytes 9220
  13.0 107.7 %copy-start.42 = (f32[768]{0:T(1024)}, f32[768]{0:T(1024)S(1)}, u32[]{:S(2)}) copy-start(f32[768]{0:T(1024)S(1)} %convert_element_type.153) | copy-start | bytes 9220
  20.4 100.3 %copy-start.28 = (f32[512]{0:T(512)}, f32[512]{0:T(512)S(1)}, u32[]{:S(2)}) copy-start(f32[512]{0:T(512)S(1)} %broadcast_multiply_fusion.1) | copy-start | bytes 6148
  21.9 55.8 %copy-start.33 = (f32[512]{0:T(512)}, f32[512]{0:T(512)S(1)}, u32[]{:S(2)}) copy-start(f32[512]{0:T(512)S(1)} %fusion.51) | copy-start | bytes 6148
  21.9 98.8 %copy-start.30 = (f32[512]{0:T(512)}, f32[512]{0:T(512)S(1)}, u32[]{:S(2)}) copy-start(f32[512]{0:T(512)S(1)} %fusion.61) | copy-start | bytes 6148
  23.3 122.5 %copy-start.4 = (pred[512,512]{0,1:T(8,128)(4,1)}, pred[512,512]{0,1:T(8,128)(4,1)S(1)}, u32[]{:S(2)}) copy-start(pred[512,512]{0,1:T(8,128)(4,1)S(1)} %get-tuple-element.104) | copy-start | bytes 786436
  86.5 9.7 %copy-start.2 = (bf16[512,768]{1,0:T(8,128)(2,1)S(1)}, bf16[512,768]{1,0:T(8,128)(2,1)}, u32[]{:S(2)}) copy-start(bf16[512,768]{1,0:T(8,128)(2,1)} %param.18) | copy-start | bytes 2359300
  96.3 10.2 %copy-start.15 = (bf16[768,768]{0,1:T(8,128)(2,1)}, bf16[768,768]{0,1:T(8,128)(2,1)S(1)}, u32[]{:S(2)}) copy-start(bf16[768,768]{0,1:T(8,128)(2,1)S(1)} %reshape.379) | copy-start | bytes 3538948
  99.5 34.2 %collective-permute-start = (bf16[512,12,64]{0,2,1:T(8,128)(2,1)S(1)}, bf16[512,12,64]{0,2,1:T(8,128)(2,1)}, u32[]{:S(2)}, u32[]{:S(2)}) collective-permute-start(bf16[512,12,64]{0,2,1:T(8,128)(2,1)S(1)} %bitcast.152), channel_id=1, source_target_pairs={{0,1},{2,3},{4,5},{6,7},{8,9},{10,11},{12,13},{14,15},{16,17},{18,... | collective-permute-start | bytes 2359304 | tf_op jit(solution)/shard_map/ppermute | solution.py:144
  113.6 56.3 %collective-permute-start.2 = (bf16[512,12,64]{0,2,1:T(8,128)(2,1)}, bf16[512,12,64]{0,2,1:T(8,128)(2,1)}, u32[]{:S(2)}, u32[]{:S(2)}) collective-permute-start(bf16[512,12,64]{0,2,1:T(8,128)(2,1)} %bitcast.6), channel_id=1, source_target_pairs={{1,0},{3,2},{5,4},{7,6},{9,8},{11,10},{13,12},{15,14},{17,16},{19,... | collective-permute-start | bytes 2359304 | tf_op jit(solution)/shard_map/ppermute | solution.py:159
  120.7 13.0 %copy-start.9 = (bf16[768,768]{0,1:T(8,128)(2,1)}, bf16[768,768]{0,1:T(8,128)(2,1)S(1)}, u32[]{:S(2)}) copy-start(bf16[768,768]{0,1:T(8,128)(2,1)S(1)} %reshape.375) | copy-start | bytes 3538948
  124.8 37.4 %collective-permute-start.1 = (bf16[512,12,64]{0,2,1:T(8,128)(2,1)}, bf16[512,12,64]{0,2,1:T(8,128)(2,1)S(1)}, u32[]{:S(2)}, u32[]{:S(2)}) collective-permute-start(bf16[512,12,64]{0,2,1:T(8,128)(2,1)} %bitcast.166), channel_id=1, source_target_pairs={{0,1},{2,3},{4,5},{6,7},{8,9},{10,11},{12,13},{14,15},{16,17},{18,... | collective-permute-start | bytes 2359304 | tf_op jit(solution)/shard_map/ppermute | solution.py:144
  133.7 12.1 %copy-start.1 = (f32[12,512,512]{1,2,0:T(8,128)}, f32[12,512,512]{1,2,0:T(8,128)S(1)}, u32[]{:S(2)}) copy-start(f32[12,512,512]{1,2,0:T(8,128)S(1)} %get-tuple-element.106) | copy-start | bytes 37748740
  138.3 23.9 %copy-start = (f32[12,512,512]{1,2,0:T(8,128)}, f32[12,512,512]{1,2,0:T(8,128)S(1)}, u32[]{:S(2)}) copy-start(f32[12,512,512]{1,2,0:T(8,128)S(1)} %get-tuple-element.108) | copy-start | bytes 37748740
  144.5 169.1 %collective-permute-start.3 = (f32[12,512,1]{1,0,2:T(8,128)}, f32[12,512,1]{1,0,2:T(8,128)}, u32[]{:S(2)}, u32[]{:S(2)}) collective-permute-start(f32[12,512,1]{1,0,2:T(8,128)} %bitcast.24), channel_id=1, source_target_pairs={{1,0},{3,2},{5,4},{7,6},{9,8},{11,10},{13,12},{15,14},{17,16},{19,... | collective-permute-start | bytes 73736 | tf_op jit(solution)/shard_map/ppermute | solution.py:159
  150.2 17.3 %copy-start.17 = (bf16[768,768]{0,1:T(8,128)(2,1)S(1)}, bf16[768,768]{0,1:T(8,128)(2,1)}, u32[]{:S(2)}) copy-start(bf16[768,768]{0,1:T(8,128)(2,1)} %reshape.381) | copy-start | bytes 3538948
  191.2 23.6 %copy-start.8 = (bf16[96,8,4,768]{3,1,2,0:T(8,128)(2,1)}, bf16[96,8,4,768]{3,1,2,0:T(8,128)(2,1)S(1)}, u32[]{:S(2)}) copy-start(bf16[96,8,4,768]{3,1,2,0:T(8,128)(2,1)S(1)} %copy.114) | copy-start | bytes 14155780
  196.3 18.5 %copy-start.19 = (bf16[512,768]{1,0:T(8,128)(2,1)S(1)}, bf16[512,768]{1,0:T(8,128)(2,1)}, u32[]{:S(2)}) copy-start(bf16[512,768]{1,0:T(8,128)(2,1)} %param.20) | copy-start | bytes 2359300
  214.7 13.3 %copy-start.45 = (bf16[512,3072]{1,0:T(8,128)(2,1)}, bf16[512,3072]{1,0:T(8,128)(2,1)S(1)}, u32[]{:S(2)}) copy-start(bf16[512,3072]{1,0:T(8,128)(2,1)S(1)} %get-tuple-element.81) | copy-start | bytes 9437188
  241.1 68.8 %copy-start.39 = (f32[512]{0:T(512)}, f32[512]{0:T(512)S(1)}, u32[]{:S(2)}) copy-start(f32[512]{0:T(512)S(1)} %negate_multiply_fusion.2) | copy-start | bytes 6148
  245.5 68.2 %collective-permute-start.4 = (bf16[512,12,64]{0,2,1:T(8,128)(2,1)S(1)}, bf16[512,12,64]{0,2,1:T(8,128)(2,1)}, u32[]{:S(2)}, u32[]{:S(2)}) collective-permute-start(bf16[512,12,64]{0,2,1:T(8,128)(2,1)S(1)} %bitcast.158), channel_id=1, source_target_pairs={{1,0},{3,2},{5,4},{7,6},{9,8},{11,10},{13,12},{15,14},{17,16},{19,... | collective-permute-start | bytes 2359304 | tf_op jit(solution)/shard_map/ppermute | solution.py:195
  311.9 11.2 %collective-permute-start.5 = (f32[12,512,1]{1,0,2:T(8,128)S(1)}, f32[12,512,1]{1,0,2:T(8,128)S(1)}, u32[]{:S(2)}, u32[]{:S(2)}) collective-permute-start(f32[12,512,1]{1,0,2:T(8,128)S(1)} %bitcast.181), channel_id=1, source_target_pairs={{1,0},{3,2},{5,4},{7,6},{9,8},{11,10},{13,12},{15,14},{17,16},{19,... | collective-permute-start | bytes 73736 | tf_op jit(solution)/shard_map/ppermute | solution.py:195
  323.1 12.2 %copy-start.3 = (bf16[512,768]{1,0:T(8,128)(2,1)S(1)}, bf16[512,768]{1,0:T(8,128)(2,1)}, u32[]{:S(2)}) copy-start(bf16[512,768]{1,0:T(8,128)(2,1)} %param.18) | copy-start | bytes 2359300
  323.1 12.2 %copy-start.27 = (f32[768]{0:T(1024)S(1)}, f32[768]{0:T(1024)}, u32[]{:S(2)}) copy-start(f32[768]{0:T(1024)} %copy-done.26) | copy-start | bytes 9220
  323.1 12.2 %copy-start.29 = (f32[512]{0:T(512)S(1)}, f32[512]{0:T(512)}, u32[]{:S(2)}) copy-start(f32[512]{0:T(512)} %copy-done.28) | copy-start | bytes 6148
  323.1 12.2 %copy-start.31 = (f32[512]{0:T(512)S(1)}, f32[512]{0:T(512)}, u32[]{:S(2)}) copy-start(f32[512]{0:T(512)} %copy-done.30) | copy-start | bytes 6148
  323.1 12.2 %copy-start.43 = (f32[768]{0:T(1024)S(1)}, f32[768]{0:T(1024)}, u32[]{:S(2)}) copy-start(f32[768]{0:T(1024)} %copy-done.42) | copy-start | bytes 9220
  342.1 145.3 %reduce-scatter.6.cloned.1.call-start = ((), (), s32[]{:S(2)}) async-start(), calls=%async_computation.4 | async-start | bytes 10616832 | tf_op jit(solution)/shard_map/reduce_scatter | solution.py:61
  342.7 215.0 %reduce-scatter.8.cloned.1.call-start = ((), (), s32[]{:S(2)}) async-start(), calls=%async_computation.5 | async-start | bytes 2211840 | tf_op jit(solution)/shard_map/reduce_scatter | solution.py:70
  (29 other events, 129.1 us)
Sparse Core Ops, SparseCore 0:
  11.4 66.2 all-gather.4
  81.1 93.9 all-gather.6
  342.3 65.0 reduce-scatter.3
  410.7 76.6 reduce-scatter.5
  497.4 38.4 reduce-scatter.7
where the time goes:
time: 578 us; the launch traced here: 568 us
  waiting for transfers between devices  207 us (36%)
  matrix products  168 us (29%)
  local copies, waits for them, and re-layouts  77.1 us (13%)
  other arithmetic  44 us (8%)
  blocking collectives  40.9 us (7%)
  starting transfers between devices  15.9 us (3%)
  between operations  14.8 us (3%)
    reduce_scatter x2, waiting for transfers between devices, scatter_rows(): lax.psum_scatter(grad.astype(LINK), 'dp', scatter_dimension=axis, tiled=T...  140 us
    all_gather x2, waiting for transfers between devices, gather_joined(): lax.all_gather(joined, AXES, axis=0, tiled=False).reshape(dp, tp, r, -1)  54.4 us
    psum x1, blocking collectives, layer(): lax.psum((jnp.sum(grad_q, axis=0, dtype=f32), jnp.sum(grad_v, axis=0, dty...  40.9 us
    dot_general x6, matrix products, dot_right(): return jnp.dot(first_op, second_op, preferred_element_type=jnp.float32)  31.2 us
    dot_general x6, matrix products, dot_back(): lax.dot_general(first_op, second_op, (((1,), (1,)), ((), ())), preferred_...  23.5 us
    dot_general x1, matrix products, layer(): dp_oth = jnp.einsum('qhe,khe->hqk', do3, v_oth, preferred_element_type=f32)  20.1 us
    transpose x5, local copies, waits for them, and re-layouts, gather_joined(): out.append(block.transpose(0, 2, 1, 3).reshape(dp * r, tp * c))  17.3 us
    dot_general x3, matrix products, scores_of(): jnp.einsum('qhe,khe->hqk', queries, key_rows, preferred_element_type=jnp....  15.3 us
  transfers between devices with their start and end apart: 11, of which 4 were waited for; matrix products, arithmetic and copies ran while one was open for 45% of the time, Pallas kernels for 0%

commit v1 on v0

--- a/solution.py
+++ b/solution.py
@@ -2,6 +2,9 @@
 import jax.numpy as jnp
 from jax import lax
 from jax.sharding import PartitionSpec as P
+
+from jax.experimental import pallas as pl
+from jax.experimental.pallas import tpu as pltpu
 
 
 HEAD = 64
@@ -77,11 +80,134 @@
     return out
 
 
-def scores_of(queries, key_rows, qpos, kpos, prefix_len):
-    scaling = HEAD ** (-0.5)
-    scores = jnp.einsum("qhe,khe->hqk", queries, key_rows, preferred_element_type=jnp.float32) * scaling
-    visible = (kpos[None, :] <= qpos[:, None]) | (kpos[None, :] < prefix_len)
-    return jnp.where(visible[None], scores, masked_score)
+NT = (((1,), (1,)), ((), ()))
+LANES = 128
+
+
+def attn_fwd_kernel(meta_ref, q_ref, k_ref, v_ref, ko_ref, vo_ref, o_ref, of_ref, lse_ref):
+    half = meta_ref[0]
+    prefix_len = meta_ref[1]
+    rows = q_ref.shape[1]
+    scale = HEAD ** (-0.5)
+    q = q_ref[0]
+    s = lax.dot_general(q, k_ref[0], NT, preferred_element_type=jnp.float32) * scale
+    row = lax.broadcasted_iota(jnp.int32, s.shape, 0)
+    col = lax.broadcasted_iota(jnp.int32, s.shape, 1)
+    visible = (col <= row) | (half * rows + col < prefix_len)
+    s = jnp.where(visible, s, masked_score)
+    so = lax.dot_general(q, ko_ref[0], NT, preferred_element_type=jnp.float32) * scale
+    so = jnp.where(half == 1, so, masked_score)
+    top = jnp.maximum(jnp.max(s, axis=1, keepdims=True), jnp.max(so, axis=1, keepdims=True))
+    e = jnp.exp(s - top)
+    eo = jnp.exp(so - top)
+    total = jnp.sum(e, axis=1, keepdims=True) + jnp.sum(eo, axis=1, keepdims=True)
+    inv = 1.0 / total
+    p = (e * inv).astype(jnp.bfloat16)
+    po = (eo * inv).astype(jnp.bfloat16)
+    o = jnp.dot(p, v_ref[0], preferred_element_type=jnp.float32) + jnp.dot(
+        po, vo_ref[0], preferred_element_type=jnp.float32
+    )
+    o_ref[0] = o.astype(o_ref.dtype)
+    of_ref[0] = o
+    lse_ref[0] = jnp.broadcast_to(top + jnp.log(total), (rows, LANES))
+
+
+def attn_bwd_kernel(
+    meta_ref, q_ref, k_ref, v_ref, do_ref, lse_ref, dl_ref, ko_ref, vo_ref, qr_ref, dor_ref, lser_ref, dlr_ref,
+    dq_ref, dk_ref, dv_ref,
+):
+    f32 = jnp.float32
+    bf16 = jnp.bfloat16
+    half = meta_ref[0]
+    prefix_len = meta_ref[1]
+    rows = q_ref.shape[1]
+    reps = rows // LANES
+    scale = HEAD ** (-0.5)
+    q = q_ref[0]
+    k = k_ref[0]
+    v = v_ref[0]
+    do = do_ref[0]
+    s = lax.dot_general(q, k, NT, preferred_element_type=f32) * scale
+    row = lax.broadcasted_iota(jnp.int32, s.shape, 0)
+    col = lax.broadcasted_iota(jnp.int32, s.shape, 1)
+    visible = (col <= row) | (half * rows + col < prefix_len)
+    s = jnp.where(visible, s, masked_score)
+    p = jnp.exp(s - jnp.tile(lse_ref[0], (1, reps)))
+    dp = lax.dot_general(do, v, NT, preferred_element_type=f32)
+    ds = (p * (dp - jnp.tile(dl_ref[0], (1, reps)))).astype(bf16)
+    dq = jnp.dot(ds, k, preferred_element_type=f32)
+    dk = jnp.dot(ds.T, q, preferred_element_type=f32)
+    dv = jnp.dot(p.astype(bf16).T, do, preferred_element_type=f32)
+    second = half == 1
+    xq = jnp.where(second, q, qr_ref[0])
+    xdo = jnp.where(second, do, dor_ref[0])
+    xlse = jnp.tile(jnp.where(second, lse_ref[0], lser_ref[0]), (1, reps))
+    xdl = jnp.tile(jnp.where(second, dl_ref[0], dlr_ref[0]), (1, reps))
+    xk = jnp.where(second, ko_ref[0], k)
+    xv = jnp.where(second, vo_ref[0], v)
+    s2 = lax.dot_general(xq, xk, NT, preferred_element_type=f32) * scale
+    p2 = jnp.exp(s2 - xlse)
+    dp2 = lax.dot_general(xdo, xv, NT, preferred_element_type=f32)
+    ds2 = (p2 * (dp2 - xdl)).astype(bf16)
+    dq_x = jnp.dot(ds2, xk, preferred_element_type=f32)
+    dk_x = jnp.dot(ds2.T, xq, preferred_element_type=f32)
+    dv_x = jnp.dot(p2.astype(bf16).T, xdo, preferred_element_type=f32)
+    dq = dq + jnp.where(second, dq_x, 0.0)
+    dk = dk + jnp.where(second, 0.0, dk_x)
+    dv = dv + jnp.where(second, 0.0, dv_x)
+    dq_ref[0] = (dq * scale).astype(dq_ref.dtype)
+    dk_ref[0] = (dk * scale).astype(dk_ref.dtype)
+    dv_ref[0] = dv.astype(dv_ref.dtype)
+
+
+def head_spec(shape):
+    return pl.BlockSpec((1,) + tuple(shape[1:]), lambda h, meta: (h, 0, 0))
+
+
+def attention_forward(meta, q, k, v, ko, vo):
+    heads, rows, size = q.shape
+    spec = head_spec(q.shape)
+    lse_spec = head_spec((heads, rows, LANES))
+    return pl.pallas_call(
+        attn_fwd_kernel,
+        out_shape=(
+            jax.ShapeDtypeStruct(q.shape, jnp.bfloat16),
+            jax.ShapeDtypeStruct(q.shape, jnp.float32),
+            jax.ShapeDtypeStruct((heads, rows, LANES), jnp.float32),
+        ),
+        grid_spec=pltpu.PrefetchScalarGridSpec(
+            num_scalar_prefetch=1,
+            grid=(heads,),
+            in_specs=[spec] * 5,
+            out_specs=(spec, spec, lse_spec),
+        ),
+        cost_estimate=pl.CostEstimate(
+            flops=8 * heads * rows * rows * size,
+            transcendentals=2 * heads * rows * rows,
+            bytes_accessed=5 * q.size * 2 + q.size * 6 + heads * rows * LANES * 4,
+        ),
+    )(meta, q, k, v, ko, vo)
+
+
+def attention_backward(meta, q, k, v, do, lse, dl, ko, vo, qr, dor, lser, dlr):
+    heads, rows, size = q.shape
+    spec = head_spec(q.shape)
+    lse_spec = head_spec(lse.shape)
+    return pl.pallas_call(
+        attn_bwd_kernel,
+        out_shape=tuple(jax.ShapeDtypeStruct(q.shape, jnp.bfloat16) for _ in range(3)),
+        grid_spec=pltpu.PrefetchScalarGridSpec(
+            num_scalar_prefetch=1,
+            grid=(heads,),
+            in_specs=[spec, spec, spec, spec, lse_spec, lse_spec, spec, spec, spec, spec, lse_spec, lse_spec],
+            out_specs=(spec, spec, spec),
+        ),
+        cost_estimate=pl.CostEstimate(
+            flops=20 * heads * rows * rows * size,
+            transcendentals=2 * heads * rows * rows,
+            bytes_accessed=11 * q.size * 2 + 4 * lse.size * 4,
+        ),
+    )(meta, q, k, v, do, lse, dl, ko, vo, qr, dor, lser, dlr)
 
 
 def layer(
@@ -115,8 +241,6 @@
     half = t_index % pieces
     seq_here = (t_index * rows) // SEQ_LEN
     prefix_len = lax.dynamic_index_in_dim(prefix, seq_here, keepdims=False)
-    pos_own = half * rows + lax.iota(jnp.int32, rows)
-    pos_oth = (1 - half) * rows + lax.iota(jnp.int32, rows)
     to_second = [(t, t + 1) for t in range(0, tp, 2)]
     to_first = [(t + 1, t) for t in range(0, tp, 2)]
 
@@ -137,26 +261,18 @@
     key_rows = dot_right(normed_one, full_key).astype(bf16)
     value_rows = (dot_right(normed_one, full_value) + b_value.astype(f32)).astype(bf16)
     queries = (dot_right(normed_one, full_query) + b_query.astype(f32)).astype(bf16)
-    shape3 = (rows, heads, HEAD)
-    q3 = queries.reshape(shape3)
-    k3 = key_rows.reshape(shape3)
-    v3 = value_rows.reshape(shape3)
+
+    def by_heads(x):
+        return x.reshape(rows, heads, HEAD).transpose(1, 0, 2)
+
+    meta = jnp.stack([half, prefix_len]).astype(jnp.int32)
+    q3 = by_heads(queries)
+    k3 = by_heads(key_rows)
+    v3 = by_heads(value_rows)
     k_oth, v_oth = lax.ppermute((k3, v3), "tensor", to_second)
-
-    s_own = scores_of(q3, k3, pos_own, pos_own, prefix_len)
-    s_oth = scores_of(q3, k_oth, pos_own, pos_oth, prefix_len)
-    row_top = jnp.maximum(jnp.max(s_own, axis=-1, keepdims=True), jnp.max(s_oth, axis=-1, keepdims=True))
-    e_own = jnp.exp(s_own - row_top)
-    e_oth = jnp.exp(s_oth - row_top)
-    row_total = jnp.sum(e_own, axis=-1, keepdims=True) + jnp.sum(e_oth, axis=-1, keepdims=True)
-    p_own = (e_own / row_total).astype(bf16)
-    p_oth = (e_oth / row_total).astype(bf16)
-    attended = jnp.einsum("hqk,khe->qhe", p_own, v3, preferred_element_type=f32) + jnp.einsum(
-        "hqk,khe->qhe", p_oth, v_oth, preferred_element_type=f32
-    )
-    log_sums = row_top + jnp.log(row_total)
-    attended = attended.reshape(rows, width).astype(bf16)
-    q_rcv, lse_rcv = lax.ppermute((q3, log_sums), "tensor", to_first)
+    o_heads, o_full, lse_wide = attention_forward(meta, q3, k3, v3, k_oth, v_oth)
+    attended = o_heads.transpose(1, 0, 2).reshape(rows, width)
+    q_rcv, lse_rcv = lax.ppermute((q3, lse_wide[:, :, 0]), "tensor", to_first)
 
     middle = in_rows + dot_right(attended, full_out) + b_out.astype(f32)
     normed_two = layer_norm(middle, gain_second, shift_second).astype(bf16)
@@ -182,35 +298,24 @@
     grad_middle = grad_result + norm_two_back[0]
     grad_attn_rows = grad_middle.astype(bf16)
     grad_attended = dot_back(grad_attn_rows, full_out).astype(bf16)
-    do3 = grad_attended.reshape(shape3)
-
-    scaling = HEAD ** (-0.5)
-    prob_own = jnp.exp(s_own - log_sums)
-    prob_oth = jnp.exp(s_oth - log_sums)
-    dp_own = jnp.einsum("qhe,khe->hqk", do3, v3, preferred_element_type=f32)
-    dp_oth = jnp.einsum("qhe,khe->hqk", do3, v_oth, preferred_element_type=f32)
-    delta = jnp.sum(prob_own * dp_own, axis=-1, keepdims=True) + jnp.sum(
-        prob_oth * dp_oth, axis=-1, keepdims=True
-    )
+
+    do3 = by_heads(grad_attended)
+    delta = jnp.sum(do3.astype(f32) * o_full, axis=-1)
     do_rcv, delta_rcv = lax.ppermute((do3, delta), "tensor", to_first)
-    ds_own = (prob_own * (dp_own - delta)).astype(bf16)
-    ds_oth = (prob_oth * (dp_oth - delta)).astype(bf16)
-    dq = (
-        jnp.einsum("hqk,khe->qhe", ds_own, k3, preferred_element_type=f32)
-        + jnp.einsum("hqk,khe->qhe", ds_oth, k_oth, preferred_element_type=f32)
-    ) * scaling
-    dk = jnp.einsum("hqk,qhe->khe", ds_own, q3, preferred_element_type=f32)
-    dv = jnp.einsum("hqk,qhe->khe", prob_own.astype(bf16), do3, preferred_element_type=f32)
-    s_x = scores_of(q_rcv, k3, pos_oth, pos_own, prefix_len)
-    prob_x = jnp.exp(s_x - lse_rcv)
-    dp_x = jnp.einsum("qhe,khe->hqk", do_rcv, v3, preferred_element_type=f32)
-    ds_x = (prob_x * (dp_x - delta_rcv)).astype(bf16)
-    dk = (dk + jnp.einsum("hqk,qhe->khe", ds_x, q_rcv, preferred_element_type=f32)) * scaling
-    dv = dv + jnp.einsum("hqk,qhe->khe", prob_x.astype(bf16), do_rcv, preferred_element_type=f32)
-
-    grad_q = dq.reshape(rows, width).astype(bf16)
-    grad_k = dk.reshape(rows, width).astype(bf16)
-    grad_v = dv.reshape(rows, width).astype(bf16)
+
+    def wide(x):
+        return jnp.broadcast_to(x[:, :, None], x.shape + (LANES,))
+
+    dq3, dk3, dv3 = attention_backward(
+        meta, q3, k3, v3, do3, lse_wide, wide(delta), k_oth, v_oth, q_rcv, do_rcv, wide(lse_rcv), wide(delta_rcv)
+    )
+
+    def by_rows(x):
+        return x.transpose(1, 0, 2).reshape(rows, width)
+
+    grad_q = by_rows(dq3)
+    grad_k = by_rows(dk3)
+    grad_v = by_rows(dv3)
     grad_qkv = jnp.concatenate([grad_q, grad_k, grad_v], axis=1)
     attn_grad = jnp.concatenate(
         [dot_over_rows(normed_one, grad_qkv), dot_over_rows(grad_attn_rows, attended)], axis=1

time: 578 us -> 575 us (level)
  matrix products: 168 us -> 68.9 us
  local copies, waits for them, and re-layouts: 77.1 us -> 137 us
  Pallas kernels: 0 us -> 46.9 us
  other arithmetic: 44 us -> 29.7 us
  waiting for transfers between devices: 207 us -> 217 us
    dot_general x13 -> x0, matrix products: 99.3 us -> none  [the longest x1 20.1 us: layer(): dp_oth = jnp.einsum('qhe,khe->hqk', do3, v_oth, preferred_element_type=f32)]
    pallas_call x0 -> x2, Pallas kernels: none -> 46.9 us  [the longest x1 24.6 us: attention_backward(): pl.pallas_call(attn_bwd_kernel, out_shape=tuple((jax.ShapeDtypeStruct(q.s...]
    transpose x0 -> x7, local copies, waits for them, and re-layouts: none -> 16.2 us  [the longest x3 7.24 us: by_rows(): return x.transpose(1, 0, 2).reshape(rows, width)]
    reduce_scatter x2, waiting for transfers between devices: 140 us -> 129 us  [scatter_rows(): lax.psum_scatter(grad.astype(LINK), 'dp', scatter_dimension=axis, tiled=T...]
    convert_element_type x1 -> x0, other arithmetic: 10.1 us -> none  [layer(): ds_own = (prob_own * (dp_own - delta)).astype(bf16)]
    ppermute x0 -> x4, local copies, waits for them, and re-layouts: none -> 10 us  [the longest x2 5.05 us: layer(): k_oth, v_oth = lax.ppermute((k3, v3), 'tensor', to_second)]
    reshape x0 -> x4, local copies, waits for them, and re-layouts: none -> 9.99 us  [by_heads(): return x.reshape(rows, heads, HEAD).transpose(1, 0, 2)]
    ppermute x2, waiting for transfers between devices: 12 us -> 21.2 us  [layer(): k_oth, v_oth = lax.ppermute((k3, v3), 'tensor', to_second)]
  transfers between devices with their start and end apart: 11 -> 11, of which waited for: 4 -> 5; matrix products, arithmetic and copies ran while one was open for 45% -> 33% of each run, Pallas kernels for 0% -> 4%
where the time goes in v1:
time: 575 us; the launch traced here: 567 us
  waiting for transfers between devices  217 us (38%)
  local copies, waits for them, and re-layouts  137 us (24%)
  matrix products  68.9 us (12%)
  Pallas kernels  46.9 us (8%)
  blocking collectives  41.4 us (7%)
  other arithmetic  29.7 us (5%)
  between operations  14.8 us (3%)
  starting transfers between devices  12.1 us (2%)
    reduce_scatter x2, waiting for transfers between devices, scatter_rows(): lax.psum_scatter(grad.astype(LINK), 'dp', scatter_dimension=axis, tiled=T...  129 us
    all_gather x2, waiting for transfers between devices, gather_joined(): lax.all_gather(joined, AXES, axis=0, tiled=False).reshape(dp, tp, r, -1)  62.2 us
    psum x1, blocking collectives, layer(): lax.psum((jnp.sum(grad_q, axis=0, dtype=f32), jnp.sum(grad_v, axis=0, dty...  41.4 us
    dot_general x6, matrix products, dot_right(): return jnp.dot(first_op, second_op, preferred_element_type=jnp.float32)  35.2 us
    pallas_call x1, Pallas kernels, attention_backward(): pl.pallas_call(attn_bwd_kernel, out_shape=tuple((jax.ShapeDtypeStruct(q.s...  24.6 us
    pallas_call x1, Pallas kernels, attention_forward(): pl.pallas_call(attn_fwd_kernel, out_shape=(jax.ShapeDtypeStruct(q.shape,...  22.2 us
    ppermute x2, waiting for transfers between devices, layer(): k_oth, v_oth = lax.ppermute((k3, v3), 'tensor', to_second)  21.2 us
    dot_general x6, matrix products, dot_back(): lax.dot_general(first_op, second_op, (((1,), (1,)), ((), ())), preferred_...  19.2 us
  transfers between devices with their start and end apart: 11, of which 5 were waited for; matrix products, arithmetic and copies ran while one was open for 33% of the time, Pallas kernels for 4%

profile of v1, /device:TPU:0, one launch (start us, length us, event | category | flops | bytes accessed | tf_op | source)
XLA Modules:
  0.0 567.2 jit_solution(14276431816790861481)
XLA Ops:
  15.5 62.2 %all-gather.5.cloned.1.call-done = bf16[3072,768]{1,0:T(8,128)(2,1)} async-done(((bf16[96,768]{1,0:T(8,128)(2,1)}), bf16[3072,768]{1,0:T(8,128)(2,1)}) %all-gather.5.cloned.1.call-update) | async-done | bytes 4718608 | tf_op jit(solution)/shard_map/all_gather | solution.py:49
  77.7 7.1 %slice_bitcast_fusion = (bf16[8,96,4,192]{3,1,2,0:T(8,128)(2,1)S(1)}, bf16[8,96,4,192]{3,1,2,0:T(8,128)(2,1)}, bf16[8,96,4,192]{3,1,2,0:T(8,128)(2,1)}, bf16[8,96,4,192]{3,1,2,0:T(8,128)(2,1)}) fusion(bf16[8,4,96,768]{3,2,1,0:T(8,128)(2,1)} %bitcast.135), kind=kLoop, calls=%fused_computation.60 | loop fusion | bytes 9437184 | tf_op jit(solution)/shard_map/transpose | solution.py:55
  84.8 2.8 copy.79
  87.6 3.0 reshape.173
  94.7 2.8 copy.82
  97.5 2.9 reshape.175
  105.3 4.2 collective-permute-start
  122.3 3.8 reshape.171
  126.1 3.1 add_convert_fusion.3
  140.8 3.8 reshape.178
  148.4 21.2 %collective-permute-done.1 = bf16[12,512,64]{1,2,0:T(8,128)(2,1)} collective-permute-done((bf16[12,512,64]{1,2,0:T(8,128)(2,1)}, bf16[12,512,64]{1,2,0:T(8,128)(2,1)}, u32[]{:S(2)}, u32[]{:S(2)}) %collective-permute-start.1) | collective-permute-done | bytes 786464 | tf_op jit(solution)/shard_map/ppermute | solution.py:272
  172.2 22.2 %shard_map.305 = (bf16[12,512,64]{2,1,0:T(8,128)(2,1)}, f32[12,512,64]{2,1,0:T(8,128)}, f32[12,512,128]{2,1,0:T(8,128)}) custom-call(s32[2]{0:T(128)} %pad_add_fusion.meta_ref, bf16[12,512,64]{2,1,0:T(8,128)(2,1)} %bitcast.138, bf16[12,512,64]{2,1,0:T(8,128)(2,1)} %bitcast.140, bf16[12,512,64]{2,1,0:T(8,128)(2,1)} %bitcast.142, ...), custom_call_target="tpu_custom_call" | custom-call | flops 1610612736 | bytes 9437184 | tf_op jit(solution)/shard_map/pallas_call | solution.py:171
  202.4 6.8 %fusion.54 = (bf16[8,4,96,768]{3,2,1,0:T(8,128)(2,1)S(1)}, bf16[8,4,96,768]{3,2,1,0:T(8,128)(2,1)}) fusion(bf16[8,4,96,1536]{3,2,1,0:T(8,128)(2,1)} %bitcast.134), kind=kLoop, calls=%fused_computation.111 | loop fusion | bytes 18874368 | tf_op jit(solution)/shard_map/slice | solution.py:54
  209.2 6.0 %copy.123 = bf16[8,4,96,768]{3,1,2,0:T(4,128)(2,1)S(1)} copy(bf16[8,4,96,768]{3,2,1,0:T(8,128)(2,1)} %get-tuple-element.107) | data formatting | bytes 9437184
  216.3 3.6 copy.124
  221.1 18.5 %multiply_convert_fusion = (bf16[512,3072]{1,0:T(8,128)(2,1)S(1)}, f32[512,3072]{1,0:T(8,128)}, f32[512,3072]{1,0:T(8,128)}) fusion(f32[3072]{0:T(1024)S(1)} %copy-done.35, bf16[768,3072]{1,0:T(8,128)(2,1)S(1)} %bitcast.146, f32[512,768]{1,0:T(8,128)S(1)} %get-tuple-element.126, f32[768]{0:T(1024)S(1)} %copy-done.32, f32[768]{0:T(1024)S(1)} %convert_element_type.97, ...), kind=kOutput, calls=%fused_computation.16 | convolution fusion | flops 2521694208 | bytes 22042624 | tf_op jit(solution)/shard_map/dot_general | solution.py:28
  239.6 9.5 %convert_reduce_fusion = (f32[3072]{0:T(1024)}, bf16[512,3072]{1,0:T(8,128)(2,1)S(1)}) fusion(f32[512,3072]{1,0:T(8,128)} %get-tuple-element.105, bf16[512,768]{1,0:T(8,128)(2,1)S(1)} %copy-done.14, bf16[768,3072]{1,0:T(8,128)(2,1)S(1)} %bitcast.144, f32[512,3072]{1,0:T(8,128)} %get-tuple-element.127, f32[3072]{0:T(1024)S(1)} %copy-done.35), kind=kOutput, calls=%fused_computation.15 | convolution fusion | flops 2442654720 | bytes 21258240 | tf_op jit(solution)/shard_map/dot_general | solution.py:32
  249.0 3.9 fusion.58
  252.9 8.4 %fusion.1 = bf16[2,768,3072]{2,1,0:T(8,128)(2,1)} fusion(bf16[1,512,3072]{2,1,0:T(8,128)(2,1)S(1)} %bitcast.167, bf16[1,512,3072]{2,1,0:T(8,128)(2,1)S(1)} %bitcast.168, bf16[1,512,768]{2,1,0:T(8,128)(2,1)S(1)} %bitcast.158, bf16[1,512,768]{2,1,0:T(8,128)(2,1)S(1)} %copy-done.20), kind=kOutput, calls=%fused_computation.2 | convolution fusion | flops 4835770368 | bytes 17301504 | tf_op jit(solution)/shard_map/dot_general | solution.py:286
  271.3 3.4 slice_reduce_fusion
  280.9 4.0 multiply_reduce_fusion
  288.3 3.6 collective-permute-done.3
  294.3 2.9 broadcast_in_dim.16.dl_ref
  297.2 2.9 broadcast_in_dim.17.lser_ref
  300.1 2.9 broadcast_in_dim.18.dlr_ref
  303.0 24.6 %shard_map.306 = (bf16[12,512,64]{2,1,0:T(8,128)(2,1)}, bf16[12,512,64]{2,1,0:T(8,128)(2,1)}, bf16[12,512,64]{2,1,0:T(8,128)(2,1)}) custom-call(s32[2]{0:T(128)} %pad_add_fusion.meta_ref, bf16[12,512,64]{2,1,0:T(8,128)(2,1)} %bitcast.139, bf16[12,512,64]{2,1,0:T(8,128)(2,1)} %bitcast.141, bf16[12,512,64]{2,1,0:T(8,128)(2,1)} %bitcast.143, ...), custom_call_target="tpu_custom_call" | custom-call | flops 4026531840 | bytes 21233664 | tf_op jit(solution)/shard_map/pallas_call | solution.py:196
  334.9 4.0 convolution_convert_fusion
  342.7 62.0 %reduce-scatter.4.cloned.1.call-done = bf16[96,3072]{1,0:T(8,128)(2,1)} async-done(((bf16[768,3072]{1,0:T(8,128)(2,1)}), bf16[96,3072]{1,0:T(8,128)(2,1)}) %reduce-scatter.4.cloned.1.call-update) | async-done | bytes 589840 | tf_op jit(solution)/shard_map/reduce_scatter | solution.py:64
  417.6 67.1 %reduce-scatter.6.cloned.1.call-done = bf16[2,96,3072]{2,1,0:T(8,128)(2,1)} async-done(((bf16[2,768,3072]{2,1,0:T(8,128)(2,1)}), bf16[2,96,3072]{2,1,0:T(8,128)(2,1)}) %reduce-scatter.6.cloned.1.call-update) | async-done | bytes 1179664 | tf_op jit(solution)/shard_map/reduce_scatter | solution.py:64
  494.5 4.0 concatenate.20
  499.1 7.0 %add_convert_fusion = bf16[512,768]{1,0:T(8,128)(2,1)} fusion(f32[512,768]{1,0:T(8,128)S(1)} %get-tuple-element.126, bf16[512,3072]{1,0:T(8,128)(2,1)} %copy-done.44, bf16[768,3072]{1,0:T(8,128)(2,1)} %bitcast.145, f32[768]{0:T(1024)S(1)} %convert_element_type.102), kind=kOutput, calls=%fused_computation.71 | convolution fusion | flops 2417098752 | bytes 10226688 | tf_op jit(solution)/shard_map/dot_general | solution.py:28
  515.4 41.4 %all-reduce = (f32[768]{0:T(1024)}, f32[768]{0:T(1024)}, f32[768]{0:T(1024)}, f32[3072]{0:T(1024)}, f32[768]{0:T(1024)}, /*index=5*/f32[768]{0:T(1024)}, f32[768]{0:T(1024)}, f32[768]{0:T(1024)}, f32[768]{0:T(1024)}) all-reduce(f32[768]{0:T(1024)S(1)} %reduce_sum.182, ...), channel_id=1, replica_groups=mesh['dp'=8,'tensor'=4] {'dp','tensor'}, use_global_device_ids=true, to_apply=%region_13.14 | all-reduce | flops 9216 | bytes 73728 | tf_op jit(solution)/shard_map/psum | solution.py:336
  (188 shorter events, 126.8 us)
Async XLA Ops:
  7.2 7.7 %copy-start = (bf16[512,768]{1,0:T(8,128)(2,1)S(1)}, bf16[512,768]{1,0:T(8,128)(2,1)}, u32[]{:S(2)}) copy-start(bf16[512,768]{1,0:T(8,128)(2,1)} %param.18) | copy-start | bytes 2359300
  7.2 70.5 %all-gather.5.cloned.1.call-start = ((), (), s32[]{:S(2)}) async-start(), calls=%async_computation.6 | async-start | bytes 4866048 | tf_op jit(solution)/shard_map/all_gather | solution.py:49
  9.8 192.6 %all-gather.7.cloned.1.call-start = ((), (), s32[]{:S(2)}) async-start(), calls=%async_computation.7 | async-start | bytes 9732096 | tf_op jit(solution)/shard_map/all_gather | solution.py:49
  11.6 393.1 %reduce-scatter.4.cloned.1.call-start = ((), (), s32[]{:S(2)}) async-start(), calls=%async_computation.3 | async-start | bytes 5308416 | tf_op jit(solution)/shard_map/reduce_scatter | solution.py:64
  15.5 69.4 %copy-start.27 = (f32[512]{0:T(512)}, f32[512]{0:T(512)S(1)}, u32[]{:S(2)}) copy-start(f32[512]{0:T(512)S(1)} %fusion.31) | copy-start | bytes 6148
  15.5 110.6 %copy-start.24 = (f32[512]{0:T(512)}, f32[512]{0:T(512)S(1)}, u32[]{:S(2)}) copy-start(f32[512]{0:T(512)S(1)} %fusion.39) | copy-start | bytes 6148
  87.6 3.0 copy-start.39
  103.0 8.9 %copy-start.42 = (bf16[768]{0:T(1024)(128)(2,1)S(1)}, bf16[768]{0:T(1024)(128)(2,1)}, u32[]{:S(2)}) copy-start(bf16[768]{0:T(1024)(128)(2,1)} %param.29) | copy-start | bytes 4612
  105.3 40.6 %collective-permute-start = (bf16[12,512,64]{1,2,0:T(8,128)(2,1)}, bf16[12,512,64]{1,2,0:T(8,128)(2,1)}, u32[]{:S(2)}, u32[]{:S(2)}) collective-permute-start(bf16[12,512,64]{1,2,0:T(8,128)(2,1)} %bitcast.148), channel_id=1, source_target_pairs={{0,1},{2,3},{4,5},{6,7},{8,9},{10,11},{12,13},{14,15},{16,17},{18,... | collective-permute-start | bytes 2359304 | tf_op jit(solution)/shard_map/ppermute | solution.py:272
  109.5 60.1 %collective-permute-start.1 = (bf16[12,512,64]{1,2,0:T(8,128)(2,1)}, bf16[12,512,64]{1,2,0:T(8,128)(2,1)}, u32[]{:S(2)}, u32[]{:S(2)}) collective-permute-start(bf16[12,512,64]{1,2,0:T(8,128)(2,1)} %bitcast.150), channel_id=1, source_target_pairs={{0,1},{2,3},{4,5},{6,7},{8,9},{10,11},{12,13},{14,15},{16,17},{18,... | collective-permute-start | bytes 2359304 | tf_op jit(solution)/shard_map/ppermute | solution.py:272
  144.6 131.3 %collective-permute-start.2 = (bf16[12,512,64]{1,2,0:T(8,128)(2,1)}, bf16[12,512,64]{1,2,0:T(8,128)(2,1)}, u32[]{:S(2)}, u32[]{:S(2)}) collective-permute-start(bf16[12,512,64]{1,2,0:T(8,128)(2,1)} %bitcast.51), channel_id=1, source_target_pairs={{1,0},{3,2},{5,4},{7,6},{9,8},{11,10},{13,12},{15,14},{17,16},{19,... | collective-permute-start | bytes 2359304 | tf_op jit(solution)/shard_map/ppermute | solution.py:275
  194.4 2.8 copy-start.41
  221.0 18.5 %copy-start.7 = (bf16[96,8,4,768]{3,1,2,0:T(8,128)(2,1)}, bf16[96,8,4,768]{3,1,2,0:T(8,128)(2,1)S(1)}, u32[]{:S(2)}) copy-start(bf16[96,8,4,768]{3,1,2,0:T(8,128)(2,1)S(1)} %copy.126) | copy-start | bytes 14155780
  221.1 18.5 %copy-start.14 = (bf16[512,768]{1,0:T(8,128)(2,1)S(1)}, bf16[512,768]{1,0:T(8,128)(2,1)}, u32[]{:S(2)}) copy-start(bf16[512,768]{1,0:T(8,128)(2,1)} %param.20) | copy-start | bytes 2359300
  239.6 13.3 %copy-start.44 = (bf16[512,3072]{1,0:T(8,128)(2,1)}, bf16[512,3072]{1,0:T(8,128)(2,1)S(1)}, u32[]{:S(2)}) copy-start(bf16[512,3072]{1,0:T(8,128)(2,1)S(1)} %get-tuple-element.104) | copy-start | bytes 9437188
  249.0 3.9 copy-start.20
  261.3 2.8 copy-start.30
  261.3 2.8 copy-start.6
  261.3 2.8 copy-start.23
  264.8 21.4 %copy-start.37 = (f32[512]{0:T(512)}, f32[512]{0:T(512)S(1)}, u32[]{:S(2)}) copy-start(f32[512]{0:T(512)S(1)} %negate_multiply_fusion.2) | copy-start | bytes 6148
  270.0 21.9 %collective-permute-start.3 = (bf16[12,512,64]{1,2,0:T(8,128)(2,1)}, bf16[12,512,64]{1,2,0:T(8,128)(2,1)}, u32[]{:S(2)}, u32[]{:S(2)}) collective-permute-start(bf16[12,512,64]{1,2,0:T(8,128)(2,1)} %bitcast.152), channel_id=1, source_target_pairs={{1,0},{3,2},{5,4},{7,6},{9,8},{11,10},{13,12},{15,14},{17,16},{19,... | collective-permute-start | bytes 2359304 | tf_op jit(solution)/shard_map/ppermute | solution.py:304
  274.6 19.7 %collective-permute-start.4 = (f32[12,512]{1,0:T(8,128)}, f32[12,512]{1,0:T(8,128)}, u32[]{:S(2)}, u32[]{:S(2)}) collective-permute-start(f32[12,512]{1,0:T(8,128)} %slice_reduce_fusion), channel_id=1, source_target_pairs={{1,0},{3,2},{5,4},{7,6},{9,8},{11,10},{13,12},{15,14},{17,16},{19,... | collective-permute-start | bytes 73736 | tf_op jit(solution)/shard_map/ppermute | solution.py:275
  280.9 5.3 copy-start.4
  280.9 5.3 copy-start.16
  280.9 5.3 copy-start.19
  284.9 9.4 %collective-permute-start.5 = (f32[12,512]{1,0:T(8,128)}, f32[12,512]{1,0:T(8,128)}, u32[]{:S(2)}, u32[]{:S(2)}) collective-permute-start(f32[12,512]{1,0:T(8,128)} %multiply_reduce_fusion), channel_id=1, source_target_pairs={{1,0},{3,2},{5,4},{7,6},{9,8},{11,10},{13,12},{15,14},{17,16},{19,... | collective-permute-start | bytes 73736 | tf_op jit(solution)/shard_map/ppermute | solution.py:304
  332.5 2.4 copy-start.40
  334.9 4.0 copy-start.9
  341.8 142.9 %reduce-scatter.6.cloned.1.call-start = ((), (), s32[]{:S(2)}) async-start(), calls=%async_computation.4 | async-start | bytes 10616832 | tf_op jit(solution)/shard_map/reduce_scatter | solution.py:64
  342.4 214.4 %reduce-scatter.8.cloned.1.call-start = ((), (), s32[]{:S(2)}) async-start(), calls=%async_computation.5 | async-start | bytes 2211840 | tf_op jit(solution)/shard_map/reduce_scatter | solution.py:73
  499.1 7.0 %copy-start.1 = (bf16[12,512,64]{2,1,0:T(8,128)(2,1)S(1)}, bf16[12,512,64]{2,1,0:T(8,128)(2,1)}, u32[]{:S(2)}) copy-start(bf16[12,512,64]{2,1,0:T(8,128)(2,1)} %get-tuple-element.29) | copy-start | bytes 2359300
  499.1 7.0 %copy-start.2 = (bf16[12,512,64]{2,1,0:T(8,128)(2,1)S(1)}, bf16[12,512,64]{2,1,0:T(8,128)(2,1)}, u32[]{:S(2)}) copy-start(bf16[12,512,64]{2,1,0:T(8,128)(2,1)} %get-tuple-element.31) | copy-start | bytes 2359300
  (24 other events, 35.4 us)
Sparse Core Ops, SparseCore 0:
  11.4 66.2 all-gather.4
  81.1 96.8 all-gather.6
  341.9 62.7 reduce-scatter.3
  408.1 76.6 reduce-scatter.5
  498.6 38.6 reduce-scatter.7

commit v2 on v1

--- a/solution.py
+++ b/solution.py
@@ -244,9 +244,9 @@
     to_second = [(t, t + 1) for t in range(0, tp, 2)]
     to_first = [(t + 1, t) for t in range(0, tp, 2)]
 
-    full_query, full_key, full_value, out_t = gather_joined([w_query, w_key, w_value, w_out.T], dp, tp)
+    full_query, full_key, full_value = gather_joined([w_query, w_key, w_value], dp, tp)
+    out_t, full_up, down_t = gather_joined([w_out.T, w_up, w_down.T], dp, tp)
     full_out = out_t.T
-    full_up, down_t = gather_joined([w_up, w_down.T], dp, tp)
     full_down = down_t.T
     width = full_query.shape[1]
     heads = width // HEAD
@@ -345,8 +345,9 @@
         norm_two_back[1],
         norm_two_back[2],
         ),
-        AXES,
-    )
+        "tensor",
+    )
+    vector_sums = lax.psum(vector_sums, "dp")
     return (
         result,
         grad_input,

time: 575 us -> 595 us (1.035)
  waiting for transfers between devices: 217 us -> 230 us
    psum x0 -> x1, blocking collectives: none -> 23.4 us  [layer(): vector_sums = lax.psum(vector_sums, 'dp')]
    psum x1, blocking collectives: 41.4 us -> 21.4 us  [layer(): lax.psum((jnp.sum(grad_q, axis=0, dtype=f32), jnp.sum(grad_v, axis=0, dty...]
    transpose x5 -> x0, local copies, waits for them, and re-layouts: 17.3 us -> none  [gather_joined(): out.append(block.transpose(0, 2, 1, 3).reshape(dp * r, tp * c))]
    slice x1 -> x3, local copies, waits for them, and re-layouts: 6.85 us -> 20.3 us  [gather_joined(): block = full[:, :, :, start:start + c]]
    ppermute x2, waiting for transfers between devices: 21.2 us -> 32.1 us  [layer(): k_oth, v_oth = lax.ppermute((k3, v3), 'tensor', to_second)]
    unnamed x96 -> x116, local copies, waits for them, and re-layouts: 18.1 us -> 28.5 us
  transfers between devices with their start and end apart: 11 -> 11, of which waited for: 5 -> 6; matrix products, arithmetic and copies ran while one was open for 33% -> 33% of each run, Pallas kernels for 4% -> 4%
where the time goes in v2:
time: 595 us; the launch traced here: 586 us
  waiting for transfers between devices  230 us (39%)
  local copies, waits for them, and re-layouts  142 us (24%)
  matrix products  68 us (11%)
  Pallas kernels  46.9 us (8%)
  blocking collectives  44.8 us (8%)
  other arithmetic  27.1 us (5%)
  between operations  14.7 us (2%)
  starting transfers between devices  12 us (2%)
    reduce_scatter x2, waiting for transfers between devices, scatter_rows(): lax.psum_scatter(grad.astype(LINK), 'dp', scatter_dimension=axis, tiled=T...  135 us
    all_gather x2, waiting for transfers between devices, gather_joined(): lax.all_gather(joined, AXES, axis=0, tiled=False).reshape(dp, tp, r, -1)  59.4 us
    dot_general x6, matrix products, dot_right(): return jnp.dot(first_op, second_op, preferred_element_type=jnp.float32)  35.1 us
    ppermute x2, waiting for transfers between devices, layer(): k_oth, v_oth = lax.ppermute((k3, v3), 'tensor', to_second)  32.1 us
    unnamed x116, local copies, waits for them, and re-layouts  28.5 us
    pallas_call x1, Pallas kernels, attention_backward(): pl.pallas_call(attn_bwd_kernel, out_shape=tuple((jax.ShapeDtypeStruct(q.s...  24.7 us
    psum x1, blocking collectives, layer(): vector_sums = lax.psum(vector_sums, 'dp')  23.4 us
    pallas_call x1, Pallas kernels, attention_forward(): pl.pallas_call(attn_fwd_kernel, out_shape=(jax.ShapeDtypeStruct(q.shape,...  22.3 us
  transfers between devices with their start and end apart: 11, of which 6 were waited for; matrix products, arithmetic and copies ran while one was open for 33% of the time, Pallas kernels for 4%

profile of v2, /device:TPU:0, one launch (start us, length us, event | category | flops | bytes accessed | tf_op | source)
XLA Modules:
  0.0 586.0 jit_solution(13122168028332875743)
XLA Ops:
  15.7 59.4 %all-gather.5.cloned.1.call-done = bf16[3072,576]{1,0:T(8,128)(2,1)} async-done(((bf16[96,576]{1,0:T(8,128)(2,1)}), bf16[3072,576]{1,0:T(8,128)(2,1)}) %all-gather.5.cloned.1.call-update) | async-done | bytes 3538960 | tf_op jit(solution)/shard_map/all_gather | solution.py:49
  75.1 5.2 fusion.55
  83.1 3.0 reshape.173
  90.3 2.8 copy.123
  93.1 2.9 reshape.175
  100.9 4.0 collective-permute-start
  116.4 3.0 reshape.171
  131.0 4.9 collective-permute-done
  138.3 27.2 %collective-permute-done.1 = bf16[12,512,64]{1,2,0:T(8,128)(2,1)} collective-permute-done((bf16[12,512,64]{1,2,0:T(8,128)(2,1)}, bf16[12,512,64]{1,2,0:T(8,128)(2,1)}, u32[]{:S(2)}, u32[]{:S(2)}) %collective-permute-start.1) | collective-permute-done | bytes 786464 | tf_op jit(solution)/shard_map/ppermute | solution.py:272
  168.0 22.3 %shard_map.305 = (bf16[12,512,64]{2,1,0:T(8,128)(2,1)}, f32[12,512,64]{2,1,0:T(8,128)}, f32[12,512,128]{2,1,0:T(8,128)}) custom-call(s32[2]{0:T(128)} %pad_add_fusion.meta_ref, bf16[12,512,64]{2,1,0:T(8,128)(2,1)} %bitcast.140, bf16[12,512,64]{2,1,0:T(8,128)(2,1)} %bitcast.142, bf16[12,512,64]{2,1,0:T(8,128)(2,1)} %bitcast.144, ...), custom_call_target="tpu_custom_call" | custom-call | flops 1610612736 | bytes 9437184 | tf_op jit(solution)/shard_map/pallas_call | solution.py:171
  194.2 13.6 %fusion.54 = (bf16[8,4,96,768]{3,2,1,0:T(8,128)(2,1)}, bf16[8,4,96,768]{3,2,1,0:T(8,128)(2,1)}) fusion(bf16[8,4,96,1728]{3,2,1,0:T(8,128)(2,1)} %bitcast.133), kind=kLoop, calls=%fused_computation.106 | loop fusion | bytes 18874368 | tf_op jit(solution)/shard_map/slice | solution.py:54
  209.6 3.9 reshape.179
  213.5 6.0 %copy.125 = bf16[8,4,96,768]{3,1,2,0:T(4,128)(2,1)S(1)} copy(bf16[8,4,96,768]{3,2,1,0:T(8,128)(2,1)} %get-tuple-element.116) | data formatting | bytes 9437184
  219.5 3.5 copy.127
  224.3 3.6 copy.126
  229.4 21.2 %multiply_convert_fusion = (bf16[512,3072]{1,0:T(8,128)(2,1)S(1)}, f32[512,3072]{1,0:T(8,128)S(1)}, f32[512,3072]{1,0:T(8,128)}) fusion(f32[3072]{0:T(1024)S(1)} %copy-done.37, bf16[768,3072]{1,0:T(8,128)(2,1)} %bitcast.149, f32[512,768]{1,0:T(8,128)S(1)} %get-tuple-element.134, f32[768]{0:T(1024)S(1)} %copy-done.34, f32[768]{0:T(1024)S(1)} %convert_element_type.97, ...), kind=kOutput, calls=%fused_computation.16 | convolution fusion | flops 2521694208 | bytes 22042624 | tf_op jit(solution)/shard_map/dot_general | solution.py:28
  250.6 9.0 %convert_reduce_fusion = (f32[3072]{0:T(1024)}, bf16[512,3072]{1,0:T(8,128)(2,1)S(1)}) fusion(f32[512,3072]{1,0:T(8,128)S(1)} %get-tuple-element.114, bf16[512,768]{1,0:T(8,128)(2,1)S(1)} %copy-done.18, bf16[768,3072]{1,0:T(8,128)(2,1)S(1)} %bitcast.147, f32[512,3072]{1,0:T(8,128)} %get-tuple-element.135, f32[3072]{0:T(1024)S(1)} %copy-done.37), kind=kOutput, calls=%fused_computation.15 | convolution fusion | flops 2442654720 | bytes 21258240 | tf_op jit(solution)/shard_map/dot_general | solution.py:32
  259.6 3.8 fusion.59
  263.4 8.2 %fusion.1 = bf16[2,768,3072]{2,1,0:T(8,128)(2,1)} fusion(bf16[1,512,3072]{2,1,0:T(8,128)(2,1)S(1)} %bitcast.172, bf16[1,512,3072]{2,1,0:T(8,128)(2,1)S(1)} %bitcast.173, bf16[1,512,768]{2,1,0:T(8,128)(2,1)S(1)} %bitcast.163, bf16[1,512,768]{2,1,0:T(8,128)(2,1)S(1)} %fusion.44), kind=kOutput, calls=%fused_computation.2 | convolution fusion | flops 4835770368 | bytes 17301504 | tf_op jit(solution)/shard_map/dot_general | solution.py:286
  281.6 3.4 slice_reduce_fusion
  291.2 4.0 multiply_reduce_fusion
  298.6 3.5 collective-permute-done.3
  304.6 2.8 broadcast_in_dim.16.dl_ref
  310.3 2.9 broadcast_in_dim.18.dlr_ref
  313.2 24.7 %shard_map.306 = (bf16[12,512,64]{2,1,0:T(8,128)(2,1)}, bf16[12,512,64]{2,1,0:T(8,128)(2,1)}, bf16[12,512,64]{2,1,0:T(8,128)(2,1)}) custom-call(s32[2]{0:T(128)} %pad_add_fusion.meta_ref, bf16[12,512,64]{2,1,0:T(8,128)(2,1)} %bitcast.141, bf16[12,512,64]{2,1,0:T(8,128)(2,1)} %bitcast.143, bf16[12,512,64]{2,1,0:T(8,128)(2,1)} %bitcast.145, ...), custom_call_target="tpu_custom_call" | custom-call | flops 4026531840 | bytes 21233664 | tf_op jit(solution)/shard_map/pallas_call | solution.py:196
  345.2 4.0 convolution_convert_fusion
  352.7 67.3 %reduce-scatter.4.cloned.1.call-done = bf16[96,3072]{1,0:T(8,128)(2,1)} async-done(((bf16[768,3072]{1,0:T(8,128)(2,1)}), bf16[96,3072]{1,0:T(8,128)(2,1)}) %reduce-scatter.4.cloned.1.call-update) | async-done | bytes 589840 | tf_op jit(solution)/shard_map/reduce_scatter | solution.py:64
  432.8 67.2 %reduce-scatter.6.cloned.1.call-done = bf16[2,96,3072]{2,1,0:T(8,128)(2,1)} async-done(((bf16[2,768,3072]{2,1,0:T(8,128)(2,1)}), bf16[2,96,3072]{2,1,0:T(8,128)(2,1)}) %reduce-scatter.6.cloned.1.call-update) | async-done | bytes 1179664 | tf_op jit(solution)/shard_map/reduce_scatter | solution.py:64
  509.9 4.0 concatenate.20
  514.6 7.0 %add_convert_fusion = bf16[512,768]{1,0:T(8,128)(2,1)} fusion(f32[512,768]{1,0:T(8,128)S(1)} %get-tuple-element.134, bf16[512,3072]{1,0:T(8,128)(2,1)} %copy-done.48, bf16[768,3072]{1,0:T(8,128)(2,1)} %bitcast.148, f32[768]{0:T(1024)S(1)} %convert_element_type.102), kind=kOutput, calls=%fused_computation.67 | convolution fusion | flops 2417098752 | bytes 10226688 | tf_op jit(solution)/shard_map/dot_general | solution.py:28
  530.9 21.4 %all-reduce.1 = (f32[768]{0:T(1024)S(1)}, f32[768]{0:T(1024)S(1)}, f32[768]{0:T(1024)S(1)}, f32[3072]{0:T(1024)S(1)}, f32[768]{0:T(1024)S(1)}, /*index=5*/f32[76...) all-reduce(f32[768]{0:T(1024)S(1)} %reduce_sum.182, ...), channel_id=1, replica_groups=mesh['dp'=8,'tensor'=4] {'tensor'}, use_global_device_ids=true, to_apply=%region_13.14 | all-reduce | flops 9216 | bytes 73728 | tf_op jit(solution)/shard_map/psum | solution.py:336
  552.4 23.4 %all-reduce = (f32[768]{0:T(1024)}, f32[768]{0:T(1024)}, f32[768]{0:T(1024)}, f32[3072]{0:T(1024)}, f32[768]{0:T(1024)}, /*index=5*/f32[768]{0:T(1024)}, f32[768]{0:T(1024)}, f32[768]{0:T(1024)}, f32[768]{0:T(1024)}) all-reduce(f32[768]{0:T(1024)S(1)} %get-tuple-element.102, ...), channel_id=1, replica_groups=mesh['dp'=8,'tensor'=4] {'dp'}, use_global_device_ids=true, to_apply=%region_14.15 | all-reduce | flops 9216 | bytes 73728 | tf_op jit(solution)/shard_map/psum | solution.py:350
  (208 shorter events, 128.3 us)
Async XLA Ops:
  7.2 7.9 %copy-start = (bf16[512,768]{1,0:T(8,128)(2,1)S(1)}, bf16[512,768]{1,0:T(8,128)(2,1)}, u32[]{:S(2)}) copy-start(bf16[512,768]{1,0:T(8,128)(2,1)} %param.18) | copy-start | bytes 2359300
  7.2 67.9 %all-gather.5.cloned.1.call-start = ((), (), s32[]{:S(2)}) async-start(), calls=%async_computation.6 | async-start | bytes 4055040 | tf_op jit(solution)/shard_map/all_gather | solution.py:49
  8.9 183.7 %all-gather.7.cloned.1.call-start = ((), (), s32[]{:S(2)}) async-start(), calls=%async_computation.7 | async-start | bytes 11354112 | tf_op jit(solution)/shard_map/all_gather | solution.py:49
  11.8 408.1 %reduce-scatter.4.cloned.1.call-start = ((), (), s32[]{:S(2)}) async-start(), calls=%async_computation.3 | async-start | bytes 5308416 | tf_op jit(solution)/shard_map/reduce_scatter | solution.py:64
  15.7 64.6 %copy-start.30 = (f32[512]{0:T(512)}, f32[512]{0:T(512)S(1)}, u32[]{:S(2)}) copy-start(f32[512]{0:T(512)S(1)} %fusion.31) | copy-start | bytes 6148
  15.7 103.7 %copy-start.27 = (f32[512]{0:T(512)}, f32[512]{0:T(512)S(1)}, u32[]{:S(2)}) copy-start(f32[512]{0:T(512)S(1)} %fusion.39) | copy-start | bytes 6148
  98.5 8.5 %copy-start.46 = (bf16[768]{0:T(1024)(128)(2,1)S(1)}, bf16[768]{0:T(1024)(128)(2,1)}, u32[]{:S(2)}) copy-start(bf16[768]{0:T(1024)(128)(2,1)} %param.29) | copy-start | bytes 4612
  100.9 35.0 %collective-permute-start = (bf16[12,512,64]{1,2,0:T(8,128)(2,1)}, bf16[12,512,64]{1,2,0:T(8,128)(2,1)}, u32[]{:S(2)}, u32[]{:S(2)}) collective-permute-start(bf16[12,512,64]{1,2,0:T(8,128)(2,1)} %bitcast.153), channel_id=1, source_target_pairs={{0,1},{2,3},{4,5},{6,7},{8,9},{10,11},{12,13},{14,15},{16,17},{18,... | collective-permute-start | bytes 2359304 | tf_op jit(solution)/shard_map/ppermute | solution.py:272
  104.8 60.6 %collective-permute-start.1 = (bf16[12,512,64]{1,2,0:T(8,128)(2,1)}, bf16[12,512,64]{1,2,0:T(8,128)(2,1)}, u32[]{:S(2)}, u32[]{:S(2)}) collective-permute-start(bf16[12,512,64]{1,2,0:T(8,128)(2,1)} %bitcast.155), channel_id=1, source_target_pairs={{0,1},{2,3},{4,5},{6,7},{8,9},{10,11},{12,13},{14,15},{16,17},{18,... | collective-permute-start | bytes 2359304 | tf_op jit(solution)/shard_map/ppermute | solution.py:272
  129.2 157.1 %collective-permute-start.2 = (bf16[12,512,64]{1,2,0:T(8,128)(2,1)}, bf16[12,512,64]{1,2,0:T(8,128)(2,1)}, u32[]{:S(2)}, u32[]{:S(2)}) collective-permute-start(bf16[12,512,64]{1,2,0:T(8,128)(2,1)} %bitcast.51), channel_id=1, source_target_pairs={{1,0},{3,2},{5,4},{7,6},{9,8},{11,10},{13,12},{15,14},{17,16},{19,... | collective-permute-start | bytes 2359304 | tf_op jit(solution)/shard_map/ppermute | solution.py:275
  219.5 4.8 slice-start
  219.5 3.5 copy-start.16
  219.5 4.8 slice-start.1
  224.2 3.7 copy-start.32
  224.3 5.1 copy-start.25
  229.1 21.5 %copy-start.7 = (bf16[96,8,4,768]{3,1,2,0:T(8,128)(2,1)}, bf16[96,8,4,768]{3,1,2,0:T(8,128)(2,1)S(1)}, u32[]{:S(2)}) copy-start(bf16[96,8,4,768]{3,1,2,0:T(8,128)(2,1)S(1)} %copy.128) | copy-start | bytes 14155780
  229.1 30.5 %slice-start.2 = ((s8[4718592]{0:T(1024)(128)(4,1)}), s8[4194304]{0:T(1024)(128)(4,1)S(1)}, s32[]{:S(2)}) async-start(s8[4718592]{0:T(1024)(128)(4,1)} %bitcast.150), calls=%async_computation.10 | async-start | bytes 8388608
  229.4 21.2 %copy-start.18 = (bf16[512,768]{1,0:T(8,128)(2,1)S(1)}, bf16[512,768]{1,0:T(8,128)(2,1)}, u32[]{:S(2)}) copy-start(bf16[512,768]{1,0:T(8,128)(2,1)} %param.20) | copy-start | bytes 2359300
  229.4 30.2 %slice-start.3 = ((s8[4718592]{0:T(1024)(128)(4,1)}), s8[524288]{0:T(1024)(128)(4,1)S(1)}, s32[]{:S(2)}) async-start(s8[4718592]{0:T(1024)(128)(4,1)} %bitcast.150), calls=%async_computation.11 | async-start | bytes 1048576
  250.6 12.8 %copy-start.48 = (bf16[512,3072]{1,0:T(8,128)(2,1)}, bf16[512,3072]{1,0:T(8,128)(2,1)S(1)}, u32[]{:S(2)}) copy-start(bf16[512,3072]{1,0:T(8,128)(2,1)S(1)} %get-tuple-element.113) | copy-start | bytes 9437188
  275.1 21.4 %copy-start.39 = (f32[512]{0:T(512)}, f32[512]{0:T(512)S(1)}, u32[]{:S(2)}) copy-start(f32[512]{0:T(512)S(1)} %negate_multiply_fusion.2) | copy-start | bytes 6148
  280.3 21.7 %collective-permute-start.3 = (bf16[12,512,64]{1,2,0:T(8,128)(2,1)}, bf16[12,512,64]{1,2,0:T(8,128)(2,1)}, u32[]{:S(2)}, u32[]{:S(2)}) collective-permute-start(bf16[12,512,64]{1,2,0:T(8,128)(2,1)} %bitcast.157), channel_id=1, source_target_pairs={{1,0},{3,2},{5,4},{7,6},{9,8},{11,10},{13,12},{15,14},{17,16},{19,... | collective-permute-start | bytes 2359304 | tf_op jit(solution)/shard_map/ppermute | solution.py:304
  285.0 19.7 %collective-permute-start.4 = (f32[12,512]{1,0:T(8,128)}, f32[12,512]{1,0:T(8,128)}, u32[]{:S(2)}, u32[]{:S(2)}) collective-permute-start(f32[12,512]{1,0:T(8,128)} %slice_reduce_fusion), channel_id=1, source_target_pairs={{1,0},{3,2},{5,4},{7,6},{9,8},{11,10},{13,12},{15,14},{17,16},{19,... | collective-permute-start | bytes 73736 | tf_op jit(solution)/shard_map/ppermute | solution.py:275
  291.2 5.3 copy-start.4
  291.2 5.3 copy-start.20
  291.2 5.3 copy-start.24
  295.2 9.4 %collective-permute-start.5 = (f32[12,512]{1,0:T(8,128)}, f32[12,512]{1,0:T(8,128)}, u32[]{:S(2)}, u32[]{:S(2)}) collective-permute-start(f32[12,512]{1,0:T(8,128)} %multiply_reduce_fusion), channel_id=1, source_target_pairs={{1,0},{3,2},{5,4},{7,6},{9,8},{11,10},{13,12},{15,14},{17,16},{19,... | collective-permute-start | bytes 73736 | tf_op jit(solution)/shard_map/ppermute | solution.py:304
  345.2 4.0 copy-start.11
  352.0 148.0 %reduce-scatter.6.cloned.1.call-start = ((), (), s32[]{:S(2)}) async-start(), calls=%async_computation.4 | async-start | bytes 10616832 | tf_op jit(solution)/shard_map/reduce_scatter | solution.py:64
  352.6 223.1 %reduce-scatter.8.cloned.1.call-start = ((), (), s32[]{:S(2)}) async-start(), calls=%async_computation.5 | async-start | bytes 2211840 | tf_op jit(solution)/shard_map/reduce_scatter | solution.py:73
  514.6 7.0 %copy-start.1 = (bf16[12,512,64]{2,1,0:T(8,128)(2,1)S(1)}, bf16[12,512,64]{2,1,0:T(8,128)(2,1)}, u32[]{:S(2)}) copy-start(bf16[12,512,64]{2,1,0:T(8,128)(2,1)} %get-tuple-element.29) | copy-start | bytes 2359300
  514.6 7.0 %copy-start.2 = (bf16[12,512,64]{2,1,0:T(8,128)(2,1)S(1)}, bf16[12,512,64]{2,1,0:T(8,128)(2,1)}, u32[]{:S(2)}) copy-start(bf16[12,512,64]{2,1,0:T(8,128)(2,1)} %get-tuple-element.31) | copy-start | bytes 2359300
  (32 other events, 64.6 us)
Sparse Core Ops, SparseCore 0:
  11.4 63.6 all-gather.4
  77.9 104.5 all-gather.6
  352.2 67.7 reduce-scatter.3
  423.3 76.6 reduce-scatter.5
  514.1 40.0 reduce-scatter.7

commit v3 on v1

--- a/solution.py
+++ b/solution.py
@@ -46,7 +46,13 @@
 def gather_joined(shards, dp, tp):
     r = shards[0].shape[0]
     joined = jnp.concatenate(shards, axis=1)
-    full = lax.all_gather(joined, AXES, axis=0, tiled=False).reshape(dp, tp, r, -1)
+    pieces = [joined] + [
+        lax.ppermute(joined, "tensor", [(i, (i + step) % tp) for i in range(tp)]) for step in range(1, tp)
+    ]
+    t_index = lax.axis_index("tensor")
+    order = (t_index - jnp.arange(tp, dtype=jnp.int32)) % tp
+    by_tensor = jnp.take(jnp.stack(pieces), order, axis=0)
+    full = lax.all_gather(by_tensor, "dp", axis=0, tiled=False)
     out = []
     start = 0
     for piece in shards:

time: 575 us -> 536 us (0.932)
  waiting for transfers between devices: 217 us -> 166 us
  starting transfers between devices: 12.1 us -> 23.3 us
    all_gather x2, waiting for transfers between devices: 62.2 us -> 7.06 us  [gather_joined(): full = lax.all_gather(by_tensor, 'dp', axis=0, tiled=False)]
    ppermute x0 -> x6, waiting for transfers between devices: none -> 33.9 us  [gather_joined(): lax.ppermute(joined, 'tensor', [(i, (i + step) % tp) for i in range(tp)])]
    ppermute x2, waiting for transfers between devices: 21.2 us -> 0.01 us  [layer(): k_oth, v_oth = lax.ppermute((k3, v3), 'tensor', to_second)]
    transpose x5 -> x8, local copies, waits for them, and re-layouts: 17.3 us -> 33.8 us  [gather_joined(): out.append(block.transpose(0, 2, 1, 3).reshape(dp * r, tp * c))]
    ppermute x0 -> x6, starting transfers between devices: none -> 11 us  [gather_joined(): lax.ppermute(joined, 'tensor', [(i, (i + step) % tp) for i in range(tp)])]
    unnamed x96 -> x104, local copies, waits for them, and re-layouts: 18.1 us -> 8.41 us
    reduce_scatter x2, waiting for transfers between devices: 129 us -> 120 us  [scatter_rows(): lax.psum_scatter(grad.astype(LINK), 'dp', scatter_dimension=axis, tiled=T...]
    slice x1 -> x0, local copies, waits for them, and re-layouts: 6.85 us -> none  [gather_joined(): block = full[:, :, :, start:start + c]]
  transfers between devices with their start and end apart: 11 -> 17, of which waited for: 5 -> 8; matrix products, arithmetic and copies ran while one was open for 33% -> 35% of each run, Pallas kernels for 4% -> 4%
where the time goes in v3:
time: 536 us; the launch traced here: 528 us
  waiting for transfers between devices  166 us (31%)
  local copies, waits for them, and re-layouts  138 us (26%)
  matrix products  68.9 us (13%)
  Pallas kernels  47 us (9%)
  blocking collectives  41.3 us (8%)
  other arithmetic  28.7 us (5%)
  starting transfers between devices  23.3 us (4%)
  between operations  15 us (3%)
    reduce_scatter x2, waiting for transfers between devices, scatter_rows(): lax.psum_scatter(grad.astype(LINK), 'dp', scatter_dimension=axis, tiled=T...  120 us
    psum x1, blocking collectives, layer(): lax.psum((jnp.sum(grad_q, axis=0, dtype=f32), jnp.sum(grad_v, axis=0, dty...  41.3 us
    dot_general x6, matrix products, dot_right(): return jnp.dot(first_op, second_op, preferred_element_type=jnp.float32)  35.2 us
    ppermute x6, waiting for transfers between devices, gather_joined(): lax.ppermute(joined, 'tensor', [(i, (i + step) % tp) for i in range(tp)])  33.9 us
    transpose x8, local copies, waits for them, and re-layouts, gather_joined(): out.append(block.transpose(0, 2, 1, 3).reshape(dp * r, tp * c))  33.8 us
    pallas_call x1, Pallas kernels, attention_backward(): pl.pallas_call(attn_bwd_kernel, out_shape=tuple((jax.ShapeDtypeStruct(q.s...  24.7 us
    pallas_call x1, Pallas kernels, attention_forward(): pl.pallas_call(attn_fwd_kernel, out_shape=(jax.ShapeDtypeStruct(q.shape,...  22.3 us
    dot_general x6, matrix products, dot_back(): lax.dot_general(first_op, second_op, (((1,), (1,)), ((), ())), preferred_...  19.2 us
  transfers between devices with their start and end apart: 17, of which 8 were waited for; matrix products, arithmetic and copies ran while one was open for 35% of the time, Pallas kernels for 4%

profile of v3, /device:TPU:0, one launch (start us, length us, event | category | flops | bytes accessed | tf_op | source)
XLA Modules:
  0.0 527.7 jit_solution(4121155534576173140)
XLA Ops:
  9.1 5.1 collective-permute-start.2
  18.5 8.2 %collective-permute-done.1 = bf16[96,768]{1,0:T(8,128)(2,1)S(1)} collective-permute-done((bf16[96,768]{1,0:T(8,128)(2,1)S(1)}, bf16[96,768]{1,0:T(8,128)(2,1)S(1)}, u32[]{:S(2)}, u32[]{:S(2)}) %collective-permute-start.1) | collective-permute-done | bytes 147488 | tf_op jit(solution)/shard_map/ppermute | solution.py:50
  33.4 4.0 collective-permute-done.7
  37.4 19.4 %collective-permute-done.6 = bf16[96,1536]{1,0:T(8,128)(2,1)S(1)} collective-permute-done((bf16[96,1536]{1,0:T(8,128)(2,1)S(1)}, bf16[96,1536]{1,0:T(8,128)(2,1)S(1)}, u32[]{:S(2)}, u32[]{:S(2)}) %collective-permute-start.6) | collective-permute-done | bytes 294944 | tf_op jit(solution)/shard_map/ppermute | solution.py:50
  60.7 7.1 %all-gather.3.cloned.1.call-done = bf16[8,4,96,768]{3,2,1,0:T(8,128)(2,1)} async-done(((bf16[1,4,96,768]{3,2,1,0:T(8,128)(2,1)}), bf16[8,4,96,768]{3,2,1,0:T(8,128)(2,1)}) %all-gather.3.cloned.1.call-update) | async-done | bytes 4718608 | tf_op jit(solution)/shard_map/all_gather | solution.py:55
  67.7 7.0 %slice_bitcast_fusion.2 = (bf16[8,96,4,192]{3,1,2,0:T(8,128)(2,1)S(1)}, bf16[8,96,4,192]{3,1,2,0:T(8,128)(2,1)}, bf16[8,96,4,192]{3,1,2,0:T(8,128)(2,1)}, bf16[8,96,4,192]{3,1,2,0:T(8,128)(2,1)}) fusion(bf16[8,4,96,768]{3,2,1,0:T(8,128)(2,1)} %all-gather.3.cloned.1.call-done), kind=kLoop, calls=%fused_computation.64 | loop fusion | bytes 9437184 | tf_op jit(solution)/shard_map/transpose | solution.py:61
  77.6 3.0 reshape.234
  87.6 2.9 reshape.236
  95.3 4.4 collective-permute-start.3
  112.5 3.8 reshape.232
  116.3 3.1 add_convert_fusion.3
  131.0 3.8 reshape.239
  141.0 22.3 %shard_map.305 = (bf16[12,512,64]{2,1,0:T(8,128)(2,1)}, f32[12,512,64]{2,1,0:T(8,128)}, f32[12,512,128]{2,1,0:T(8,128)}) custom-call(s32[2]{0:T(128)} %pad_add_fusion.meta_ref, bf16[12,512,64]{2,1,0:T(8,128)(2,1)} %bitcast.152, bf16[12,512,64]{2,1,0:T(8,128)(2,1)} %bitcast.154, bf16[12,512,64]{2,1,0:T(8,128)(2,1)} %bitcast.156, ...), custom_call_target="tpu_custom_call" | custom-call | flops 1610612736 | bytes 9437184 | tf_op jit(solution)/shard_map/pallas_call | solution.py:177
  171.3 6.8 %slice_bitcast_fusion = (bf16[8,96,4,768]{3,1,2,0:T(8,128)(2,1)S(1)}, bf16[8,96,4,768]{3,1,2,0:T(8,128)(2,1)}) fusion(bf16[8,4,96,1536]{3,2,1,0:T(8,128)(2,1)} %all-gather.5.cloned.1.call-done), kind=kLoop, calls=%fused_computation.33 | loop fusion | bytes 18874368 | tf_op jit(solution)/shard_map/transpose | solution.py:61
  178.1 6.0 %copy.133 = bf16[8,96,4,768]{3,2,1,0:T(4,128)(2,1)S(1)} copy(bf16[8,96,4,768]{3,1,2,0:T(8,128)(2,1)} %get-tuple-element.124) | data formatting | bytes 9437184 | tf_op jit(solution)/shard_map/transpose | solution.py:61
  185.2 3.6 copy.134
  190.0 18.5 %multiply_convert_fusion = (bf16[512,3072]{1,0:T(8,128)(2,1)S(1)}, f32[512,3072]{1,0:T(8,128)}, f32[512,3072]{1,0:T(8,128)}) fusion(f32[3072]{0:T(1024)S(1)} %copy-done.37, bf16[768,3072]{1,0:T(8,128)(2,1)S(1)} %bitcast.160, f32[512,768]{1,0:T(8,128)S(1)} %get-tuple-element.145, f32[768]{0:T(1024)S(1)} %copy-done.34, f32[768]{0:T(1024)S(1)} %convert_element_type.97, ...), kind=kOutput, calls=%fused_computation.18 | convolution fusion | flops 2521694208 | bytes 22042624 | tf_op jit(solution)/shard_map/dot_general | solution.py:28
  208.4 9.5 %convert_reduce_fusion = (f32[3072]{0:T(1024)}, bf16[512,3072]{1,0:T(8,128)(2,1)S(1)}) fusion(f32[512,3072]{1,0:T(8,128)} %get-tuple-element.122, bf16[512,768]{1,0:T(8,128)(2,1)S(1)} %copy-done.14, bf16[768,3072]{1,0:T(8,128)(2,1)S(1)} %bitcast.158, f32[512,3072]{1,0:T(8,128)} %get-tuple-element.146, f32[3072]{0:T(1024)S(1)} %copy-done.37), kind=kOutput, calls=%fused_computation.17 | convolution fusion | flops 2442654720 | bytes 21258240 | tf_op jit(solution)/shard_map/dot_general | solution.py:32
  217.9 3.9 fusion.61
  221.8 8.4 %fusion.1 = bf16[2,768,3072]{2,1,0:T(8,128)(2,1)} fusion(bf16[1,512,3072]{2,1,0:T(8,128)(2,1)S(1)} %bitcast.188, bf16[1,512,3072]{2,1,0:T(8,128)(2,1)S(1)} %bitcast.189, bf16[1,512,768]{2,1,0:T(8,128)(2,1)S(1)} %bitcast.172, bf16[1,512,768]{2,1,0:T(8,128)(2,1)S(1)} %copy-done.20), kind=kOutput, calls=%fused_computation.4 | convolution fusion | flops 4835770368 | bytes 17301504 | tf_op jit(solution)/shard_map/dot_general | solution.py:292
  240.2 3.4 slice_reduce_fusion
  249.8 4.0 multiply_reduce_fusion
  257.2 4.8 collective-permute-done.9
  264.5 2.9 broadcast_in_dim.40.dl_ref
  270.2 2.9 broadcast_in_dim.42.dlr_ref
  273.1 24.7 %shard_map.306 = (bf16[12,512,64]{2,1,0:T(8,128)(2,1)}, bf16[12,512,64]{2,1,0:T(8,128)(2,1)}, bf16[12,512,64]{2,1,0:T(8,128)(2,1)}) custom-call(s32[2]{0:T(128)} %pad_add_fusion.meta_ref, bf16[12,512,64]{2,1,0:T(8,128)(2,1)} %bitcast.153, bf16[12,512,64]{2,1,0:T(8,128)(2,1)} %bitcast.155, bf16[12,512,64]{2,1,0:T(8,128)(2,1)} %bitcast.157, ...), custom_call_target="tpu_custom_call" | custom-call | flops 4026531840 | bytes 21233664 | tf_op jit(solution)/shard_map/pallas_call | solution.py:202
  305.1 4.0 convolution_convert_fusion
  312.9 52.4 %reduce-scatter.4.cloned.1.call-done = bf16[96,3072]{1,0:T(8,128)(2,1)} async-done(((bf16[768,3072]{1,0:T(8,128)(2,1)}), bf16[96,3072]{1,0:T(8,128)(2,1)}) %reduce-scatter.4.cloned.1.call-update) | async-done | bytes 589840 | tf_op jit(solution)/shard_map/reduce_scatter | solution.py:70
  378.1 67.2 %reduce-scatter.6.cloned.1.call-done = bf16[2,96,3072]{2,1,0:T(8,128)(2,1)} async-done(((bf16[2,768,3072]{2,1,0:T(8,128)(2,1)}), bf16[2,96,3072]{2,1,0:T(8,128)(2,1)}) %reduce-scatter.6.cloned.1.call-update) | async-done | bytes 1179664 | tf_op jit(solution)/shard_map/reduce_scatter | solution.py:70
  455.0 4.0 concatenate.20
  459.6 7.0 %add_convert_fusion = bf16[512,768]{1,0:T(8,128)(2,1)} fusion(f32[512,768]{1,0:T(8,128)S(1)} %get-tuple-element.145, bf16[512,3072]{1,0:T(8,128)(2,1)} %copy-done.49, bf16[768,3072]{1,0:T(8,128)(2,1)} %bitcast.159, f32[768]{0:T(1024)S(1)} %convert_element_type.102), kind=kOutput, calls=%fused_computation.75 | convolution fusion | flops 2417098752 | bytes 10226688 | tf_op jit(solution)/shard_map/dot_general | solution.py:28
  475.9 41.3 %all-reduce = (f32[768]{0:T(1024)}, f32[768]{0:T(1024)}, f32[768]{0:T(1024)}, f32[3072]{0:T(1024)}, f32[768]{0:T(1024)}, /*index=5*/f32[768]{0:T(1024)}, f32[768]{0:T(1024)}, f32[768]{0:T(1024)}, f32[768]{0:T(1024)}) all-reduce(f32[768]{0:T(1024)S(1)} %reduce_sum.182, ...), channel_id=1, replica_groups=mesh['dp'=8,'tensor'=4] {'dp','tensor'}, use_global_device_ids=true, to_apply=%region_13.14 | all-reduce | flops 9216 | bytes 73728 | tf_op jit(solution)/shard_map/psum | solution.py:342
  (220 shorter events, 143.4 us)
Async XLA Ops:
  7.2 60.6 %all-gather.3.cloned.1.call-start = ((), (), s32[]{:S(2)}) async-start(), calls=%async_computation.3 | async-start | bytes 5308416 | tf_op jit(solution)/shard_map/all_gather | solution.py:55
  9.1 9.4 %collective-permute-start.2 = (bf16[96,768]{1,0:T(8,128)(2,1)S(1)}, bf16[96,768]{1,0:T(8,128)(2,1)S(1)}, u32[]{:S(2)}, u32[]{:S(2)}) collective-permute-start(bf16[96,768]{1,0:T(8,128)(2,1)S(1)} %pad_maximum_fusion.4), channel_id=1, source_target_pairs={{0,3},{1,0},{2,1},{3,2},{4,7},{5,4},{6,5},{7,6},{8,11},{9,8},{10,9... | collective-permute-start | bytes 442376 | tf_op jit(solution)/shard_map/ppermute | solution.py:50
  14.2 12.5 %collective-permute-start.1 = (bf16[96,768]{1,0:T(8,128)(2,1)S(1)}, bf16[96,768]{1,0:T(8,128)(2,1)S(1)}, u32[]{:S(2)}, u32[]{:S(2)}) collective-permute-start(bf16[96,768]{1,0:T(8,128)(2,1)S(1)} %pad_maximum_fusion.4), channel_id=1, source_target_pairs={{0,2},{1,3},{2,0},{3,1},{4,6},{5,7},{6,4},{7,5},{8,10},{9,11},{10,... | collective-permute-start | bytes 442376 | tf_op jit(solution)/shard_map/ppermute | solution.py:50
  14.2 12.5 %collective-permute-start = (bf16[96,768]{1,0:T(8,128)(2,1)S(1)}, bf16[96,768]{1,0:T(8,128)(2,1)S(1)}, u32[]{:S(2)}, u32[]{:S(2)}) collective-permute-start(bf16[96,768]{1,0:T(8,128)(2,1)S(1)} %pad_maximum_fusion.4), channel_id=1, source_target_pairs={{0,1},{1,2},{2,3},{3,0},{4,5},{5,6},{6,7},{7,4},{8,9},{9,10},{10,1... | collective-permute-start | bytes 442376 | tf_op jit(solution)/shard_map/ppermute | solution.py:50
  28.4 142.9 %all-gather.5.cloned.1.call-start = ((), (), s32[]{:S(2)}) async-start(), calls=%async_computation.4 | async-start | bytes 10616832 | tf_op jit(solution)/shard_map/all_gather | solution.py:55
  28.5 8.9 %collective-permute-start.7 = (bf16[96,1536]{1,0:T(8,128)(2,1)S(1)}, bf16[96,1536]{1,0:T(8,128)(2,1)S(1)}, u32[]{:S(2)}, u32[]{:S(2)}) collective-permute-start(bf16[96,1536]{1,0:T(8,128)(2,1)S(1)} %get-tuple-element.143), channel_id=1, source_target_pairs={{0,3},{1,0},{2,1},{3,2},{4,7},{5,4},{6,5},{7,6},{8,11},{9,8},{10,9... | collective-permute-start | bytes 884744 | tf_op jit(solution)/shard_map/ppermute | solution.py:50
  29.9 26.9 %collective-permute-start.6 = (bf16[96,1536]{1,0:T(8,128)(2,1)S(1)}, bf16[96,1536]{1,0:T(8,128)(2,1)S(1)}, u32[]{:S(2)}, u32[]{:S(2)}) collective-permute-start(bf16[96,1536]{1,0:T(8,128)(2,1)S(1)} %get-tuple-element.143), channel_id=1, source_target_pairs={{0,2},{1,3},{2,0},{3,1},{4,6},{5,7},{6,4},{7,5},{8,10},{9,11},{10,... | collective-permute-start | bytes 884744 | tf_op jit(solution)/shard_map/ppermute | solution.py:50
  31.4 25.3 %collective-permute-start.5 = (bf16[96,1536]{1,0:T(8,128)(2,1)S(1)}, bf16[96,1536]{1,0:T(8,128)(2,1)S(1)}, u32[]{:S(2)}, u32[]{:S(2)}) collective-permute-start(bf16[96,1536]{1,0:T(8,128)(2,1)S(1)} %get-tuple-element.143), channel_id=1, source_target_pairs={{0,1},{1,2},{2,3},{3,0},{4,5},{5,6},{6,7},{7,4},{8,9},{9,10},{10,1... | collective-permute-start | bytes 884744 | tf_op jit(solution)/shard_map/ppermute | solution.py:50
  58.8 306.4 %reduce-scatter.4.cloned.1.call-start = ((), (), s32[]{:S(2)}) async-start(), calls=%async_computation.5 | async-start | bytes 5308416 | tf_op jit(solution)/shard_map/reduce_scatter | solution.py:70
  60.6 14.1 %copy-start.29 = (f32[512]{0:T(512)}, f32[512]{0:T(512)S(1)}, u32[]{:S(2)}) copy-start(f32[512]{0:T(512)S(1)} %fusion.31) | copy-start | bytes 6148
  60.7 55.7 %copy-start.26 = (f32[512]{0:T(512)}, f32[512]{0:T(512)S(1)}, u32[]{:S(2)}) copy-start(f32[512]{0:T(512)S(1)} %fusion.39) | copy-start | bytes 6148
  77.6 3.0 copy-start.41
  93.0 9.1 %copy-start.47 = (bf16[768]{0:T(1024)(128)(2,1)S(1)}, bf16[768]{0:T(1024)(128)(2,1)}, u32[]{:S(2)}) copy-start(bf16[768]{0:T(1024)(128)(2,1)} %param.29) | copy-start | bytes 4612
  95.3 40.8 %collective-permute-start.3 = (bf16[12,512,64]{1,2,0:T(8,128)(2,1)}, bf16[12,512,64]{1,2,0:T(8,128)(2,1)}, u32[]{:S(2)}, u32[]{:S(2)}) collective-permute-start(bf16[12,512,64]{1,2,0:T(8,128)(2,1)} %bitcast.162), channel_id=1, source_target_pairs={{0,1},{2,3},{4,5},{6,7},{8,9},{10,11},{12,13},{14,15},{16,17},{18,... | collective-permute-start | bytes 2359304 | tf_op jit(solution)/shard_map/ppermute | solution.py:278
  99.7 38.9 %collective-permute-start.4 = (bf16[12,512,64]{1,2,0:T(8,128)(2,1)}, bf16[12,512,64]{1,2,0:T(8,128)(2,1)}, u32[]{:S(2)}, u32[]{:S(2)}) collective-permute-start(bf16[12,512,64]{1,2,0:T(8,128)(2,1)} %bitcast.164), channel_id=1, source_target_pairs={{0,1},{2,3},{4,5},{6,7},{8,9},{10,11},{12,13},{14,15},{16,17},{18,... | collective-permute-start | bytes 2359304 | tf_op jit(solution)/shard_map/ppermute | solution.py:278
  134.8 110.0 %collective-permute-start.8 = (bf16[12,512,64]{1,2,0:T(8,128)(2,1)}, bf16[12,512,64]{1,2,0:T(8,128)(2,1)}, u32[]{:S(2)}, u32[]{:S(2)}) collective-permute-start(bf16[12,512,64]{1,2,0:T(8,128)(2,1)} %bitcast.60), channel_id=1, source_target_pairs={{1,0},{3,2},{5,4},{7,6},{9,8},{11,10},{13,12},{15,14},{17,16},{19,... | collective-permute-start | bytes 2359304 | tf_op jit(solution)/shard_map/ppermute | solution.py:281
  189.9 18.5 %copy-start.7 = (bf16[96,8,4,768]{3,1,2,0:T(8,128)(2,1)}, bf16[96,8,4,768]{3,1,2,0:T(8,128)(2,1)S(1)}, u32[]{:S(2)}) copy-start(bf16[96,8,4,768]{3,1,2,0:T(8,128)(2,1)S(1)} %copy.166) | copy-start | bytes 14155780
  190.0 18.5 %copy-start.14 = (bf16[512,768]{1,0:T(8,128)(2,1)S(1)}, bf16[512,768]{1,0:T(8,128)(2,1)}, u32[]{:S(2)}) copy-start(bf16[512,768]{1,0:T(8,128)(2,1)} %param.20) | copy-start | bytes 2359300
  208.4 13.4 %copy-start.49 = (bf16[512,3072]{1,0:T(8,128)(2,1)}, bf16[512,3072]{1,0:T(8,128)(2,1)S(1)}, u32[]{:S(2)}) copy-start(bf16[512,3072]{1,0:T(8,128)(2,1)S(1)} %get-tuple-element.121) | copy-start | bytes 9437188
  217.9 3.9 copy-start.20
  233.7 21.4 %copy-start.39 = (f32[512]{0:T(512)}, f32[512]{0:T(512)S(1)}, u32[]{:S(2)}) copy-start(f32[512]{0:T(512)S(1)} %negate_multiply_fusion.2) | copy-start | bytes 6148
  238.9 23.1 %collective-permute-start.9 = (bf16[12,512,64]{1,2,0:T(8,128)(2,1)}, bf16[12,512,64]{1,2,0:T(8,128)(2,1)}, u32[]{:S(2)}, u32[]{:S(2)}) collective-permute-start(bf16[12,512,64]{1,2,0:T(8,128)(2,1)} %bitcast.166), channel_id=1, source_target_pairs={{1,0},{3,2},{5,4},{7,6},{9,8},{11,10},{13,12},{15,14},{17,16},{19,... | collective-permute-start | bytes 2359304 | tf_op jit(solution)/shard_map/ppermute | solution.py:310
  243.6 20.9 %collective-permute-start.10 = (f32[12,512]{1,0:T(8,128)}, f32[12,512]{1,0:T(8,128)}, u32[]{:S(2)}, u32[]{:S(2)}) collective-permute-start(f32[12,512]{1,0:T(8,128)} %slice_reduce_fusion), channel_id=1, source_target_pairs={{1,0},{3,2},{5,4},{7,6},{9,8},{11,10},{13,12},{15,14},{17,16},{19,... | collective-permute-start | bytes 73736 | tf_op jit(solution)/shard_map/ppermute | solution.py:281
  249.8 5.3 %copy-start.4 = (f32[512,768]{1,0:T(8,128)S(1)}, f32[512,768]{1,0:T(8,128)}, u32[]{:S(2)}) copy-start(f32[512,768]{1,0:T(8,128)} %copy-done.3) | copy-start | bytes 4718596
  249.8 5.3 %copy-start.16 = (bf16[512,768]{1,0:T(8,128)(2,1)S(1)}, bf16[512,768]{1,0:T(8,128)(2,1)}, u32[]{:S(2)}) copy-start(bf16[512,768]{1,0:T(8,128)(2,1)} %param.20) | copy-start | bytes 2359300
  249.8 5.3 %copy-start.19 = (bf16[512,12,64]{0,2,1:T(8,128)(2,1)S(1)}, bf16[512,12,64]{0,2,1:T(8,128)(2,1)}, u32[]{:S(2)}) copy-start(bf16[512,12,64]{0,2,1:T(8,128)(2,1)} %copy.131) | copy-start | bytes 2359300
  253.8 10.6 %collective-permute-start.11 = (f32[12,512]{1,0:T(8,128)}, f32[12,512]{1,0:T(8,128)}, u32[]{:S(2)}, u32[]{:S(2)}) collective-permute-start(f32[12,512]{1,0:T(8,128)} %multiply_reduce_fusion), channel_id=1, source_target_pairs={{1,0},{3,2},{5,4},{7,6},{9,8},{11,10},{13,12},{15,14},{17,16},{19,... | collective-permute-start | bytes 73736 | tf_op jit(solution)/shard_map/ppermute | solution.py:310
  305.1 4.0 copy-start.9
  312.0 133.3 %reduce-scatter.6.cloned.1.call-start = ((), (), s32[]{:S(2)}) async-start(), calls=%async_computation.6 | async-start | bytes 10616832 | tf_op jit(solution)/shard_map/reduce_scatter | solution.py:70
  312.6 204.7 %reduce-scatter.8.cloned.1.call-start = ((), (), s32[]{:S(2)}) async-start(), calls=%async_computation.7 | async-start | bytes 2211840 | tf_op jit(solution)/shard_map/reduce_scatter | solution.py:79
  459.6 7.0 %copy-start.1 = (bf16[12,512,64]{2,1,0:T(8,128)(2,1)S(1)}, bf16[12,512,64]{2,1,0:T(8,128)(2,1)}, u32[]{:S(2)}) copy-start(bf16[12,512,64]{2,1,0:T(8,128)(2,1)} %get-tuple-element.29) | copy-start | bytes 2359300
  459.6 7.0 %copy-start.2 = (bf16[12,512,64]{2,1,0:T(8,128)(2,1)S(1)}, bf16[12,512,64]{2,1,0:T(8,128)(2,1)}, u32[]{:S(2)}) copy-start(bf16[12,512,64]{2,1,0:T(8,128)(2,1)} %get-tuple-element.31) | copy-start | bytes 2359300
  (35 other events, 60.1 us)
Sparse Core Ops, SparseCore 0:
  28.5 39.2 all-gather.2
  69.6 58.6 all-gather.4
  312.1 53.0 reduce-scatter.3
  368.6 76.6 reduce-scatter.5
  459.1 38.6 reduce-scatter.7

commit v4 on v3

--- a/solution.py
+++ b/solution.py
@@ -70,13 +70,17 @@
     return lax.psum_scatter(grad.astype(LINK), "dp", scatter_dimension=axis, tiled=True)
 
 
-def scatter_cols_joined(pieces, tp):
+def sum_over_tensor(pieces, tp):
     parts = []
     for piece in pieces:
         r, c = piece.shape
         parts.append(piece.reshape(r, tp, c // tp).transpose(1, 0, 2))
     joined = jnp.concatenate(parts, axis=2)
-    mine = lax.psum_scatter(joined, "tensor", scatter_dimension=0, tiled=False).astype(jnp.float32)
+    t_index = lax.axis_index("tensor")
+    mine = lax.dynamic_index_in_dim(joined, t_index, keepdims=False).astype(jnp.float32)
+    for step in range(1, tp):
+        sent = lax.dynamic_index_in_dim(joined, (t_index + step) % tp, keepdims=False)
+        mine = mine + lax.ppermute(sent, "tensor", [(i, (i + step) % tp) for i in range(tp)]).astype(jnp.float32)
     out = []
     start = 0
     for piece in pieces:
@@ -333,9 +337,9 @@
     norm_one_back = jax.vjp(layer_norm, in_rows, gain_first, shift_first)[1](grad_norm_one)
     grad_input = grad_middle + norm_one_back[0]
 
-    shard_query, shard_key, shard_value, shard_out_t, shard_up, shard_down_t = scatter_cols_joined(
-        [qkv_rows[:, :width], qkv_rows[:, width : 2 * width], qkv_rows[:, 2 * width :], out_rows, up_rows, down_rows],
-        tp,
+    shard_up, shard_down_t = sum_over_tensor([up_rows, down_rows], tp)
+    shard_query, shard_key, shard_value, shard_out_t = sum_over_tensor(
+        [qkv_rows[:, :width], qkv_rows[:, width : 2 * width], qkv_rows[:, 2 * width :], out_rows], tp
     )
     shard_out = shard_out_t.T
     shard_down = shard_down_t.T

time: 536 us -> 495 us (0.924)
  waiting for transfers between devices: 166 us -> 135 us
  local copies, waits for them, and re-layouts: 138 us -> 117 us
  starting transfers between devices: 23.3 us -> 31.4 us
    reduce_scatter x2, waiting for transfers between devices: 120 us -> 68.6 us  [scatter_rows(): lax.psum_scatter(grad.astype(LINK), 'dp', scatter_dimension=axis, tiled=T...]
    ppermute x0 -> x6, waiting for transfers between devices: none -> 20.2 us  [sum_over_tensor(): lax.ppermute(sent, 'tensor', [(i, (i + step) % tp) for i in range(tp)])]
    ppermute x0 -> x6, starting transfers between devices: none -> 8.13 us  [sum_over_tensor(): lax.ppermute(sent, 'tensor', [(i, (i + step) % tp) for i in range(tp)])]
    reshape x4, local copies, waits for them, and re-layouts: 7.15 us -> 0.67 us  [sum_over_tensor(): parts.append(piece.reshape(r, tp, c // tp).transpose(1, 0, 2))]
    transpose x3 -> x1, local copies, waits for them, and re-layouts: 6.15 us -> 0.12 us  [sum_over_tensor(): parts.append(piece.reshape(r, tp, c // tp).transpose(1, 0, 2))]
  transfers between devices with their start and end apart: 17 -> 22, of which waited for: 8 -> 9; matrix products, arithmetic and copies ran while one was open for 35% -> 38% of each run, Pallas kernels for 4% -> 5%
where the time goes in v4:
time: 495 us; the launch traced here: 486 us
  waiting for transfers between devices  135 us (27%)
  local copies, waits for them, and re-layouts  117 us (24%)
  matrix products  69 us (14%)
  Pallas kernels  46.9 us (9%)
  blocking collectives  41.3 us (8%)
  starting transfers between devices  31.4 us (6%)
  other arithmetic  30.9 us (6%)
  between operations  15 us (3%)
    reduce_scatter x2, waiting for transfers between devices, scatter_rows(): lax.psum_scatter(grad.astype(LINK), 'dp', scatter_dimension=axis, tiled=T...  68.6 us
    psum x1, blocking collectives, layer(): lax.psum((jnp.sum(grad_q, axis=0, dtype=f32), jnp.sum(grad_v, axis=0, dty...  41.3 us
    dot_general x6, matrix products, dot_right(): return jnp.dot(first_op, second_op, preferred_element_type=jnp.float32)  35.2 us
    ppermute x6, waiting for transfers between devices, gather_joined(): lax.ppermute(joined, 'tensor', [(i, (i + step) % tp) for i in range(tp)])  33.9 us
    transpose x8, local copies, waits for them, and re-layouts, gather_joined(): out.append(block.transpose(0, 2, 1, 3).reshape(dp * r, tp * c))  33.7 us
    pallas_call x1, Pallas kernels, attention_backward(): pl.pallas_call(attn_bwd_kernel, out_shape=tuple((jax.ShapeDtypeStruct(q.s...  24.7 us
    pallas_call x1, Pallas kernels, attention_forward(): pl.pallas_call(attn_fwd_kernel, out_shape=(jax.ShapeDtypeStruct(q.shape,...  22.3 us
    ppermute x6, waiting for transfers between devices, sum_over_tensor(): lax.ppermute(sent, 'tensor', [(i, (i + step) % tp) for i in range(tp)])  20.2 us
  transfers between devices with their start and end apart: 22, of which 9 were waited for; matrix products, arithmetic and copies ran while one was open for 38% of the time, Pallas kernels for 5%

profile of v4, /device:TPU:0, one launch (start us, length us, event | category | flops | bytes accessed | tf_op | source)
XLA Modules:
  0.0 486.2 jit_solution(2466976372590400056)
XLA Ops:
  9.1 5.1 %collective-permute-start.2 = (bf16[96,768]{1,0:T(8,128)(2,1)S(1)}, bf16[96,768]{1,0:T(8,128)(2,1)S(1)}, u32[]{:S(2)}, u32[]{:S(2)}) collective-permute-start(bf16[96,768]{1,0:T(8,128)(2,1)S(1)} %pad_maximum_fusion.5), channel_id=1, source_target_pairs={{0,3},{1,0},{2,1},{3,2},{4,7},{5,4},{6,5},{7,6},{8,11},{9,8},{10,9... | collective-permute-start | bytes 442376 | tf_op jit(solution)/shard_map/ppermute | solution.py:50
  18.5 8.2 %collective-permute-done.1 = bf16[96,768]{1,0:T(8,128)(2,1)S(1)} collective-permute-done((bf16[96,768]{1,0:T(8,128)(2,1)S(1)}, bf16[96,768]{1,0:T(8,128)(2,1)S(1)}, u32[]{:S(2)}, u32[]{:S(2)}) %collective-permute-start.1) | collective-permute-done | bytes 147488 | tf_op jit(solution)/shard_map/ppermute | solution.py:50
  33.4 4.0 collective-permute-done.7
  37.4 19.4 %collective-permute-done.6 = bf16[96,1536]{1,0:T(8,128)(2,1)S(1)} collective-permute-done((bf16[96,1536]{1,0:T(8,128)(2,1)S(1)}, bf16[96,1536]{1,0:T(8,128)(2,1)S(1)}, u32[]{:S(2)}, u32[]{:S(2)}) %collective-permute-start.6) | collective-permute-done | bytes 294944 | tf_op jit(solution)/shard_map/ppermute | solution.py:50
  60.7 7.1 %all-gather.3.cloned.1.call-done = bf16[8,4,96,768]{3,2,1,0:T(8,128)(2,1)} async-done(((bf16[1,4,96,768]{3,2,1,0:T(8,128)(2,1)}), bf16[8,4,96,768]{3,2,1,0:T(8,128)(2,1)}) %all-gather.3.cloned.1.call-update) | async-done | bytes 4718608 | tf_op jit(solution)/shard_map/all_gather | solution.py:55
  67.7 7.0 %slice_bitcast_fusion.2 = (bf16[8,96,4,192]{3,1,2,0:T(8,128)(2,1)S(1)}, bf16[8,96,4,192]{3,1,2,0:T(8,128)(2,1)}, bf16[8,96,4,192]{3,1,2,0:T(8,128)(2,1)}, bf16[8,96,4,192]{3,1,2,0:T(8,128)(2,1)}) fusion(bf16[8,4,96,768]{3,2,1,0:T(8,128)(2,1)} %all-gather.3.cloned.1.call-done), kind=kLoop, calls=%fused_computation.72 | loop fusion | bytes 9437184 | tf_op jit(solution)/shard_map/transpose | solution.py:61
  77.6 3.0 reshape.236
  87.5 2.9 reshape.238
  95.3 4.4 collective-permute-start.3
  112.5 3.8 reshape.234
  116.3 3.1 add_convert_fusion.3
  130.8 3.8 reshape.241
  140.9 22.3 %shard_map.305 = (bf16[12,512,64]{2,1,0:T(8,128)(2,1)}, f32[12,512,64]{2,1,0:T(8,128)}, f32[12,512,128]{2,1,0:T(8,128)}) custom-call(s32[2]{0:T(128)} %pad_add_fusion.meta_ref, bf16[12,512,64]{2,1,0:T(8,128)(2,1)} %bitcast.173, bf16[12,512,64]{2,1,0:T(8,128)(2,1)} %bitcast.175, bf16[12,512,64]{2,1,0:T(8,128)(2,1)} %bitcast.177, ...), custom_call_target="tpu_custom_call" | custom-call | flops 1610612736 | bytes 9437184 | tf_op jit(solution)/shard_map/pallas_call | solution.py:181
  171.1 6.8 %slice_bitcast_fusion = (bf16[8,96,4,768]{3,1,2,0:T(8,128)(2,1)S(1)}, bf16[8,96,4,768]{3,1,2,0:T(8,128)(2,1)}) fusion(bf16[8,4,96,1536]{3,2,1,0:T(8,128)(2,1)} %all-gather.5.cloned.1.call-done), kind=kLoop, calls=%fused_computation.33 | loop fusion | bytes 18874368 | tf_op jit(solution)/shard_map/transpose | solution.py:61
  177.9 6.0 %copy.139 = bf16[8,96,4,768]{3,2,1,0:T(4,128)(2,1)S(1)} copy(bf16[8,96,4,768]{3,1,2,0:T(8,128)(2,1)} %get-tuple-element.124) | data formatting | bytes 9437184 | tf_op jit(solution)/shard_map/transpose | solution.py:61
  185.0 3.6 copy.140
  189.8 18.5 %multiply_convert_fusion = (bf16[512,3072]{1,0:T(8,128)(2,1)S(1)}, f32[512,3072]{1,0:T(8,128)}, f32[512,3072]{1,0:T(8,128)}) fusion(f32[3072]{0:T(1024)S(1)} %copy-done.37, bf16[768,3072]{1,0:T(8,128)(2,1)S(1)} %bitcast.181, f32[512,768]{1,0:T(8,128)S(1)} %get-tuple-element.151, f32[768]{0:T(1024)S(1)} %copy-done.34, f32[768]{0:T(1024)S(1)} %convert_element_type.121, ...), kind=kOutput, calls=%fused_computation.18 | convolution fusion | flops 2521694208 | bytes 22042624 | tf_op jit(solution)/shard_map/dot_general | solution.py:28
  208.3 9.5 %convert_reduce_fusion = (f32[3072]{0:T(1024)}, bf16[512,3072]{1,0:T(8,128)(2,1)S(1)}) fusion(f32[512,3072]{1,0:T(8,128)} %get-tuple-element.122, bf16[512,768]{1,0:T(8,128)(2,1)S(1)} %copy-done.14, bf16[768,3072]{1,0:T(8,128)(2,1)S(1)} %bitcast.179, f32[512,3072]{1,0:T(8,128)} %get-tuple-element.152, f32[3072]{0:T(1024)S(1)} %copy-done.37), kind=kOutput, calls=%fused_computation.17 | convolution fusion | flops 2442654720 | bytes 21258240 | tf_op jit(solution)/shard_map/dot_general | solution.py:32
  217.7 3.9 fusion.73
  221.6 8.4 %fusion.1 = bf16[2,768,3072]{2,1,0:T(8,128)(2,1)} fusion(bf16[1,512,3072]{2,1,0:T(8,128)(2,1)S(1)} %bitcast.213, bf16[1,512,3072]{2,1,0:T(8,128)(2,1)S(1)} %bitcast.214, bf16[1,512,768]{2,1,0:T(8,128)(2,1)S(1)} %bitcast.193, bf16[1,512,768]{2,1,0:T(8,128)(2,1)S(1)} %copy-done.20), kind=kOutput, calls=%fused_computation.4 | convolution fusion | flops 4835770368 | bytes 17301504 | tf_op jit(solution)/shard_map/dot_general | solution.py:296
  240.0 3.4 slice_reduce_fusion
  249.6 4.0 multiply_reduce_fusion
  257.0 5.0 %collective-permute-done.9 = bf16[12,512,64]{1,2,0:T(8,128)(2,1)} collective-permute-done((bf16[12,512,64]{1,2,0:T(8,128)(2,1)}, bf16[12,512,64]{1,2,0:T(8,128)(2,1)}, u32[]{:S(2)}, u32[]{:S(2)}) %collective-permute-start.9) | collective-permute-done | bytes 786464 | tf_op jit(solution)/shard_map/ppermute | solution.py:314
  264.4 2.9 broadcast_in_dim.40.dl_ref
  270.1 2.9 broadcast_in_dim.42.dlr_ref
  273.0 24.7 %shard_map.306 = (bf16[12,512,64]{2,1,0:T(8,128)(2,1)}, bf16[12,512,64]{2,1,0:T(8,128)(2,1)}, bf16[12,512,64]{2,1,0:T(8,128)(2,1)}) custom-call(s32[2]{0:T(128)} %pad_add_fusion.meta_ref, bf16[12,512,64]{2,1,0:T(8,128)(2,1)} %bitcast.174, bf16[12,512,64]{2,1,0:T(8,128)(2,1)} %bitcast.176, bf16[12,512,64]{2,1,0:T(8,128)(2,1)} %bitcast.178, ...), custom_call_target="tpu_custom_call" | custom-call | flops 4026531840 | bytes 21233664 | tf_op jit(solution)/shard_map/pallas_call | solution.py:206
  304.9 4.0 convolution_convert_fusion
  312.5 7.0 %add_convert_fusion = bf16[512,768]{1,0:T(8,128)(2,1)} fusion(f32[512,768]{1,0:T(8,128)S(1)} %get-tuple-element.151, bf16[512,3072]{1,0:T(8,128)(2,1)} %copy-done.49, bf16[768,3072]{1,0:T(8,128)(2,1)} %bitcast.180, f32[768]{0:T(1024)S(1)} %convert_element_type.126), kind=kOutput, calls=%fused_computation.83 | convolution fusion | flops 2417098752 | bytes 10226688 | tf_op jit(solution)/shard_map/dot_general | solution.py:28
  329.2 41.3 %all-reduce = (f32[768]{0:T(1024)}, f32[768]{0:T(1024)}, f32[768]{0:T(1024)}, f32[3072]{0:T(1024)}, f32[768]{0:T(1024)}, /*index=5*/f32[768]{0:T(1024)}, f32[768]{0:T(1024)}, f32[768]{0:T(1024)}, f32[768]{0:T(1024)}) all-reduce(f32[768]{0:T(1024)S(1)} %reduce_sum.182, ...), channel_id=1, replica_groups=mesh['dp'=8,'tensor'=4] {'dp','tensor'}, use_global_device_ids=true, to_apply=%region_12.13 | all-reduce | flops 9216 | bytes 73728 | tf_op jit(solution)/shard_map/psum | solution.py:346
  376.9 68.6 %reduce-scatter.5.cloned.1.call-done = bf16[2,96,3072]{2,1,0:T(8,128)(2,1)} async-done(((bf16[2,768,3072]{2,1,0:T(8,128)(2,1)}), bf16[2,96,3072]{2,1,0:T(8,128)(2,1)}) %reduce-scatter.5.cloned.1.call-update) | async-done | bytes 1179664 | tf_op jit(solution)/shard_map/reduce_scatter | solution.py:70
  448.6 3.3 collective-permute-start.17
  459.7 17.6 %collective-permute-done.16 = bf16[96,1536]{1,0:T(8,128)(2,1)S(1)} collective-permute-done((bf16[96,1536]{1,0:T(8,128)(2,1)S(1)}, bf16[96,1536]{1,0:T(8,128)(2,1)S(1)}, u32[]{:S(2)}, u32[]{:S(2)}) %collective-permute-start.16) | collective-permute-done | bytes 294944 | tf_op jit(solution)/shard_map/ppermute | solution.py:83
  (232 shorter events, 135.8 us)
Async XLA Ops:
  7.2 60.6 %all-gather.3.cloned.1.call-start = ((), (), s32[]{:S(2)}) async-start(), calls=%async_computation.2 | async-start | bytes 5308416 | tf_op jit(solution)/shard_map/all_gather | solution.py:55
  9.1 9.4 %collective-permute-start.2 = (bf16[96,768]{1,0:T(8,128)(2,1)S(1)}, bf16[96,768]{1,0:T(8,128)(2,1)S(1)}, u32[]{:S(2)}, u32[]{:S(2)}) collective-permute-start(bf16[96,768]{1,0:T(8,128)(2,1)S(1)} %pad_maximum_fusion.5), channel_id=1, source_target_pairs={{0,3},{1,0},{2,1},{3,2},{4,7},{5,4},{6,5},{7,6},{8,11},{9,8},{10,9... | collective-permute-start | bytes 442376 | tf_op jit(solution)/shard_map/ppermute | solution.py:50
  14.2 12.5 %collective-permute-start.1 = (bf16[96,768]{1,0:T(8,128)(2,1)S(1)}, bf16[96,768]{1,0:T(8,128)(2,1)S(1)}, u32[]{:S(2)}, u32[]{:S(2)}) collective-permute-start(bf16[96,768]{1,0:T(8,128)(2,1)S(1)} %pad_maximum_fusion.5), channel_id=1, source_target_pairs={{0,2},{1,3},{2,0},{3,1},{4,6},{5,7},{6,4},{7,5},{8,10},{9,11},{10,... | collective-permute-start | bytes 442376 | tf_op jit(solution)/shard_map/ppermute | solution.py:50
  14.2 12.5 %collective-permute-start = (bf16[96,768]{1,0:T(8,128)(2,1)S(1)}, bf16[96,768]{1,0:T(8,128)(2,1)S(1)}, u32[]{:S(2)}, u32[]{:S(2)}) collective-permute-start(bf16[96,768]{1,0:T(8,128)(2,1)S(1)} %pad_maximum_fusion.5), channel_id=1, source_target_pairs={{0,1},{1,2},{2,3},{3,0},{4,5},{5,6},{6,7},{7,4},{8,9},{9,10},{10,1... | collective-permute-start | bytes 442376 | tf_op jit(solution)/shard_map/ppermute | solution.py:50
  28.4 142.7 %all-gather.5.cloned.1.call-start = ((), (), s32[]{:S(2)}) async-start(), calls=%async_computation.3 | async-start | bytes 10616832 | tf_op jit(solution)/shard_map/all_gather | solution.py:55
  28.5 8.9 %collective-permute-start.7 = (bf16[96,1536]{1,0:T(8,128)(2,1)S(1)}, bf16[96,1536]{1,0:T(8,128)(2,1)S(1)}, u32[]{:S(2)}, u32[]{:S(2)}) collective-permute-start(bf16[96,1536]{1,0:T(8,128)(2,1)S(1)} %get-tuple-element.149), channel_id=1, source_target_pairs={{0,3},{1,0},{2,1},{3,2},{4,7},{5,4},{6,5},{7,6},{8,11},{9,8},{10,9... | collective-permute-start | bytes 884744 | tf_op jit(solution)/shard_map/ppermute | solution.py:50
  29.9 26.9 %collective-permute-start.6 = (bf16[96,1536]{1,0:T(8,128)(2,1)S(1)}, bf16[96,1536]{1,0:T(8,128)(2,1)S(1)}, u32[]{:S(2)}, u32[]{:S(2)}) collective-permute-start(bf16[96,1536]{1,0:T(8,128)(2,1)S(1)} %get-tuple-element.149), channel_id=1, source_target_pairs={{0,2},{1,3},{2,0},{3,1},{4,6},{5,7},{6,4},{7,5},{8,10},{9,11},{10,... | collective-permute-start | bytes 884744 | tf_op jit(solution)/shard_map/ppermute | solution.py:50
  31.4 25.3 %collective-permute-start.5 = (bf16[96,1536]{1,0:T(8,128)(2,1)S(1)}, bf16[96,1536]{1,0:T(8,128)(2,1)S(1)}, u32[]{:S(2)}, u32[]{:S(2)}) collective-permute-start(bf16[96,1536]{1,0:T(8,128)(2,1)S(1)} %get-tuple-element.149), channel_id=1, source_target_pairs={{0,1},{1,2},{2,3},{3,0},{4,5},{5,6},{6,7},{7,4},{8,9},{9,10},{10,1... | collective-permute-start | bytes 884744 | tf_op jit(solution)/shard_map/ppermute | solution.py:50
  58.8 311.6 %reduce-scatter.3.cloned.1.call-start = ((), (), s32[]{:S(2)}) async-start(), calls=%async_computation.4 | async-start | bytes 5308416 | tf_op jit(solution)/shard_map/reduce_scatter | solution.py:70
  60.6 14.1 %copy-start.29 = (f32[512]{0:T(512)}, f32[512]{0:T(512)S(1)}, u32[]{:S(2)}) copy-start(f32[512]{0:T(512)S(1)} %fusion.31) | copy-start | bytes 6148
  60.7 55.6 %copy-start.26 = (f32[512]{0:T(512)}, f32[512]{0:T(512)S(1)}, u32[]{:S(2)}) copy-start(f32[512]{0:T(512)S(1)} %fusion.51) | copy-start | bytes 6148
  93.0 9.1 %copy-start.47 = (bf16[768]{0:T(1024)(128)(2,1)S(1)}, bf16[768]{0:T(1024)(128)(2,1)}, u32[]{:S(2)}) copy-start(bf16[768]{0:T(1024)(128)(2,1)} %param.29) | copy-start | bytes 4612
  95.3 40.6 %collective-permute-start.3 = (bf16[12,512,64]{1,2,0:T(8,128)(2,1)}, bf16[12,512,64]{1,2,0:T(8,128)(2,1)}, u32[]{:S(2)}, u32[]{:S(2)}) collective-permute-start(bf16[12,512,64]{1,2,0:T(8,128)(2,1)} %bitcast.183), channel_id=1, source_target_pairs={{0,1},{2,3},{4,5},{6,7},{8,9},{10,11},{12,13},{14,15},{16,17},{18,... | collective-permute-start | bytes 2359304 | tf_op jit(solution)/shard_map/ppermute | solution.py:282
  99.7 38.7 %collective-permute-start.4 = (bf16[12,512,64]{1,2,0:T(8,128)(2,1)}, bf16[12,512,64]{1,2,0:T(8,128)(2,1)}, u32[]{:S(2)}, u32[]{:S(2)}) collective-permute-start(bf16[12,512,64]{1,2,0:T(8,128)(2,1)} %bitcast.185), channel_id=1, source_target_pairs={{0,1},{2,3},{4,5},{6,7},{8,9},{10,11},{12,13},{14,15},{16,17},{18,... | collective-permute-start | bytes 2359304 | tf_op jit(solution)/shard_map/ppermute | solution.py:282
  134.6 110.0 %collective-permute-start.8 = (bf16[12,512,64]{1,2,0:T(8,128)(2,1)}, bf16[12,512,64]{1,2,0:T(8,128)(2,1)}, u32[]{:S(2)}, u32[]{:S(2)}) collective-permute-start(bf16[12,512,64]{1,2,0:T(8,128)(2,1)} %bitcast.70), channel_id=1, source_target_pairs={{1,0},{3,2},{5,4},{7,6},{9,8},{11,10},{13,12},{15,14},{17,16},{19,... | collective-permute-start | bytes 2359304 | tf_op jit(solution)/shard_map/ppermute | solution.py:285
  189.7 18.6 %copy-start.7 = (bf16[96,8,4,768]{3,1,2,0:T(8,128)(2,1)}, bf16[96,8,4,768]{3,1,2,0:T(8,128)(2,1)S(1)}, u32[]{:S(2)}) copy-start(bf16[96,8,4,768]{3,1,2,0:T(8,128)(2,1)S(1)} %copy.178) | copy-start | bytes 14155780
  189.7 18.5 %copy-start.14 = (bf16[512,768]{1,0:T(8,128)(2,1)S(1)}, bf16[512,768]{1,0:T(8,128)(2,1)}, u32[]{:S(2)}) copy-start(bf16[512,768]{1,0:T(8,128)(2,1)} %param.20) | copy-start | bytes 2359300
  208.3 13.3 %copy-start.49 = (bf16[512,3072]{1,0:T(8,128)(2,1)}, bf16[512,3072]{1,0:T(8,128)(2,1)S(1)}, u32[]{:S(2)}) copy-start(bf16[512,3072]{1,0:T(8,128)(2,1)S(1)} %get-tuple-element.121) | copy-start | bytes 9437188
  233.5 21.4 %copy-start.39 = (f32[512]{0:T(512)}, f32[512]{0:T(512)S(1)}, u32[]{:S(2)}) copy-start(f32[512]{0:T(512)S(1)} %negate_multiply_fusion.2) | copy-start | bytes 6148
  238.7 23.2 %collective-permute-start.9 = (bf16[12,512,64]{1,2,0:T(8,128)(2,1)}, bf16[12,512,64]{1,2,0:T(8,128)(2,1)}, u32[]{:S(2)}, u32[]{:S(2)}) collective-permute-start(bf16[12,512,64]{1,2,0:T(8,128)(2,1)} %bitcast.187), channel_id=1, source_target_pairs={{1,0},{3,2},{5,4},{7,6},{9,8},{11,10},{13,12},{15,14},{17,16},{19,... | collective-permute-start | bytes 2359304 | tf_op jit(solution)/shard_map/ppermute | solution.py:314
  243.4 21.0 %collective-permute-start.10 = (f32[12,512]{1,0:T(8,128)}, f32[12,512]{1,0:T(8,128)}, u32[]{:S(2)}, u32[]{:S(2)}) collective-permute-start(f32[12,512]{1,0:T(8,128)} %slice_reduce_fusion), channel_id=1, source_target_pairs={{1,0},{3,2},{5,4},{7,6},{9,8},{11,10},{13,12},{15,14},{17,16},{19,... | collective-permute-start | bytes 73736 | tf_op jit(solution)/shard_map/ppermute | solution.py:285
  249.6 5.3 %copy-start.19 = (bf16[512,12,64]{0,2,1:T(8,128)(2,1)S(1)}, bf16[512,12,64]{0,2,1:T(8,128)(2,1)}, u32[]{:S(2)}) copy-start(bf16[512,12,64]{0,2,1:T(8,128)(2,1)} %copy.137) | copy-start | bytes 2359300
  253.6 10.8 %collective-permute-start.11 = (f32[12,512]{1,0:T(8,128)}, f32[12,512]{1,0:T(8,128)}, u32[]{:S(2)}, u32[]{:S(2)}) collective-permute-start(f32[12,512]{1,0:T(8,128)} %multiply_reduce_fusion), channel_id=1, source_target_pairs={{1,0},{3,2},{5,4},{7,6},{9,8},{11,10},{13,12},{15,14},{17,16},{19,... | collective-permute-start | bytes 73736 | tf_op jit(solution)/shard_map/ppermute | solution.py:314
  311.8 133.7 %reduce-scatter.5.cloned.1.call-start = ((), (), s32[]{:S(2)}) async-start(), calls=%async_computation.5 | async-start | bytes 10616832 | tf_op jit(solution)/shard_map/reduce_scatter | solution.py:70
  312.5 7.0 %copy-start.1 = (bf16[12,512,64]{2,1,0:T(8,128)(2,1)S(1)}, bf16[12,512,64]{2,1,0:T(8,128)(2,1)}, u32[]{:S(2)}) copy-start(bf16[12,512,64]{2,1,0:T(8,128)(2,1)} %get-tuple-element.29) | copy-start | bytes 2359300
  312.5 7.0 %copy-start.2 = (bf16[12,512,64]{2,1,0:T(8,128)(2,1)S(1)}, bf16[12,512,64]{2,1,0:T(8,128)(2,1)}, u32[]{:S(2)}) copy-start(bf16[12,512,64]{2,1,0:T(8,128)(2,1)} %get-tuple-element.31) | copy-start | bytes 2359300
  373.2 78.7 %collective-permute-start.14 = (bf16[96,768]{0,1:T(8,128)(2,1)}, bf16[96,768]{0,1:T(8,128)(2,1)}, u32[]{:S(2)}, u32[]{:S(2)}) collective-permute-start(bf16[96,768]{0,1:T(8,128)(2,1)} %get-tuple-element.136), channel_id=1, source_target_pairs={{0,3},{1,0},{2,1},{3,2},{4,7},{5,4},{6,5},{7,6},{8,11},{9,8},{10,9... | collective-permute-start | bytes 442376 | tf_op jit(solution)/shard_map/ppermute | solution.py:83
  375.8 77.2 %collective-permute-start.13 = (bf16[96,768]{0,1:T(8,128)(2,1)S(1)}, bf16[96,768]{0,1:T(8,128)(2,1)}, u32[]{:S(2)}, u32[]{:S(2)}) collective-permute-start(bf16[96,768]{0,1:T(8,128)(2,1)S(1)} %get-tuple-element.137), channel_id=1, source_target_pairs={{0,2},{1,3},{2,0},{3,1},{4,6},{5,7},{6,4},{7,5},{8,10},{9,11},{10,... | collective-permute-start | bytes 442376 | tf_op jit(solution)/shard_map/ppermute | solution.py:83
  375.8 77.2 %collective-permute-start.12 = (bf16[96,768]{0,1:T(8,128)(2,1)S(1)}, bf16[96,768]{0,1:T(8,128)(2,1)}, u32[]{:S(2)}, u32[]{:S(2)}) collective-permute-start(bf16[96,768]{0,1:T(8,128)(2,1)S(1)} %get-tuple-element.135), channel_id=1, source_target_pairs={{0,1},{1,2},{2,3},{3,0},{4,5},{5,6},{6,7},{7,4},{8,9},{9,10},{10,1... | collective-permute-start | bytes 442376 | tf_op jit(solution)/shard_map/ppermute | solution.py:83
  448.6 11.1 %collective-permute-start.17 = (bf16[96,1536]{1,0:T(8,128)(2,1)}, bf16[96,1536]{1,0:T(8,128)(2,1)S(1)}, u32[]{:S(2)}, u32[]{:S(2)}) collective-permute-start(bf16[96,1536]{1,0:T(8,128)(2,1)} %get-tuple-element.132), channel_id=1, source_target_pairs={{0,3},{1,0},{2,1},{3,2},{4,7},{5,4},{6,5},{7,6},{8,11},{9,8},{10,9... | collective-permute-start | bytes 884744 | tf_op jit(solution)/shard_map/ppermute | solution.py:83
  451.9 25.3 %collective-permute-start.16 = (bf16[96,1536]{1,0:T(8,128)(2,1)S(1)}, bf16[96,1536]{1,0:T(8,128)(2,1)S(1)}, u32[]{:S(2)}, u32[]{:S(2)}) collective-permute-start(bf16[96,1536]{1,0:T(8,128)(2,1)S(1)} %get-tuple-element.131), channel_id=1, source_target_pairs={{0,2},{1,3},{2,0},{3,1},{4,6},{5,7},{6,4},{7,5},{8,10},{9,11},{10,... | collective-permute-start | bytes 884744 | tf_op jit(solution)/shard_map/ppermute | solution.py:83
  451.9 25.3 %collective-permute-start.15 = (bf16[96,1536]{1,0:T(8,128)(2,1)S(1)}, bf16[96,1536]{1,0:T(8,128)(2,1)}, u32[]{:S(2)}, u32[]{:S(2)}) collective-permute-start(bf16[96,1536]{1,0:T(8,128)(2,1)S(1)} %get-tuple-element.130), channel_id=1, source_target_pairs={{0,1},{1,2},{2,3},{3,0},{4,5},{5,6},{6,7},{7,4},{8,9},{9,10},{10,1... | collective-permute-start | bytes 884744 | tf_op jit(solution)/shard_map/ppermute | solution.py:83
  (40 other events, 82.0 us)
Sparse Core Ops, SparseCore 0:
  28.5 39.2 all-gather.2
  69.6 58.6 all-gather.4
  312.0 53.4 reduce-scatter.2
  368.8 76.6 reduce-scatter.4

commit v5 on v4

--- a/solution.py
+++ b/solution.py
@@ -38,9 +38,6 @@
     return lax.dot_general(
         first_op, second_op, (((0,), (0,)), ((), ())), preferred_element_type=jnp.float32
     )
-
-
-AXES = ("dp", "tensor")
 
 
 def gather_joined(shards, dp, tp):
@@ -343,8 +340,7 @@
     )
     shard_out = shard_out_t.T
     shard_down = shard_down_t.T
-    vector_sums = lax.psum(
-        (
+    vectors = [
         jnp.sum(grad_q, axis=0, dtype=f32),
         jnp.sum(grad_v, axis=0, dtype=f32),
         jnp.sum(grad_middle, axis=0),
@@ -354,9 +350,16 @@
         norm_one_back[2],
         norm_two_back[1],
         norm_two_back[2],
-        ),
-        AXES,
-    )
+    ]
+    joined = lax.psum(jnp.concatenate(vectors), "dp")
+    total = joined
+    for step in range(1, tp):
+        total = total + lax.ppermute(joined, "tensor", [(i, (i + step) % tp) for i in range(tp)])
+    vector_sums = []
+    start = 0
+    for v in vectors:
+        vector_sums.append(total[start : start + v.shape[0]])
+        start += v.shape[0]
     return (
         result,
         grad_input,

time: 495 us -> 494 us (level)
  blocking collectives: 41.3 us -> 24.1 us
  local copies, waits for them, and re-layouts: 117 us -> 122 us
    psum x1, blocking collectives: 41.3 us -> 24.1 us  [layer(): joined = lax.psum(jnp.concatenate(vectors), 'dp')]
    unnamed x106 -> x112, local copies, waits for them, and re-layouts: 9.43 us -> 11.5 us
  transfers between devices with their start and end apart: 22 -> 25, of which waited for: 9 -> 9; matrix products, arithmetic and copies ran while one was open for 38% -> 40% of each run, Pallas kernels for 5% -> 5%
where the time goes in v5:
time: 494 us; the launch traced here: 486 us
  waiting for transfers between devices  139 us (28%)
  local copies, waits for them, and re-layouts  122 us (25%)
  matrix products  69.5 us (14%)
  Pallas kernels  46.9 us (9%)
  starting transfers between devices  36.1 us (7%)
  other arithmetic  33.3 us (7%)
  blocking collectives  24.1 us (5%)
  between operations  15.1 us (3%)
    reduce_scatter x2, waiting for transfers between devices, scatter_rows(): lax.psum_scatter(grad.astype(LINK), 'dp', scatter_dimension=axis, tiled=T...  72.6 us
    dot_general x6, matrix products, dot_right(): return jnp.dot(first_op, second_op, preferred_element_type=jnp.float32)  35.2 us
    ppermute x6, waiting for transfers between devices, gather_joined(): lax.ppermute(joined, 'tensor', [(i, (i + step) % tp) for i in range(tp)])  33.9 us
    transpose x8, local copies, waits for them, and re-layouts, gather_joined(): out.append(block.transpose(0, 2, 1, 3).reshape(dp * r, tp * c))  33.7 us
    pallas_call x1, Pallas kernels, attention_backward(): pl.pallas_call(attn_bwd_kernel, out_shape=tuple((jax.ShapeDtypeStruct(q.s...  24.7 us
    psum x1, blocking collectives, layer(): joined = lax.psum(jnp.concatenate(vectors), 'dp')  24.1 us
    pallas_call x1, Pallas kernels, attention_forward(): pl.pallas_call(attn_fwd_kernel, out_shape=(jax.ShapeDtypeStruct(q.shape,...  22.3 us
    ppermute x6, waiting for transfers between devices, sum_over_tensor(): lax.ppermute(sent, 'tensor', [(i, (i + step) % tp) for i in range(tp)])  19.9 us
  transfers between devices with their start and end apart: 25, of which 9 were waited for; matrix products, arithmetic and copies ran while one was open for 40% of the time, Pallas kernels for 5%

profile of v5, /device:TPU:0, one launch (start us, length us, event | category | flops | bytes accessed | tf_op | source)
XLA Modules:
  0.0 485.6 jit_solution(7618140292109693513)
XLA Ops:
  9.1 5.1 %collective-permute-start.2 = (bf16[96,768]{1,0:T(8,128)(2,1)S(1)}, bf16[96,768]{1,0:T(8,128)(2,1)S(1)}, u32[]{:S(2)}, u32[]{:S(2)}) collective-permute-start(bf16[96,768]{1,0:T(8,128)(2,1)S(1)} %pad_maximum_fusion.5), channel_id=1, source_target_pairs={{0,3},{1,0},{2,1},{3,2},{4,7},{5,4},{6,5},{7,6},{8,11},{9,8},{10,9... | collective-permute-start | bytes 442376 | tf_op jit(solution)/shard_map/ppermute | solution.py:47
  18.5 8.2 %collective-permute-done.1 = bf16[96,768]{1,0:T(8,128)(2,1)S(1)} collective-permute-done((bf16[96,768]{1,0:T(8,128)(2,1)S(1)}, bf16[96,768]{1,0:T(8,128)(2,1)S(1)}, u32[]{:S(2)}, u32[]{:S(2)}) %collective-permute-start.1) | collective-permute-done | bytes 147488 | tf_op jit(solution)/shard_map/ppermute | solution.py:47
  33.4 4.0 collective-permute-done.7
  37.4 19.4 %collective-permute-done.6 = bf16[96,1536]{1,0:T(8,128)(2,1)S(1)} collective-permute-done((bf16[96,1536]{1,0:T(8,128)(2,1)S(1)}, bf16[96,1536]{1,0:T(8,128)(2,1)S(1)}, u32[]{:S(2)}, u32[]{:S(2)}) %collective-permute-start.6) | collective-permute-done | bytes 294944 | tf_op jit(solution)/shard_map/ppermute | solution.py:47
  60.7 7.1 %all-gather.3.cloned.1.call-done = bf16[8,4,96,768]{3,2,1,0:T(8,128)(2,1)} async-done(((bf16[1,4,96,768]{3,2,1,0:T(8,128)(2,1)}), bf16[8,4,96,768]{3,2,1,0:T(8,128)(2,1)}) %all-gather.3.cloned.1.call-update) | async-done | bytes 4718608 | tf_op jit(solution)/shard_map/all_gather | solution.py:52
  67.7 7.0 %slice_bitcast_fusion.2 = (bf16[8,96,4,192]{3,1,2,0:T(8,128)(2,1)S(1)}, bf16[8,96,4,192]{3,1,2,0:T(8,128)(2,1)}, bf16[8,96,4,192]{3,1,2,0:T(8,128)(2,1)}, bf16[8,96,4,192]{3,1,2,0:T(8,128)(2,1)}) fusion(bf16[8,4,96,768]{3,2,1,0:T(8,128)(2,1)} %all-gather.3.cloned.1.call-done), kind=kLoop, calls=%fused_computation.72 | loop fusion | bytes 9437184 | tf_op jit(solution)/shard_map/transpose | solution.py:58
  77.6 3.0 reshape.236
  87.5 2.9 reshape.238
  95.3 4.4 collective-permute-start.3
  112.5 3.8 reshape.234
  116.3 3.1 add_convert_fusion.3
  130.8 3.8 reshape.241
  140.9 22.3 %shard_map.305 = (bf16[12,512,64]{2,1,0:T(8,128)(2,1)}, f32[12,512,64]{2,1,0:T(8,128)}, f32[12,512,128]{2,1,0:T(8,128)}) custom-call(s32[2]{0:T(128)} %pad_add_fusion.meta_ref, bf16[12,512,64]{2,1,0:T(8,128)(2,1)} %bitcast.173, bf16[12,512,64]{2,1,0:T(8,128)(2,1)} %bitcast.175, bf16[12,512,64]{2,1,0:T(8,128)(2,1)} %bitcast.177, ...), custom_call_target="tpu_custom_call" | custom-call | flops 1610612736 | bytes 9437184 | tf_op jit(solution)/shard_map/pallas_call | solution.py:178
  171.1 6.8 %slice_bitcast_fusion = (bf16[8,96,4,768]{3,1,2,0:T(8,128)(2,1)S(1)}, bf16[8,96,4,768]{3,1,2,0:T(8,128)(2,1)}) fusion(bf16[8,4,96,1536]{3,2,1,0:T(8,128)(2,1)} %all-gather.5.cloned.1.call-done), kind=kLoop, calls=%fused_computation.33 | loop fusion | bytes 18874368 | tf_op jit(solution)/shard_map/transpose | solution.py:58
  177.9 6.0 %copy.139 = bf16[8,96,4,768]{3,2,1,0:T(4,128)(2,1)S(1)} copy(bf16[8,96,4,768]{3,1,2,0:T(8,128)(2,1)} %get-tuple-element.115) | data formatting | bytes 9437184 | tf_op jit(solution)/shard_map/transpose | solution.py:58
  185.0 3.6 copy.140
  189.8 18.6 %multiply_convert_fusion = (bf16[512,3072]{1,0:T(8,128)(2,1)S(1)}, f32[512,3072]{1,0:T(8,128)}, f32[512,3072]{1,0:T(8,128)}) fusion(f32[3072]{0:T(1024)S(1)} %copy-done.36, bf16[768,3072]{1,0:T(8,128)(2,1)S(1)} %bitcast.181, f32[512,768]{1,0:T(8,128)S(1)} %get-tuple-element.150, f32[768]{0:T(1024)S(1)} %copy-done.34, f32[768]{0:T(1024)S(1)} %convert_element_type.121, ...), kind=kOutput, calls=%fused_computation.18 | convolution fusion | flops 2521694208 | bytes 22042624 | tf_op jit(solution)/shard_map/dot_general | solution.py:28
  208.3 9.5 %convert_reduce_fusion = (f32[3072]{0:T(1024)}, bf16[512,3072]{1,0:T(8,128)(2,1)S(1)}) fusion(f32[512,3072]{1,0:T(8,128)} %get-tuple-element.113, bf16[512,768]{1,0:T(8,128)(2,1)S(1)} %copy-done.11, bf16[768,3072]{1,0:T(8,128)(2,1)S(1)} %bitcast.179, f32[512,3072]{1,0:T(8,128)} %get-tuple-element.151, f32[3072]{0:T(1024)S(1)} %copy-done.36), kind=kOutput, calls=%fused_computation.17 | convolution fusion | flops 2442654720 | bytes 21258240 | tf_op jit(solution)/shard_map/dot_general | solution.py:32
  217.8 3.9 fusion.74
  221.7 8.4 %fusion.1 = bf16[2,768,3072]{2,1,0:T(8,128)(2,1)} fusion(bf16[1,512,3072]{2,1,0:T(8,128)(2,1)S(1)} %bitcast.213, bf16[1,512,3072]{2,1,0:T(8,128)(2,1)S(1)} %bitcast.214, bf16[1,512,768]{2,1,0:T(8,128)(2,1)S(1)} %bitcast.193, bf16[1,512,768]{2,1,0:T(8,128)(2,1)S(1)} %copy-done.17), kind=kOutput, calls=%fused_computation.4 | convolution fusion | flops 4835770368 | bytes 17301504 | tf_op jit(solution)/shard_map/dot_general | solution.py:293
  240.1 3.4 slice_reduce_fusion
  249.7 4.0 multiply_reduce_fusion
  257.0 5.0 %collective-permute-done.9 = bf16[12,512,64]{1,2,0:T(8,128)(2,1)} collective-permute-done((bf16[12,512,64]{1,2,0:T(8,128)(2,1)}, bf16[12,512,64]{1,2,0:T(8,128)(2,1)}, u32[]{:S(2)}, u32[]{:S(2)}) %collective-permute-start.9) | collective-permute-done | bytes 786464 | tf_op jit(solution)/shard_map/ppermute | solution.py:311
  273.0 24.7 %shard_map.306 = (bf16[12,512,64]{2,1,0:T(8,128)(2,1)}, bf16[12,512,64]{2,1,0:T(8,128)(2,1)}, bf16[12,512,64]{2,1,0:T(8,128)(2,1)}) custom-call(s32[2]{0:T(128)} %pad_add_fusion.meta_ref, bf16[12,512,64]{2,1,0:T(8,128)(2,1)} %bitcast.174, bf16[12,512,64]{2,1,0:T(8,128)(2,1)} %bitcast.176, bf16[12,512,64]{2,1,0:T(8,128)(2,1)} %bitcast.178, ...), custom_call_target="tpu_custom_call" | custom-call | flops 4026531840 | bytes 21233664 | tf_op jit(solution)/shard_map/pallas_call | solution.py:203
  305.0 4.0 convolution_convert_fusion
  313.1 3.1 convert_reduce_fusion.1
  329.8 24.1 %psum.7 = f32[9216]{0:T(1024)S(1)} all-reduce(f32[9216]{0:T(1024)S(1)} %constant_dynamic-update-slice_fusion), channel_id=1, replica_groups=mesh['dp'=8,'tensor'=4] {'dp'}, use_global_device_ids=true, to_apply=%region_20.21 | all-reduce | flops 9216 | bytes 73728 | tf_op jit(solution)/shard_map/psum | solution.py:354
  353.9 3.3 collective-permute-start.20
  358.3 6.8 %add_convert_fusion = bf16[512,768]{1,0:T(8,128)(2,1)} fusion(f32[512,768]{1,0:T(8,128)S(1)} %get-tuple-element.150, bf16[512,3072]{1,0:T(8,128)(2,1)} %copy-done.48, bf16[768,3072]{1,0:T(8,128)(2,1)} %bitcast.180, f32[768]{0:T(1024)S(1)} %copy-done.41), kind=kOutput, calls=%fused_computation.83 | convolution fusion | flops 2417098752 | bytes 10226688 | tf_op jit(solution)/shard_map/dot_general | solution.py:28
  373.2 72.6 %reduce-scatter.5.cloned.1.call-done = bf16[2,96,3072]{2,1,0:T(8,128)(2,1)} async-done(((bf16[2,768,3072]{2,1,0:T(8,128)(2,1)}), bf16[2,96,3072]{2,1,0:T(8,128)(2,1)}) %reduce-scatter.5.cloned.1.call-update) | async-done | bytes 1179664 | tf_op jit(solution)/shard_map/reduce_scatter | solution.py:67
  448.2 3.4 collective-permute-start.17
  459.0 17.7 %collective-permute-done.16 = bf16[96,1536]{1,0:T(8,128)(2,1)S(1)} collective-permute-done((bf16[96,1536]{1,0:T(8,128)(2,1)S(1)}, bf16[96,1536]{1,0:T(8,128)(2,1)S(1)}, u32[]{:S(2)}, u32[]{:S(2)}) %collective-permute-start.16) | collective-permute-done | bytes 294944 | tf_op jit(solution)/shard_map/ppermute | solution.py:80
  (249 shorter events, 147.6 us)
Async XLA Ops:
  7.2 60.6 %all-gather.3.cloned.1.call-start = ((), (), s32[]{:S(2)}) async-start(), calls=%async_computation.2 | async-start | bytes 5308416 | tf_op jit(solution)/shard_map/all_gather | solution.py:52
  9.1 9.4 %collective-permute-start.2 = (bf16[96,768]{1,0:T(8,128)(2,1)S(1)}, bf16[96,768]{1,0:T(8,128)(2,1)S(1)}, u32[]{:S(2)}, u32[]{:S(2)}) collective-permute-start(bf16[96,768]{1,0:T(8,128)(2,1)S(1)} %pad_maximum_fusion.5), channel_id=1, source_target_pairs={{0,3},{1,0},{2,1},{3,2},{4,7},{5,4},{6,5},{7,6},{8,11},{9,8},{10,9... | collective-permute-start | bytes 442376 | tf_op jit(solution)/shard_map/ppermute | solution.py:47
  14.2 12.5 %collective-permute-start.1 = (bf16[96,768]{1,0:T(8,128)(2,1)S(1)}, bf16[96,768]{1,0:T(8,128)(2,1)S(1)}, u32[]{:S(2)}, u32[]{:S(2)}) collective-permute-start(bf16[96,768]{1,0:T(8,128)(2,1)S(1)} %pad_maximum_fusion.5), channel_id=1, source_target_pairs={{0,2},{1,3},{2,0},{3,1},{4,6},{5,7},{6,4},{7,5},{8,10},{9,11},{10,... | collective-permute-start | bytes 442376 | tf_op jit(solution)/shard_map/ppermute | solution.py:47
  14.2 12.5 %collective-permute-start = (bf16[96,768]{1,0:T(8,128)(2,1)S(1)}, bf16[96,768]{1,0:T(8,128)(2,1)S(1)}, u32[]{:S(2)}, u32[]{:S(2)}) collective-permute-start(bf16[96,768]{1,0:T(8,128)(2,1)S(1)} %pad_maximum_fusion.5), channel_id=1, source_target_pairs={{0,1},{1,2},{2,3},{3,0},{4,5},{5,6},{6,7},{7,4},{8,9},{9,10},{10,1... | collective-permute-start | bytes 442376 | tf_op jit(solution)/shard_map/ppermute | solution.py:47
  28.4 142.8 %all-gather.5.cloned.1.call-start = ((), (), s32[]{:S(2)}) async-start(), calls=%async_computation.3 | async-start | bytes 10616832 | tf_op jit(solution)/shard_map/all_gather | solution.py:52
  28.5 8.9 %collective-permute-start.7 = (bf16[96,1536]{1,0:T(8,128)(2,1)S(1)}, bf16[96,1536]{1,0:T(8,128)(2,1)S(1)}, u32[]{:S(2)}, u32[]{:S(2)}) collective-permute-start(bf16[96,1536]{1,0:T(8,128)(2,1)S(1)} %get-tuple-element.140), channel_id=1, source_target_pairs={{0,3},{1,0},{2,1},{3,2},{4,7},{5,4},{6,5},{7,6},{8,11},{9,8},{10,9... | collective-permute-start | bytes 884744 | tf_op jit(solution)/shard_map/ppermute | solution.py:47
  29.9 26.9 %collective-permute-start.6 = (bf16[96,1536]{1,0:T(8,128)(2,1)S(1)}, bf16[96,1536]{1,0:T(8,128)(2,1)S(1)}, u32[]{:S(2)}, u32[]{:S(2)}) collective-permute-start(bf16[96,1536]{1,0:T(8,128)(2,1)S(1)} %get-tuple-element.140), channel_id=1, source_target_pairs={{0,2},{1,3},{2,0},{3,1},{4,6},{5,7},{6,4},{7,5},{8,10},{9,11},{10,... | collective-permute-start | bytes 884744 | tf_op jit(solution)/shard_map/ppermute | solution.py:47
  31.4 25.3 %collective-permute-start.5 = (bf16[96,1536]{1,0:T(8,128)(2,1)S(1)}, bf16[96,1536]{1,0:T(8,128)(2,1)S(1)}, u32[]{:S(2)}, u32[]{:S(2)}) collective-permute-start(bf16[96,1536]{1,0:T(8,128)(2,1)S(1)} %get-tuple-element.140), channel_id=1, source_target_pairs={{0,1},{1,2},{2,3},{3,0},{4,5},{5,6},{6,7},{7,4},{8,9},{9,10},{10,1... | collective-permute-start | bytes 884744 | tf_op jit(solution)/shard_map/ppermute | solution.py:47
  58.8 307.6 %reduce-scatter.3.cloned.1.call-start = ((), (), s32[]{:S(2)}) async-start(), calls=%async_computation.4 | async-start | bytes 5308416 | tf_op jit(solution)/shard_map/reduce_scatter | solution.py:67
  60.7 14.1 %copy-start.27 = (f32[512]{0:T(512)}, f32[512]{0:T(512)S(1)}, u32[]{:S(2)}) copy-start(f32[512]{0:T(512)S(1)} %fusion.31) | copy-start | bytes 6148
  60.7 55.6 %copy-start.24 = (f32[512]{0:T(512)}, f32[512]{0:T(512)S(1)}, u32[]{:S(2)}) copy-start(f32[512]{0:T(512)S(1)} %fusion.51) | copy-start | bytes 6148
  95.3 40.7 %collective-permute-start.3 = (bf16[12,512,64]{1,2,0:T(8,128)(2,1)}, bf16[12,512,64]{1,2,0:T(8,128)(2,1)}, u32[]{:S(2)}, u32[]{:S(2)}) collective-permute-start(bf16[12,512,64]{1,2,0:T(8,128)(2,1)} %bitcast.183), channel_id=1, source_target_pairs={{0,1},{2,3},{4,5},{6,7},{8,9},{10,11},{12,13},{14,15},{16,17},{18,... | collective-permute-start | bytes 2359304 | tf_op jit(solution)/shard_map/ppermute | solution.py:279
  99.7 38.7 %collective-permute-start.4 = (bf16[12,512,64]{1,2,0:T(8,128)(2,1)}, bf16[12,512,64]{1,2,0:T(8,128)(2,1)}, u32[]{:S(2)}, u32[]{:S(2)}) collective-permute-start(bf16[12,512,64]{1,2,0:T(8,128)(2,1)} %bitcast.185), channel_id=1, source_target_pairs={{0,1},{2,3},{4,5},{6,7},{8,9},{10,11},{12,13},{14,15},{16,17},{18,... | collective-permute-start | bytes 2359304 | tf_op jit(solution)/shard_map/ppermute | solution.py:279
  134.7 110.1 %collective-permute-start.8 = (bf16[12,512,64]{1,2,0:T(8,128)(2,1)}, bf16[12,512,64]{1,2,0:T(8,128)(2,1)}, u32[]{:S(2)}, u32[]{:S(2)}) collective-permute-start(bf16[12,512,64]{1,2,0:T(8,128)(2,1)} %bitcast.70), channel_id=1, source_target_pairs={{1,0},{3,2},{5,4},{7,6},{9,8},{11,10},{13,12},{15,14},{17,16},{19,... | collective-permute-start | bytes 2359304 | tf_op jit(solution)/shard_map/ppermute | solution.py:282
  189.7 18.6 %copy-start.5 = (bf16[96,8,4,768]{3,1,2,0:T(8,128)(2,1)}, bf16[96,8,4,768]{3,1,2,0:T(8,128)(2,1)S(1)}, u32[]{:S(2)}) copy-start(bf16[96,8,4,768]{3,1,2,0:T(8,128)(2,1)S(1)} %copy.178) | copy-start | bytes 14155780
  189.8 18.6 %copy-start.11 = (bf16[512,768]{1,0:T(8,128)(2,1)S(1)}, bf16[512,768]{1,0:T(8,128)(2,1)}, u32[]{:S(2)}) copy-start(bf16[512,768]{1,0:T(8,128)(2,1)} %param.20) | copy-start | bytes 2359300
  208.3 13.3 %copy-start.48 = (bf16[512,3072]{1,0:T(8,128)(2,1)}, bf16[512,3072]{1,0:T(8,128)(2,1)S(1)}, u32[]{:S(2)}) copy-start(bf16[512,3072]{1,0:T(8,128)(2,1)S(1)} %get-tuple-element.112) | copy-start | bytes 9437188
  233.6 21.4 %copy-start.37 = (f32[512]{0:T(512)}, f32[512]{0:T(512)S(1)}, u32[]{:S(2)}) copy-start(f32[512]{0:T(512)S(1)} %negate_multiply_fusion.2) | copy-start | bytes 6148
  238.8 23.2 %collective-permute-start.9 = (bf16[12,512,64]{1,2,0:T(8,128)(2,1)}, bf16[12,512,64]{1,2,0:T(8,128)(2,1)}, u32[]{:S(2)}, u32[]{:S(2)}) collective-permute-start(bf16[12,512,64]{1,2,0:T(8,128)(2,1)} %bitcast.187), channel_id=1, source_target_pairs={{1,0},{3,2},{5,4},{7,6},{9,8},{11,10},{13,12},{15,14},{17,16},{19,... | collective-permute-start | bytes 2359304 | tf_op jit(solution)/shard_map/ppermute | solution.py:311
  243.5 20.9 %collective-permute-start.10 = (f32[12,512]{1,0:T(8,128)}, f32[12,512]{1,0:T(8,128)}, u32[]{:S(2)}, u32[]{:S(2)}) collective-permute-start(f32[12,512]{1,0:T(8,128)} %slice_reduce_fusion), channel_id=1, source_target_pairs={{1,0},{3,2},{5,4},{7,6},{9,8},{11,10},{13,12},{15,14},{17,16},{19,... | collective-permute-start | bytes 73736 | tf_op jit(solution)/shard_map/ppermute | solution.py:282
  253.7 10.7 %collective-permute-start.11 = (f32[12,512]{1,0:T(8,128)}, f32[12,512]{1,0:T(8,128)}, u32[]{:S(2)}, u32[]{:S(2)}) collective-permute-start(f32[12,512]{1,0:T(8,128)} %multiply_reduce_fusion), channel_id=1, source_target_pairs={{1,0},{3,2},{5,4},{7,6},{9,8},{11,10},{13,12},{15,14},{17,16},{19,... | collective-permute-start | bytes 73736 | tf_op jit(solution)/shard_map/ppermute | solution.py:311
  311.9 133.9 %reduce-scatter.5.cloned.1.call-start = ((), (), s32[]{:S(2)}) async-start(), calls=%async_computation.5 | async-start | bytes 10616832 | tf_op jit(solution)/shard_map/reduce_scatter | solution.py:67
  327.7 30.6 %copy-start.41 = (f32[768]{0:T(1024)S(1)}, f32[768]{0:T(1024)}, u32[]{:S(2)}) copy-start(f32[768]{0:T(1024)} %convert_element_type.126) | copy-start | bytes 9220
  353.9 11.3 %collective-permute-start.20 = (f32[9216]{0:T(1024)S(1)}, f32[9216]{0:T(1024)S(1)}, u32[]{:S(2)}, u32[]{:S(2)}) collective-permute-start(f32[9216]{0:T(1024)S(1)} %psum.7), channel_id=1, source_target_pairs={{0,3},{1,0},{2,1},{3,2},{4,7},{5,4},{6,5},{7,6},{8,11},{9,8},{10,9... | collective-permute-start | bytes 110600 | tf_op jit(solution)/shard_map/ppermute | solution.py:357
  357.2 8.0 %collective-permute-start.19 = (f32[9216]{0:T(1024)S(1)}, f32[9216]{0:T(1024)S(1)}, u32[]{:S(2)}, u32[]{:S(2)}) collective-permute-start(f32[9216]{0:T(1024)S(1)} %psum.7), channel_id=1, source_target_pairs={{0,2},{1,3},{2,0},{3,1},{4,6},{5,7},{6,4},{7,5},{8,10},{9,11},{10,... | collective-permute-start | bytes 110600 | tf_op jit(solution)/shard_map/ppermute | solution.py:357
  357.2 8.0 %collective-permute-start.18 = (f32[9216]{0:T(1024)S(1)}, f32[9216]{0:T(1024)S(1)}, u32[]{:S(2)}, u32[]{:S(2)}) collective-permute-start(f32[9216]{0:T(1024)S(1)} %psum.7), channel_id=1, source_target_pairs={{0,1},{1,2},{2,3},{3,0},{4,5},{5,6},{6,7},{7,4},{8,9},{9,10},{10,1... | collective-permute-start | bytes 110600 | tf_op jit(solution)/shard_map/ppermute | solution.py:357
  369.3 82.3 %collective-permute-start.14 = (bf16[96,768]{0,1:T(8,128)(2,1)}, bf16[96,768]{0,1:T(8,128)(2,1)}, u32[]{:S(2)}, u32[]{:S(2)}) collective-permute-start(bf16[96,768]{0,1:T(8,128)(2,1)} %get-tuple-element.127), channel_id=1, source_target_pairs={{0,3},{1,0},{2,1},{3,2},{4,7},{5,4},{6,5},{7,6},{8,11},{9,8},{10,9... | collective-permute-start | bytes 442376 | tf_op jit(solution)/shard_map/ppermute | solution.py:80
  372.0 80.7 %collective-permute-start.13 = (bf16[96,768]{0,1:T(8,128)(2,1)}, bf16[96,768]{0,1:T(8,128)(2,1)}, u32[]{:S(2)}, u32[]{:S(2)}) collective-permute-start(bf16[96,768]{0,1:T(8,128)(2,1)} %get-tuple-element.128), channel_id=1, source_target_pairs={{0,2},{1,3},{2,0},{3,1},{4,6},{5,7},{6,4},{7,5},{8,10},{9,11},{10,... | collective-permute-start | bytes 442376 | tf_op jit(solution)/shard_map/ppermute | solution.py:80
  373.2 79.5 %collective-permute-start.12 = (bf16[96,768]{0,1:T(8,128)(2,1)}, bf16[96,768]{0,1:T(8,128)(2,1)}, u32[]{:S(2)}, u32[]{:S(2)}) collective-permute-start(bf16[96,768]{0,1:T(8,128)(2,1)} %get-tuple-element.126), channel_id=1, source_target_pairs={{0,1},{1,2},{2,3},{3,0},{4,5},{5,6},{6,7},{7,4},{8,9},{9,10},{10,1... | collective-permute-start | bytes 442376 | tf_op jit(solution)/shard_map/ppermute | solution.py:80
  448.2 10.8 %collective-permute-start.17 = (bf16[96,1536]{1,0:T(8,128)(2,1)S(1)}, bf16[96,1536]{1,0:T(8,128)(2,1)S(1)}, u32[]{:S(2)}, u32[]{:S(2)}) collective-permute-start(bf16[96,1536]{1,0:T(8,128)(2,1)S(1)} %get-tuple-element.123), channel_id=1, source_target_pairs={{0,3},{1,0},{2,1},{3,2},{4,7},{5,4},{6,5},{7,6},{8,11},{9,8},{10,9... | collective-permute-start | bytes 884744 | tf_op jit(solution)/shard_map/ppermute | solution.py:80
  451.6 25.1 %collective-permute-start.16 = (bf16[96,1536]{1,0:T(8,128)(2,1)S(1)}, bf16[96,1536]{1,0:T(8,128)(2,1)S(1)}, u32[]{:S(2)}, u32[]{:S(2)}) collective-permute-start(bf16[96,1536]{1,0:T(8,128)(2,1)S(1)} %get-tuple-element.122), channel_id=1, source_target_pairs={{0,2},{1,3},{2,0},{3,1},{4,6},{5,7},{6,4},{7,5},{8,10},{9,11},{10,... | collective-permute-start | bytes 884744 | tf_op jit(solution)/shard_map/ppermute | solution.py:80
  451.6 25.1 %collective-permute-start.15 = (bf16[96,1536]{1,0:T(8,128)(2,1)S(1)}, bf16[96,1536]{1,0:T(8,128)(2,1)}, u32[]{:S(2)}, u32[]{:S(2)}) collective-permute-start(bf16[96,1536]{1,0:T(8,128)(2,1)S(1)} %get-tuple-element.121), channel_id=1, source_target_pairs={{0,1},{1,2},{2,3},{3,0},{4,5},{5,6},{6,7},{7,4},{8,9},{9,10},{10,1... | collective-permute-start | bytes 884744 | tf_op jit(solution)/shard_map/ppermute | solution.py:80
  (42 other events, 98.5 us)
Sparse Core Ops, SparseCore 0:
  28.5 39.2 all-gather.2
  69.6 58.6 all-gather.4
  312.0 53.7 reduce-scatter.2
  369.1 76.6 reduce-scatter.4

commit v6 on v5

--- a/solution.py
+++ b/solution.py
@@ -94,29 +94,39 @@
 def attn_fwd_kernel(meta_ref, q_ref, k_ref, v_ref, ko_ref, vo_ref, o_ref, of_ref, lse_ref):
     half = meta_ref[0]
     prefix_len = meta_ref[1]
-    rows = q_ref.shape[1]
+    rows = q_ref.shape[0]
     scale = HEAD ** (-0.5)
-    q = q_ref[0]
-    s = lax.dot_general(q, k_ref[0], NT, preferred_element_type=jnp.float32) * scale
-    row = lax.broadcasted_iota(jnp.int32, s.shape, 0)
-    col = lax.broadcasted_iota(jnp.int32, s.shape, 1)
-    visible = (col <= row) | (half * rows + col < prefix_len)
-    s = jnp.where(visible, s, masked_score)
-    so = lax.dot_general(q, ko_ref[0], NT, preferred_element_type=jnp.float32) * scale
-    so = jnp.where(half == 1, so, masked_score)
-    top = jnp.maximum(jnp.max(s, axis=1, keepdims=True), jnp.max(so, axis=1, keepdims=True))
-    e = jnp.exp(s - top)
-    eo = jnp.exp(so - top)
-    total = jnp.sum(e, axis=1, keepdims=True) + jnp.sum(eo, axis=1, keepdims=True)
-    inv = 1.0 / total
-    p = (e * inv).astype(jnp.bfloat16)
-    po = (eo * inv).astype(jnp.bfloat16)
-    o = jnp.dot(p, v_ref[0], preferred_element_type=jnp.float32) + jnp.dot(
-        po, vo_ref[0], preferred_element_type=jnp.float32
-    )
-    o_ref[0] = o.astype(o_ref.dtype)
-    of_ref[0] = o
-    lse_ref[0] = jnp.broadcast_to(top + jnp.log(total), (rows, LANES))
+    q_all = q_ref[...]
+    k_all = k_ref[...]
+    v_all = v_ref[...]
+    ko_all = ko_ref[...]
+    vo_all = vo_ref[...]
+    outs = []
+    for j in range(q_all.shape[1] // HEAD):
+        cols = slice(j * HEAD, (j + 1) * HEAD)
+        q = q_all[:, cols]
+        s = lax.dot_general(q, k_all[:, cols], NT, preferred_element_type=jnp.float32) * scale
+        row = lax.broadcasted_iota(jnp.int32, s.shape, 0)
+        col = lax.broadcasted_iota(jnp.int32, s.shape, 1)
+        visible = (col <= row) | (half * rows + col < prefix_len)
+        s = jnp.where(visible, s, masked_score)
+        so = lax.dot_general(q, ko_all[:, cols], NT, preferred_element_type=jnp.float32) * scale
+        so = jnp.where(half == 1, so, masked_score)
+        top = jnp.maximum(jnp.max(s, axis=1, keepdims=True), jnp.max(so, axis=1, keepdims=True))
+        e = jnp.exp(s - top)
+        eo = jnp.exp(so - top)
+        total = jnp.sum(e, axis=1, keepdims=True) + jnp.sum(eo, axis=1, keepdims=True)
+        inv = 1.0 / total
+        p = (e * inv).astype(jnp.bfloat16)
+        po = (eo * inv).astype(jnp.bfloat16)
+        o = jnp.dot(p, v_all[:, cols], preferred_element_type=jnp.float32) + jnp.dot(
+            po, vo_all[:, cols], preferred_element_type=jnp.float32
+        )
+        outs.append(o)
+        lse_ref[j] = jnp.broadcast_to(top + jnp.log(total), (rows, LANES))
+    o = jnp.concatenate(outs, axis=1)
+    o_ref[...] = o.astype(o_ref.dtype)
+    of_ref[...] = o
 
 
 def attn_bwd_kernel(
@@ -127,54 +137,74 @@
     bf16 = jnp.bfloat16
     half = meta_ref[0]
     prefix_len = meta_ref[1]
-    rows = q_ref.shape[1]
+    rows = q_ref.shape[0]
     reps = rows // LANES
     scale = HEAD ** (-0.5)
-    q = q_ref[0]
-    k = k_ref[0]
-    v = v_ref[0]
-    do = do_ref[0]
-    s = lax.dot_general(q, k, NT, preferred_element_type=f32) * scale
-    row = lax.broadcasted_iota(jnp.int32, s.shape, 0)
-    col = lax.broadcasted_iota(jnp.int32, s.shape, 1)
-    visible = (col <= row) | (half * rows + col < prefix_len)
-    s = jnp.where(visible, s, masked_score)
-    p = jnp.exp(s - jnp.tile(lse_ref[0], (1, reps)))
-    dp = lax.dot_general(do, v, NT, preferred_element_type=f32)
-    ds = (p * (dp - jnp.tile(dl_ref[0], (1, reps)))).astype(bf16)
-    dq = jnp.dot(ds, k, preferred_element_type=f32)
-    dk = jnp.dot(ds.T, q, preferred_element_type=f32)
-    dv = jnp.dot(p.astype(bf16).T, do, preferred_element_type=f32)
     second = half == 1
-    xq = jnp.where(second, q, qr_ref[0])
-    xdo = jnp.where(second, do, dor_ref[0])
-    xlse = jnp.tile(jnp.where(second, lse_ref[0], lser_ref[0]), (1, reps))
-    xdl = jnp.tile(jnp.where(second, dl_ref[0], dlr_ref[0]), (1, reps))
-    xk = jnp.where(second, ko_ref[0], k)
-    xv = jnp.where(second, vo_ref[0], v)
-    s2 = lax.dot_general(xq, xk, NT, preferred_element_type=f32) * scale
-    p2 = jnp.exp(s2 - xlse)
-    dp2 = lax.dot_general(xdo, xv, NT, preferred_element_type=f32)
-    ds2 = (p2 * (dp2 - xdl)).astype(bf16)
-    dq_x = jnp.dot(ds2, xk, preferred_element_type=f32)
-    dk_x = jnp.dot(ds2.T, xq, preferred_element_type=f32)
-    dv_x = jnp.dot(p2.astype(bf16).T, xdo, preferred_element_type=f32)
-    dq = dq + jnp.where(second, dq_x, 0.0)
-    dk = dk + jnp.where(second, 0.0, dk_x)
-    dv = dv + jnp.where(second, 0.0, dv_x)
-    dq_ref[0] = (dq * scale).astype(dq_ref.dtype)
-    dk_ref[0] = (dk * scale).astype(dk_ref.dtype)
-    dv_ref[0] = dv.astype(dv_ref.dtype)
-
-
-def head_spec(shape):
-    return pl.BlockSpec((1,) + tuple(shape[1:]), lambda h, meta: (h, 0, 0))
+    q_all = q_ref[...]
+    k_all = k_ref[...]
+    v_all = v_ref[...]
+    do_all = do_ref[...]
+    xq_all = jnp.where(second, q_all, qr_ref[...])
+    xdo_all = jnp.where(second, do_all, dor_ref[...])
+    xk_all = jnp.where(second, ko_ref[...], k_all)
+    xv_all = jnp.where(second, vo_ref[...], v_all)
+    dqs, dks, dvs = [], [], []
+    for j in range(q_all.shape[1] // HEAD):
+        cols = slice(j * HEAD, (j + 1) * HEAD)
+        q = q_all[:, cols]
+        k = k_all[:, cols]
+        v = v_all[:, cols]
+        do = do_all[:, cols]
+        lse = lse_ref[j]
+        dl = dl_ref[j]
+        s = lax.dot_general(q, k, NT, preferred_element_type=f32) * scale
+        row = lax.broadcasted_iota(jnp.int32, s.shape, 0)
+        col = lax.broadcasted_iota(jnp.int32, s.shape, 1)
+        visible = (col <= row) | (half * rows + col < prefix_len)
+        s = jnp.where(visible, s, masked_score)
+        p = jnp.exp(s - jnp.tile(lse, (1, reps)))
+        dp = lax.dot_general(do, v, NT, preferred_element_type=f32)
+        ds = (p * (dp - jnp.tile(dl, (1, reps)))).astype(bf16)
+        dq = jnp.dot(ds, k, preferred_element_type=f32)
+        dk = jnp.dot(ds.T, q, preferred_element_type=f32)
+        dv = jnp.dot(p.astype(bf16).T, do, preferred_element_type=f32)
+        xq = xq_all[:, cols]
+        xdo = xdo_all[:, cols]
+        xk = xk_all[:, cols]
+        xv = xv_all[:, cols]
+        xlse = jnp.tile(jnp.where(second, lse, lser_ref[j]), (1, reps))
+        xdl = jnp.tile(jnp.where(second, dl, dlr_ref[j]), (1, reps))
+        s2 = lax.dot_general(xq, xk, NT, preferred_element_type=f32) * scale
+        p2 = jnp.exp(s2 - xlse)
+        dp2 = lax.dot_general(xdo, xv, NT, preferred_element_type=f32)
+        ds2 = (p2 * (dp2 - xdl)).astype(bf16)
+        dq_x = jnp.dot(ds2, xk, preferred_element_type=f32)
+        dk_x = jnp.dot(ds2.T, xq, preferred_element_type=f32)
+        dv_x = jnp.dot(p2.astype(bf16).T, xdo, preferred_element_type=f32)
+        dqs.append((dq + jnp.where(second, dq_x, 0.0)) * scale)
+        dks.append((dk + jnp.where(second, 0.0, dk_x)) * scale)
+        dvs.append(dv + jnp.where(second, 0.0, dv_x))
+    dq_ref[...] = jnp.concatenate(dqs, axis=1).astype(dq_ref.dtype)
+    dk_ref[...] = jnp.concatenate(dks, axis=1).astype(dk_ref.dtype)
+    dv_ref[...] = jnp.concatenate(dvs, axis=1).astype(dv_ref.dtype)
+
+
+PAIR = 2 * HEAD
+
+
+def row_spec(rows):
+    return pl.BlockSpec((rows, PAIR), lambda g, meta: (0, g))
+
+
+def wide_spec(rows):
+    return pl.BlockSpec((2, rows, LANES), lambda g, meta: (g, 0, 0))
 
 
 def attention_forward(meta, q, k, v, ko, vo):
-    heads, rows, size = q.shape
-    spec = head_spec(q.shape)
-    lse_spec = head_spec((heads, rows, LANES))
+    rows, width = q.shape
+    heads = width // HEAD
+    spec = row_spec(rows)
     return pl.pallas_call(
         attn_fwd_kernel,
         out_shape=(
@@ -184,12 +214,12 @@
         ),
         grid_spec=pltpu.PrefetchScalarGridSpec(
             num_scalar_prefetch=1,
-            grid=(heads,),
+            grid=(width // PAIR,),
             in_specs=[spec] * 5,
-            out_specs=(spec, spec, lse_spec),
+            out_specs=(spec, spec, wide_spec(rows)),
         ),
         cost_estimate=pl.CostEstimate(
-            flops=8 * heads * rows * rows * size,
+            flops=8 * heads * rows * rows * HEAD,
             transcendentals=2 * heads * rows * rows,
             bytes_accessed=5 * q.size * 2 + q.size * 6 + heads * rows * LANES * 4,
         ),
@@ -197,20 +227,21 @@
 
 
 def attention_backward(meta, q, k, v, do, lse, dl, ko, vo, qr, dor, lser, dlr):
-    heads, rows, size = q.shape
-    spec = head_spec(q.shape)
-    lse_spec = head_spec(lse.shape)
+    rows, width = q.shape
+    heads = width // HEAD
+    spec = row_spec(rows)
+    wspec = wide_spec(rows)
     return pl.pallas_call(
         attn_bwd_kernel,
         out_shape=tuple(jax.ShapeDtypeStruct(q.shape, jnp.bfloat16) for _ in range(3)),
         grid_spec=pltpu.PrefetchScalarGridSpec(
             num_scalar_prefetch=1,
-            grid=(heads,),
-            in_specs=[spec, spec, spec, spec, lse_spec, lse_spec, spec, spec, spec, spec, lse_spec, lse_spec],
+            grid=(width // PAIR,),
+            in_specs=[spec, spec, spec, spec, wspec, wspec, spec, spec, spec, spec, wspec, wspec],
             out_specs=(spec, spec, spec),
         ),
         cost_estimate=pl.CostEstimate(
-            flops=20 * heads * rows * rows * size,
+            flops=20 * heads * rows * rows * HEAD,
             transcendentals=2 * heads * rows * rows,
             bytes_accessed=11 * q.size * 2 + 4 * lse.size * 4,
         ),
@@ -268,18 +299,10 @@
     key_rows = dot_right(normed_one, full_key).astype(bf16)
     value_rows = (dot_right(normed_one, full_value) + b_value.astype(f32)).astype(bf16)
     queries = (dot_right(normed_one, full_query) + b_query.astype(f32)).astype(bf16)
-
-    def by_heads(x):
-        return x.reshape(rows, heads, HEAD).transpose(1, 0, 2)
-
     meta = jnp.stack([half, prefix_len]).astype(jnp.int32)
-    q3 = by_heads(queries)
-    k3 = by_heads(key_rows)
-    v3 = by_heads(value_rows)
-    k_oth, v_oth = lax.ppermute((k3, v3), "tensor", to_second)
-    o_heads, o_full, lse_wide = attention_forward(meta, q3, k3, v3, k_oth, v_oth)
-    attended = o_heads.transpose(1, 0, 2).reshape(rows, width)
-    q_rcv, lse_rcv = lax.ppermute((q3, lse_wide[:, :, 0]), "tensor", to_first)
+    k_oth, v_oth = lax.ppermute((key_rows, value_rows), "tensor", to_second)
+    attended, o_full, lse_wide = attention_forward(meta, queries, key_rows, value_rows, k_oth, v_oth)
+    q_rcv, lse_rcv = lax.ppermute((queries, lse_wide[:, :, 0]), "tensor", to_first)
 
     middle = in_rows + dot_right(attended, full_out) + b_out.astype(f32)
     normed_two = layer_norm(middle, gain_second, shift_second).astype(bf16)
@@ -306,23 +329,16 @@
     grad_attn_rows = grad_middle.astype(bf16)
     grad_attended = dot_back(grad_attn_rows, full_out).astype(bf16)
 
-    do3 = by_heads(grad_attended)
-    delta = jnp.sum(do3.astype(f32) * o_full, axis=-1)
-    do_rcv, delta_rcv = lax.ppermute((do3, delta), "tensor", to_first)
+    delta = jnp.sum((grad_attended.astype(f32) * o_full).reshape(rows, heads, HEAD), axis=-1).T
+    do_rcv, delta_rcv = lax.ppermute((grad_attended, delta), "tensor", to_first)
 
     def wide(x):
         return jnp.broadcast_to(x[:, :, None], x.shape + (LANES,))
 
-    dq3, dk3, dv3 = attention_backward(
-        meta, q3, k3, v3, do3, lse_wide, wide(delta), k_oth, v_oth, q_rcv, do_rcv, wide(lse_rcv), wide(delta_rcv)
-    )
-
-    def by_rows(x):
-        return x.transpose(1, 0, 2).reshape(rows, width)
-
-    grad_q = by_rows(dq3)
-    grad_k = by_rows(dk3)
-    grad_v = by_rows(dv3)
+    grad_q, grad_k, grad_v = attention_backward(
+        meta, queries, key_rows, value_rows, grad_attended, lse_wide, wide(delta), k_oth, v_oth,
+        q_rcv, do_rcv, wide(lse_rcv), wide(delta_rcv),
+    )
     grad_qkv = jnp.concatenate([grad_q, grad_k, grad_v], axis=1)
     attn_grad = jnp.concatenate(
         [dot_over_rows(normed_one, grad_qkv), dot_over_rows(grad_attn_rows, attended)], axis=1

time: 494 us -> 460 us (0.931)
  local copies, waits for them, and re-layouts: 122 us -> 90.3 us
    transpose x4 -> x0, local copies, waits for them, and re-layouts: 10.1 us -> none  [the longest x3 7.26 us: by_rows(): return x.transpose(1, 0, 2).reshape(rows, width)]
    reshape x4 -> x0, local copies, waits for them, and re-layouts: 9.8 us -> none  [by_heads(): return x.reshape(rows, heads, HEAD).transpose(1, 0, 2)]
    ppermute x4 -> x0, local copies, waits for them, and re-layouts: 9.78 us -> none  [the longest x2 4.92 us: layer(): k_oth, v_oth = lax.ppermute((k3, v3), 'tensor', to_second)]
    convert_element_type x4 -> x0, local copies, waits for them, and re-layouts: 9.24 us -> none  [the longest x1 2.33 us: layer(): (dot_right(normed_one, full_value) + b_value.astype(f32)).astype(bf16)]
    unnamed x112 -> x114, local copies, waits for them, and re-layouts: 11.5 us -> 19.2 us
    ppermute x6, waiting for transfers between devices: 4.96 us -> 10.8 us  [the longest x2 5.4 us: layer(): k_oth, v_oth = lax.ppermute((key_rows, value_rows), 'tensor', to_second)]
  transfers between devices with their start and end apart: 25 -> 25, of which waited for: 9 -> 11; matrix products, arithmetic and copies ran while one was open for 40% -> 38% of each run, Pallas kernels for 5% -> 4%
where the time goes in v6:
time: 460 us; the launch traced here: 452 us
  waiting for transfers between devices  140 us (30%)
  local copies, waits for them, and re-layouts  90.3 us (20%)
  matrix products  69.5 us (15%)
  Pallas kernels  43 us (9%)
  starting transfers between devices  35 us (8%)
  other arithmetic  33.9 us (7%)
  blocking collectives  24.7 us (5%)
  between operations  15 us (3%)
    reduce_scatter x2, waiting for transfers between devices, scatter_rows(): lax.psum_scatter(grad.astype(LINK), 'dp', scatter_dimension=axis, tiled=T...  68.3 us
    dot_general x6, matrix products, dot_right(): return jnp.dot(first_op, second_op, preferred_element_type=jnp.float32)  34.4 us
    ppermute x6, waiting for transfers between devices, gather_joined(): lax.ppermute(joined, 'tensor', [(i, (i + step) % tp) for i in range(tp)])  33.9 us
    transpose x8, local copies, waits for them, and re-layouts, gather_joined(): out.append(block.transpose(0, 2, 1, 3).reshape(dp * r, tp * c))  33.6 us
    psum x1, blocking collectives, layer(): joined = lax.psum(jnp.concatenate(vectors), 'dp')  24.7 us
    pallas_call x1, Pallas kernels, attention_backward(): pl.pallas_call(attn_bwd_kernel, out_shape=tuple((jax.ShapeDtypeStruct(q.s...  24.1 us
    ppermute x6, waiting for transfers between devices, sum_over_tensor(): lax.ppermute(sent, 'tensor', [(i, (i + step) % tp) for i in range(tp)])  20.1 us
    unnamed x114, local copies, waits for them, and re-layouts  19.2 us
  transfers between devices with their start and end apart: 25, of which 11 were waited for; matrix products, arithmetic and copies ran while one was open for 38% of the time, Pallas kernels for 4%

profile of v6, /device:TPU:0, one launch (start us, length us, event | category | flops | bytes accessed | tf_op | source)
XLA Modules:
  0.0 451.8 jit_solution(3842668504511193851)
XLA Ops:
  9.1 5.1 %collective-permute-start.2 = (bf16[96,768]{1,0:T(8,128)(2,1)S(1)}, bf16[96,768]{1,0:T(8,128)(2,1)S(1)}, u32[]{:S(2)}, u32[]{:S(2)}) collective-permute-start(bf16[96,768]{1,0:T(8,128)(2,1)S(1)} %pad_maximum_fusion.5), channel_id=1, source_target_pairs={{0,3},{1,0},{2,1},{3,2},{4,7},{5,4},{6,5},{7,6},{8,11},{9,8},{10,9... | collective-permute-start | bytes 442376 | tf_op jit(solution)/shard_map/ppermute | solution.py:47
  18.5 8.2 %collective-permute-done.1 = bf16[96,768]{1,0:T(8,128)(2,1)S(1)} collective-permute-done((bf16[96,768]{1,0:T(8,128)(2,1)S(1)}, bf16[96,768]{1,0:T(8,128)(2,1)S(1)}, u32[]{:S(2)}, u32[]{:S(2)}) %collective-permute-start.1) | collective-permute-done | bytes 147488 | tf_op jit(solution)/shard_map/ppermute | solution.py:47
  33.4 4.0 collective-permute-done.7
  37.4 19.4 %collective-permute-done.6 = bf16[96,1536]{1,0:T(8,128)(2,1)S(1)} collective-permute-done((bf16[96,1536]{1,0:T(8,128)(2,1)S(1)}, bf16[96,1536]{1,0:T(8,128)(2,1)S(1)}, u32[]{:S(2)}, u32[]{:S(2)}) %collective-permute-start.6) | collective-permute-done | bytes 294944 | tf_op jit(solution)/shard_map/ppermute | solution.py:47
  60.7 7.1 %all-gather.3.cloned.1.call-done = bf16[8,4,96,768]{3,2,1,0:T(8,128)(2,1)} async-done(((bf16[1,4,96,768]{3,2,1,0:T(8,128)(2,1)}), bf16[8,4,96,768]{3,2,1,0:T(8,128)(2,1)}) %all-gather.3.cloned.1.call-update) | async-done | bytes 4718608 | tf_op jit(solution)/shard_map/all_gather | solution.py:52
  67.7 7.0 %slice_bitcast_fusion.2 = (bf16[8,96,4,192]{3,1,2,0:T(8,128)(2,1)S(1)}, bf16[8,96,4,192]{3,1,2,0:T(8,128)(2,1)}, bf16[8,96,4,192]{3,1,2,0:T(8,128)(2,1)}, bf16[8,96,4,192]{3,1,2,0:T(8,128)(2,1)}) fusion(bf16[8,4,96,768]{3,2,1,0:T(8,128)(2,1)} %all-gather.3.cloned.1.call-done), kind=kLoop, calls=%fused_computation.69 | loop fusion | bytes 9437184 | tf_op jit(solution)/shard_map/transpose | solution.py:58
  77.6 3.9 reshape.212
  84.3 2.9 reshape.213
  87.3 3.1 convolution_convert_fusion.3.k_ref
  90.3 4.3 collective-permute-start.3
  110.0 3.8 reshape.211
  115.6 3.9 reshape.214
  122.7 5.4 %collective-permute-done.4.vo_ref = bf16[512,768]{1,0:T(8,128)(2,1)} collective-permute-done((bf16[512,768]{1,0:T(8,128)(2,1)}, bf16[512,768]{1,0:T(8,128)(2,1)}, u32[]{:S(2)}, u32[]{:S(2)}) %collective-permute-start.4) | collective-permute-done | bytes 786464 | tf_op jit(solution)/shard_map/ppermute | solution.py:303
  128.1 18.8 %shard_map.305 = (bf16[512,768]{1,0:T(8,128)(2,1)}, f32[512,768]{1,0:T(8,128)}, f32[12,512,128]{2,1,0:T(8,128)}) custom-call(s32[2]{0:T(128)} %pad_add_fusion.meta_ref, bf16[512,768]{1,0:T(8,128)(2,1)} %add_convert_fusion.3.q_ref, bf16[512,768]{1,0:T(8,128)(2,1)} %convolution_convert_fusion.3.k_ref, bf16[512,768]{1,0:T(8,128)(2,1)} %add_convert_fusion.2.v_ref, ...), custom_call_target="tpu_custom_call" | custom-call | flops 1610612736 | bytes 9437184 | tf_op jit(solution)/shard_map/pallas_call | solution.py:208
  152.1 6.7 %slice_bitcast_fusion = (bf16[8,96,4,768]{3,1,2,0:T(8,128)(2,1)S(1)}, bf16[8,96,4,768]{3,1,2,0:T(8,128)(2,1)}) fusion(bf16[8,4,96,1536]{3,2,1,0:T(8,128)(2,1)} %all-gather.5.cloned.1.call-done), kind=kLoop, calls=%fused_computation.33 | loop fusion | bytes 18874368 | tf_op jit(solution)/shard_map/transpose | solution.py:58
  158.8 6.0 %copy.96 = bf16[8,96,4,768]{3,2,1,0:T(4,128)(2,1)S(1)} copy(bf16[8,96,4,768]{3,1,2,0:T(8,128)(2,1)} %get-tuple-element.116) | data formatting | bytes 9437184 | tf_op jit(solution)/shard_map/transpose | solution.py:58
  165.8 3.6 copy.97
  170.6 18.4 %multiply_convert_fusion = (bf16[512,3072]{1,0:T(8,128)(2,1)S(1)}, f32[512,3072]{1,0:T(8,128)}, f32[512,3072]{1,0:T(8,128)}) fusion(f32[3072]{0:T(1024)S(1)} %copy-done.34, bf16[768,3072]{1,0:T(8,128)(2,1)S(1)} %bitcast.144, f32[512,768]{1,0:T(8,128)S(1)} %get-tuple-element.151, f32[768]{0:T(1024)S(1)} %copy-done.32, f32[768]{0:T(1024)S(1)} %convert_element_type.119, ...), kind=kOutput, calls=%fused_computation.18 | convolution fusion | flops 2521694208 | bytes 22042624 | tf_op jit(solution)/shard_map/dot_general | solution.py:28
  189.0 9.5 %convert_reduce_fusion = (f32[3072]{0:T(1024)}, bf16[512,3072]{1,0:T(8,128)(2,1)S(1)}) fusion(f32[512,3072]{1,0:T(8,128)} %get-tuple-element.114, bf16[512,768]{1,0:T(8,128)(2,1)S(1)} %copy-done.13, bf16[768,3072]{1,0:T(8,128)(2,1)S(1)} %bitcast.142, f32[512,3072]{1,0:T(8,128)} %get-tuple-element.152, f32[3072]{0:T(1024)S(1)} %copy-done.34), kind=kOutput, calls=%fused_computation.17 | convolution fusion | flops 2442654720 | bytes 21258240 | tf_op jit(solution)/shard_map/dot_general | solution.py:32
  198.5 3.9 fusion.74
  202.4 8.3 %fusion.1 = bf16[2,768,3072]{2,1,0:T(8,128)(2,1)} fusion(bf16[1,512,3072]{2,1,0:T(8,128)(2,1)S(1)} %bitcast.162, bf16[1,512,3072]{2,1,0:T(8,128)(2,1)S(1)} %bitcast.163, bf16[1,512,768]{2,1,0:T(8,128)(2,1)S(1)} %bitcast.146, bf16[1,512,768]{2,1,0:T(8,128)(2,1)S(1)} %copy-done.16), kind=kOutput, calls=%fused_computation.4 | convolution fusion | flops 4835770368 | bytes 17301504 | tf_op jit(solution)/shard_map/dot_general | solution.py:316
  223.4 3.0 copy.99
  230.1 3.8 convolution_convert_fusion.1
  233.9 5.1 %collective-permute-done.10 = f32[12,512]{1,0:T(8,128)} collective-permute-done((f32[12,512]{1,0:T(8,128)}, f32[12,512]{1,0:T(8,128)}, u32[]{:S(2)}, u32[]{:S(2)}) %collective-permute-start.10) | collective-permute-done | bytes 24608 | tf_op jit(solution)/shard_map/ppermute | solution.py:305
  241.3 2.9 broadcast_in_dim.41.lser_ref
  246.4 24.1 %shard_map.306 = (bf16[512,768]{1,0:T(8,128)(2,1)}, bf16[512,768]{1,0:T(8,128)(2,1)}, bf16[512,768]{1,0:T(8,128)(2,1)}) custom-call(s32[2]{0:T(128)} %pad_add_fusion.meta_ref, bf16[512,768]{1,0:T(8,128)(2,1)} %add_convert_fusion.3.q_ref, bf16[512,768]{1,0:T(8,128)(2,1)} %convolution_convert_fusion.3.k_ref, bf16[512,768]{1,0:T(8,128)(2,1)} %add_convert_fusion.2.v_ref, ...), custom_call_target="tpu_custom_call" | custom-call | flops 4026531840 | bytes 21233664 | tf_op jit(solution)/shard_map/pallas_call | solution.py:234
  270.5 3.9 convolution_convert_fusion
  300.3 24.7 %psum.7 = f32[9216]{0:T(1024)S(1)} all-reduce(f32[9216]{0:T(1024)} %constant_dynamic-update-slice_fusion), channel_id=1, replica_groups=mesh['dp'=8,'tensor'=4] {'dp'}, use_global_device_ids=true, to_apply=%region_20.21 | all-reduce | flops 9216 | bytes 73728 | tf_op jit(solution)/shard_map/psum | solution.py:370
  329.4 6.9 %add_convert_fusion = bf16[512,768]{1,0:T(8,128)(2,1)} fusion(f32[512,768]{1,0:T(8,128)S(1)} %get-tuple-element.151, bf16[512,3072]{1,0:T(8,128)(2,1)} %copy-done.49, bf16[768,3072]{1,0:T(8,128)(2,1)} %bitcast.143, f32[768]{0:T(1024)S(1)} %copy-done.40), kind=kOutput, calls=%fused_computation.83 | convolution fusion | flops 2417098752 | bytes 10226688 | tf_op jit(solution)/shard_map/dot_general | solution.py:28
  342.9 68.2 %reduce-scatter.5.cloned.1.call-done = bf16[2,96,3072]{2,1,0:T(8,128)(2,1)} async-done(((bf16[2,768,3072]{2,1,0:T(8,128)(2,1)}), bf16[2,96,3072]{2,1,0:T(8,128)(2,1)}) %reduce-scatter.5.cloned.1.call-update) | async-done | bytes 1179664 | tf_op jit(solution)/shard_map/reduce_scatter | solution.py:67
  414.2 3.3 collective-permute-start.17
  425.3 17.6 %collective-permute-done.16 = bf16[96,1536]{1,0:T(8,128)(2,1)S(1)} collective-permute-done((bf16[96,1536]{1,0:T(8,128)(2,1)S(1)}, bf16[96,1536]{1,0:T(8,128)(2,1)S(1)}, u32[]{:S(2)}, u32[]{:S(2)}) %collective-permute-start.16) | collective-permute-done | bytes 294944 | tf_op jit(solution)/shard_map/ppermute | solution.py:80
  (235 shorter events, 119.9 us)
Async XLA Ops:
  7.2 60.6 %all-gather.3.cloned.1.call-start = ((), (), s32[]{:S(2)}) async-start(), calls=%async_computation.2 | async-start | bytes 5308416 | tf_op jit(solution)/shard_map/all_gather | solution.py:52
  9.1 9.4 %collective-permute-start.2 = (bf16[96,768]{1,0:T(8,128)(2,1)S(1)}, bf16[96,768]{1,0:T(8,128)(2,1)S(1)}, u32[]{:S(2)}, u32[]{:S(2)}) collective-permute-start(bf16[96,768]{1,0:T(8,128)(2,1)S(1)} %pad_maximum_fusion.5), channel_id=1, source_target_pairs={{0,3},{1,0},{2,1},{3,2},{4,7},{5,4},{6,5},{7,6},{8,11},{9,8},{10,9... | collective-permute-start | bytes 442376 | tf_op jit(solution)/shard_map/ppermute | solution.py:47
  14.2 12.5 %collective-permute-start.1 = (bf16[96,768]{1,0:T(8,128)(2,1)S(1)}, bf16[96,768]{1,0:T(8,128)(2,1)S(1)}, u32[]{:S(2)}, u32[]{:S(2)}) collective-permute-start(bf16[96,768]{1,0:T(8,128)(2,1)S(1)} %pad_maximum_fusion.5), channel_id=1, source_target_pairs={{0,2},{1,3},{2,0},{3,1},{4,6},{5,7},{6,4},{7,5},{8,10},{9,11},{10,... | collective-permute-start | bytes 442376 | tf_op jit(solution)/shard_map/ppermute | solution.py:47
  14.2 12.5 %collective-permute-start = (bf16[96,768]{1,0:T(8,128)(2,1)S(1)}, bf16[96,768]{1,0:T(8,128)(2,1)S(1)}, u32[]{:S(2)}, u32[]{:S(2)}) collective-permute-start(bf16[96,768]{1,0:T(8,128)(2,1)S(1)} %pad_maximum_fusion.5), channel_id=1, source_target_pairs={{0,1},{1,2},{2,3},{3,0},{4,5},{5,6},{6,7},{7,4},{8,9},{9,10},{10,1... | collective-permute-start | bytes 442376 | tf_op jit(solution)/shard_map/ppermute | solution.py:47
  28.4 123.7 %all-gather.5.cloned.1.call-start = ((), (), s32[]{:S(2)}) async-start(), calls=%async_computation.3 | async-start | bytes 10616832 | tf_op jit(solution)/shard_map/all_gather | solution.py:52
  28.5 8.9 %collective-permute-start.7 = (bf16[96,1536]{1,0:T(8,128)(2,1)S(1)}, bf16[96,1536]{1,0:T(8,128)(2,1)S(1)}, u32[]{:S(2)}, u32[]{:S(2)}) collective-permute-start(bf16[96,1536]{1,0:T(8,128)(2,1)S(1)} %get-tuple-element.141), channel_id=1, source_target_pairs={{0,3},{1,0},{2,1},{3,2},{4,7},{5,4},{6,5},{7,6},{8,11},{9,8},{10,9... | collective-permute-start | bytes 884744 | tf_op jit(solution)/shard_map/ppermute | solution.py:47
  29.9 26.9 %collective-permute-start.6 = (bf16[96,1536]{1,0:T(8,128)(2,1)S(1)}, bf16[96,1536]{1,0:T(8,128)(2,1)S(1)}, u32[]{:S(2)}, u32[]{:S(2)}) collective-permute-start(bf16[96,1536]{1,0:T(8,128)(2,1)S(1)} %get-tuple-element.141), channel_id=1, source_target_pairs={{0,2},{1,3},{2,0},{3,1},{4,6},{5,7},{6,4},{7,5},{8,10},{9,11},{10,... | collective-permute-start | bytes 884744 | tf_op jit(solution)/shard_map/ppermute | solution.py:47
  31.4 25.3 %collective-permute-start.5 = (bf16[96,1536]{1,0:T(8,128)(2,1)S(1)}, bf16[96,1536]{1,0:T(8,128)(2,1)S(1)}, u32[]{:S(2)}, u32[]{:S(2)}) collective-permute-start(bf16[96,1536]{1,0:T(8,128)(2,1)S(1)} %get-tuple-element.141), channel_id=1, source_target_pairs={{0,1},{1,2},{2,3},{3,0},{4,5},{5,6},{6,7},{7,4},{8,9},{9,10},{10,1... | collective-permute-start | bytes 884744 | tf_op jit(solution)/shard_map/ppermute | solution.py:47
  58.8 278.8 %reduce-scatter.3.cloned.1.call-start = ((), (), s32[]{:S(2)}) async-start(), calls=%async_computation.4 | async-start | bytes 5308416 | tf_op jit(solution)/shard_map/reduce_scatter | solution.py:67
  60.7 58.8 %copy-start.23 = (f32[512]{0:T(512)}, f32[512]{0:T(512)S(1)}, u32[]{:S(2)}) copy-start(f32[512]{0:T(512)S(1)} %fusion.51) | copy-start | bytes 6148
  90.3 32.4 %collective-permute-start.3 = (bf16[512,768]{1,0:T(8,128)(2,1)}, bf16[512,768]{1,0:T(8,128)(2,1)}, u32[]{:S(2)}, u32[]{:S(2)}) collective-permute-start(bf16[512,768]{1,0:T(8,128)(2,1)} %convolution_convert_fusion.3.k_ref), channel_id=1, source_target_pairs={{0,1},{2,3},{4,5},{6,7},{8,9},{10,11},{12,13},{14,15},{16,17},{18,... | collective-permute-start | bytes 2359304 | tf_op jit(solution)/shard_map/ppermute | solution.py:303
  96.5 31.6 %collective-permute-start.4 = (bf16[512,768]{1,0:T(8,128)(2,1)}, bf16[512,768]{1,0:T(8,128)(2,1)}, u32[]{:S(2)}, u32[]{:S(2)}) collective-permute-start(bf16[512,768]{1,0:T(8,128)(2,1)} %add_convert_fusion.2.v_ref), channel_id=1, source_target_pairs={{0,1},{2,3},{4,5},{6,7},{8,9},{10,11},{12,13},{14,15},{16,17},{18,... | collective-permute-start | bytes 2359304 | tf_op jit(solution)/shard_map/ppermute | solution.py:303
  121.3 25.7 %copy-start.41 = (f32[768]{0:T(1024)S(1)}, f32[768]{0:T(1024)}, u32[]{:S(2)}) copy-start(f32[768]{0:T(1024)} %convert_element_type.118) | copy-start | bytes 9220
  121.3 112.6 %collective-permute-start.8 = (bf16[512,768]{1,0:T(8,128)(2,1)}, bf16[512,768]{1,0:T(8,128)(2,1)}, u32[]{:S(2)}, u32[]{:S(2)}) collective-permute-start(bf16[512,768]{1,0:T(8,128)(2,1)} %add_convert_fusion.3.q_ref), channel_id=1, source_target_pairs={{1,0},{3,2},{5,4},{7,6},{9,8},{11,10},{13,12},{15,14},{17,16},{19,... | collective-permute-start | bytes 2359304 | tf_op jit(solution)/shard_map/ppermute | solution.py:305
  170.6 18.5 %copy-start.5 = (bf16[96,8,4,768]{3,1,2,0:T(8,128)(2,1)}, bf16[96,8,4,768]{3,1,2,0:T(8,128)(2,1)S(1)}, u32[]{:S(2)}) copy-start(bf16[96,8,4,768]{3,1,2,0:T(8,128)(2,1)S(1)} %copy.117) | copy-start | bytes 14155780
  170.6 18.4 %copy-start.13 = (bf16[512,768]{1,0:T(8,128)(2,1)S(1)}, bf16[512,768]{1,0:T(8,128)(2,1)}, u32[]{:S(2)}) copy-start(bf16[512,768]{1,0:T(8,128)(2,1)} %param.20) | copy-start | bytes 2359300
  216.8 22.5 %collective-permute-start.9 = (bf16[512,768]{1,0:T(8,128)(2,1)}, bf16[512,768]{1,0:T(8,128)(2,1)}, u32[]{:S(2)}, u32[]{:S(2)}) collective-permute-start(bf16[512,768]{1,0:T(8,128)(2,1)} %convolution_convert_fusion.2.do_ref), channel_id=1, source_target_pairs={{1,0},{3,2},{5,4},{7,6},{9,8},{11,10},{13,12},{15,14},{17,16},{19,... | collective-permute-start | bytes 2359304 | tf_op jit(solution)/shard_map/ppermute | solution.py:333
  219.6 19.4 %collective-permute-start.10 = (f32[12,512]{1,0:T(8,128)}, f32[12,512]{1,0:T(8,128)}, u32[]{:S(2)}, u32[]{:S(2)}) collective-permute-start(f32[12,512]{1,0:T(8,128)} %slice_reduce_fusion), channel_id=1, source_target_pairs={{1,0},{3,2},{5,4},{7,6},{9,8},{11,10},{13,12},{15,14},{17,16},{19,... | collective-permute-start | bytes 73736 | tf_op jit(solution)/shard_map/ppermute | solution.py:305
  228.7 10.6 %collective-permute-start.11 = (f32[12,512]{1,0:T(8,128)}, f32[12,512]{1,0:T(8,128)S(1)}, u32[]{:S(2)}, u32[]{:S(2)}) collective-permute-start(f32[12,512]{1,0:T(8,128)} %bitcast.160), channel_id=1, source_target_pairs={{1,0},{3,2},{5,4},{7,6},{9,8},{11,10},{13,12},{15,14},{17,16},{19,... | collective-permute-start | bytes 73736 | tf_op jit(solution)/shard_map/ppermute | solution.py:333
  246.4 24.1 %copy-start.24 = (f32[512]{0:T(512)S(1)}, f32[512]{0:T(512)}, u32[]{:S(2)}) copy-start(f32[512]{0:T(512)} %copy-done.23) | copy-start | bytes 6148
  246.4 24.1 %copy-start.39 = (f32[768]{0:T(1024)S(1)}, f32[768]{0:T(1024)}, u32[]{:S(2)}) copy-start(f32[768]{0:T(1024)} %convert_element_type.111) | copy-start | bytes 9220
  277.2 133.9 %reduce-scatter.5.cloned.1.call-start = ((), (), s32[]{:S(2)}) async-start(), calls=%async_computation.5 | async-start | bytes 10616832 | tf_op jit(solution)/shard_map/reduce_scatter | solution.py:67
  289.2 40.3 %copy-start.40 = (f32[768]{0:T(1024)S(1)}, f32[768]{0:T(1024)}, u32[]{:S(2)}) copy-start(f32[768]{0:T(1024)} %convert_element_type.124) | copy-start | bytes 9220
  325.0 11.4 %collective-permute-start.20 = (f32[9216]{0:T(1024)S(1)}, f32[9216]{0:T(1024)S(1)}, u32[]{:S(2)}, u32[]{:S(2)}) collective-permute-start(f32[9216]{0:T(1024)S(1)} %psum.7), channel_id=1, source_target_pairs={{0,3},{1,0},{2,1},{3,2},{4,7},{5,4},{6,5},{7,6},{8,11},{9,8},{10,9... | collective-permute-start | bytes 110600 | tf_op jit(solution)/shard_map/ppermute | solution.py:373
  326.4 10.0 %collective-permute-start.19 = (f32[9216]{0:T(1024)S(1)}, f32[9216]{0:T(1024)S(1)}, u32[]{:S(2)}, u32[]{:S(2)}) collective-permute-start(f32[9216]{0:T(1024)S(1)} %psum.7), channel_id=1, source_target_pairs={{0,2},{1,3},{2,0},{3,1},{4,6},{5,7},{6,4},{7,5},{8,10},{9,11},{10,... | collective-permute-start | bytes 110600 | tf_op jit(solution)/shard_map/ppermute | solution.py:373
  327.5 8.9 %collective-permute-start.18 = (f32[9216]{0:T(1024)S(1)}, f32[9216]{0:T(1024)S(1)}, u32[]{:S(2)}, u32[]{:S(2)}) collective-permute-start(f32[9216]{0:T(1024)S(1)} %psum.7), channel_id=1, source_target_pairs={{0,1},{1,2},{2,3},{3,0},{4,5},{5,6},{6,7},{7,4},{8,9},{9,10},{10,1... | collective-permute-start | bytes 110600 | tf_op jit(solution)/shard_map/ppermute | solution.py:373
  340.3 77.2 %collective-permute-start.14 = (bf16[96,768]{0,1:T(8,128)(2,1)}, bf16[96,768]{0,1:T(8,128)(2,1)}, u32[]{:S(2)}, u32[]{:S(2)}) collective-permute-start(bf16[96,768]{0,1:T(8,128)(2,1)} %get-tuple-element.128), channel_id=1, source_target_pairs={{0,3},{1,0},{2,1},{3,2},{4,7},{5,4},{6,5},{7,6},{8,11},{9,8},{10,9... | collective-permute-start | bytes 442376 | tf_op jit(solution)/shard_map/ppermute | solution.py:80
  342.2 76.5 %collective-permute-start.13 = (bf16[96,768]{0,1:T(8,128)(2,1)S(1)}, bf16[96,768]{0,1:T(8,128)(2,1)}, u32[]{:S(2)}, u32[]{:S(2)}) collective-permute-start(bf16[96,768]{0,1:T(8,128)(2,1)S(1)} %get-tuple-element.129), channel_id=1, source_target_pairs={{0,2},{1,3},{2,0},{3,1},{4,6},{5,7},{6,4},{7,5},{8,10},{9,11},{10,... | collective-permute-start | bytes 442376 | tf_op jit(solution)/shard_map/ppermute | solution.py:80
  342.3 76.4 %collective-permute-start.12 = (bf16[96,768]{0,1:T(8,128)(2,1)S(1)}, bf16[96,768]{0,1:T(8,128)(2,1)}, u32[]{:S(2)}, u32[]{:S(2)}) collective-permute-start(bf16[96,768]{0,1:T(8,128)(2,1)S(1)} %get-tuple-element.127), channel_id=1, source_target_pairs={{0,1},{1,2},{2,3},{3,0},{4,5},{5,6},{6,7},{7,4},{8,9},{9,10},{10,1... | collective-permute-start | bytes 442376 | tf_op jit(solution)/shard_map/ppermute | solution.py:80
  414.2 11.1 %collective-permute-start.17 = (bf16[96,1536]{1,0:T(8,128)(2,1)}, bf16[96,1536]{1,0:T(8,128)(2,1)S(1)}, u32[]{:S(2)}, u32[]{:S(2)}) collective-permute-start(bf16[96,1536]{1,0:T(8,128)(2,1)} %get-tuple-element.124), channel_id=1, source_target_pairs={{0,3},{1,0},{2,1},{3,2},{4,7},{5,4},{6,5},{7,6},{8,11},{9,8},{10,9... | collective-permute-start | bytes 884744 | tf_op jit(solution)/shard_map/ppermute | solution.py:80
  417.5 25.3 %collective-permute-start.16 = (bf16[96,1536]{1,0:T(8,128)(2,1)S(1)}, bf16[96,1536]{1,0:T(8,128)(2,1)S(1)}, u32[]{:S(2)}, u32[]{:S(2)}) collective-permute-start(bf16[96,1536]{1,0:T(8,128)(2,1)S(1)} %get-tuple-element.123), channel_id=1, source_target_pairs={{0,2},{1,3},{2,0},{3,1},{4,6},{5,7},{6,4},{7,5},{8,10},{9,11},{10,... | collective-permute-start | bytes 884744 | tf_op jit(solution)/shard_map/ppermute | solution.py:80
  417.6 25.3 %collective-permute-start.15 = (bf16[96,1536]{1,0:T(8,128)(2,1)S(1)}, bf16[96,1536]{1,0:T(8,128)(2,1)}, u32[]{:S(2)}, u32[]{:S(2)}) collective-permute-start(bf16[96,1536]{1,0:T(8,128)(2,1)S(1)} %get-tuple-element.122), channel_id=1, source_target_pairs={{0,1},{1,2},{2,3},{3,0},{4,5},{5,6},{6,7},{7,4},{8,9},{9,10},{10,1... | collective-permute-start | bytes 884744 | tf_op jit(solution)/shard_map/ppermute | solution.py:80
  (43 other events, 158.9 us)
Sparse Core Ops, SparseCore 0:
  28.5 39.2 all-gather.2
  69.6 58.6 all-gather.4
  277.3 53.7 reduce-scatter.2
  334.5 76.6 reduce-scatter.4

commit v7 on v6

--- a/solution.py
+++ b/solution.py
@@ -55,7 +55,7 @@
     for piece in shards:
         c = piece.shape[1]
         block = full[:, :, :, start : start + c]
-        out.append(block.transpose(0, 2, 1, 3).reshape(dp * r, tp * c))
+        out.append(block.transpose(1, 3, 0, 2).reshape(tp * c, dp * r))
         start += c
     return out
 
@@ -282,11 +282,9 @@
     to_second = [(t, t + 1) for t in range(0, tp, 2)]
     to_first = [(t + 1, t) for t in range(0, tp, 2)]
 
-    full_query, full_key, full_value, out_t = gather_joined([w_query, w_key, w_value, w_out.T], dp, tp)
-    full_out = out_t.T
-    full_up, down_t = gather_joined([w_up, w_down.T], dp, tp)
-    full_down = down_t.T
-    width = full_query.shape[1]
+    query_t, key_t, value_t, full_out = gather_joined([w_query, w_key, w_value, w_out.T], dp, tp)
+    up_t, full_down = gather_joined([w_up, w_down.T], dp, tp)
+    width = query_t.shape[0]
     heads = width // HEAD
 
     gain_first = gain_one.astype(f32)
@@ -296,9 +294,9 @@
 
     in_rows = inputs.astype(f32)
     normed_one = layer_norm(in_rows, gain_first, shift_first).astype(bf16)
-    key_rows = dot_right(normed_one, full_key).astype(bf16)
-    value_rows = (dot_right(normed_one, full_value) + b_value.astype(f32)).astype(bf16)
-    queries = (dot_right(normed_one, full_query) + b_query.astype(f32)).astype(bf16)
+    key_rows = dot_back(normed_one, key_t).astype(bf16)
+    value_rows = (dot_back(normed_one, value_t) + b_value.astype(f32)).astype(bf16)
+    queries = (dot_back(normed_one, query_t) + b_query.astype(f32)).astype(bf16)
     meta = jnp.stack([half, prefix_len]).astype(jnp.int32)
     k_oth, v_oth = lax.ppermute((key_rows, value_rows), "tensor", to_second)
     attended, o_full, lse_wide = attention_forward(meta, queries, key_rows, value_rows, k_oth, v_oth)
@@ -306,7 +304,7 @@
 
     middle = in_rows + dot_right(attended, full_out) + b_out.astype(f32)
     normed_two = layer_norm(middle, gain_second, shift_second).astype(bf16)
-    pre_act = dot_right(normed_two, full_up) + b_up.astype(f32)
+    pre_act = dot_back(normed_two, up_t) + b_up.astype(f32)
     activated = gelu_exact(pre_act).astype(bf16)
     result = (middle + dot_right(activated, full_down) + b_down.astype(f32)).astype(bf16)
 
@@ -319,7 +317,7 @@
         (((1,), (1,)), ((0,), (0,))),
         preferred_element_type=f32,
     )
-    grad_norm_two = dot_back(grad_pre, full_up)
+    grad_norm_two = dot_right(grad_pre, up_t)
     ffn_grad, grad_norm_two = lax.optimization_barrier((ffn_grad, grad_norm_two))
     ffn_rows = scatter_rows(ffn_grad, axis=1)
     up_rows = ffn_rows[0]
@@ -346,7 +344,7 @@
     attn_rows = scatter_rows(attn_grad)
     qkv_rows = attn_rows[:, : 3 * width]
     out_rows = attn_rows[:, 3 * width :]
-    grad_norm_one = dot_back(grad_q, full_query) + dot_back(grad_k, full_key) + dot_back(grad_v, full_value)
+    grad_norm_one = dot_right(grad_q, query_t) + dot_right(grad_k, key_t) + dot_right(grad_v, value_t)
     norm_one_back = jax.vjp(layer_norm, in_rows, gain_first, shift_first)[1](grad_norm_one)
     grad_input = grad_middle + norm_one_back[0]
 

time: 460 us -> 460 us (level)
    dot_general x6, matrix products: 19.2 us -> 36.3 us  [dot_back(): lax.dot_general(first_op, second_op, (((1,), (1,)), ((), ())), preferred_...]
    dot_general x6, matrix products: 34.4 us -> 17.2 us  [dot_right(): return jnp.dot(first_op, second_op, preferred_element_type=jnp.float32)]
where the time goes in v7:
time: 460 us; the launch traced here: 452 us
  waiting for transfers between devices  140 us (30%)
  local copies, waits for them, and re-layouts  90.3 us (20%)
  matrix products  69.5 us (15%)
  Pallas kernels  43 us (9%)
  starting transfers between devices  35 us (8%)
  other arithmetic  33.9 us (7%)
  blocking collectives  24.7 us (5%)
  between operations  15 us (3%)
    reduce_scatter x2, waiting for transfers between devices, scatter_rows(): lax.psum_scatter(grad.astype(LINK), 'dp', scatter_dimension=axis, tiled=T...  68.3 us
    dot_general x6, matrix products, dot_back(): lax.dot_general(first_op, second_op, (((1,), (1,)), ((), ())), preferred_...  36.3 us
    ppermute x6, waiting for transfers between devices, gather_joined(): lax.ppermute(joined, 'tensor', [(i, (i + step) % tp) for i in range(tp)])  33.9 us
    transpose x8, local copies, waits for them, and re-layouts, gather_joined(): out.append(block.transpose(1, 3, 0, 2).reshape(tp * c, dp * r))  33.6 us
    psum x1, blocking collectives, layer(): joined = lax.psum(jnp.concatenate(vectors), 'dp')  24.7 us
    pallas_call x1, Pallas kernels, attention_backward(): pl.pallas_call(attn_bwd_kernel, out_shape=tuple((jax.ShapeDtypeStruct(q.s...  24.1 us
    ppermute x6, waiting for transfers between devices, sum_over_tensor(): lax.ppermute(sent, 'tensor', [(i, (i + step) % tp) for i in range(tp)])  20.1 us
    unnamed x114, local copies, waits for them, and re-layouts  19.2 us
  transfers between devices with their start and end apart: 25, of which 11 were waited for; matrix products, arithmetic and copies ran while one was open for 38% of the time, Pallas kernels for 4%

profile of v7, /device:TPU:0, one launch (start us, length us, event | category | flops | bytes accessed | tf_op | source)
XLA Modules:
  0.0 451.8 jit_solution(3842668504511193851)
XLA Ops:
  9.1 5.1 %collective-permute-start.2 = (bf16[96,768]{1,0:T(8,128)(2,1)S(1)}, bf16[96,768]{1,0:T(8,128)(2,1)S(1)}, u32[]{:S(2)}, u32[]{:S(2)}) collective-permute-start(bf16[96,768]{1,0:T(8,128)(2,1)S(1)} %pad_maximum_fusion.5), channel_id=1, source_target_pairs={{0,3},{1,0},{2,1},{3,2},{4,7},{5,4},{6,5},{7,6},{8,11},{9,8},{10,9... | collective-permute-start | bytes 442376 | tf_op jit(solution)/shard_map/ppermute | solution.py:47
  18.5 8.2 %collective-permute-done.1 = bf16[96,768]{1,0:T(8,128)(2,1)S(1)} collective-permute-done((bf16[96,768]{1,0:T(8,128)(2,1)S(1)}, bf16[96,768]{1,0:T(8,128)(2,1)S(1)}, u32[]{:S(2)}, u32[]{:S(2)}) %collective-permute-start.1) | collective-permute-done | bytes 147488 | tf_op jit(solution)/shard_map/ppermute | solution.py:47
  33.4 4.0 collective-permute-done.7
  37.4 19.4 %collective-permute-done.6 = bf16[96,1536]{1,0:T(8,128)(2,1)S(1)} collective-permute-done((bf16[96,1536]{1,0:T(8,128)(2,1)S(1)}, bf16[96,1536]{1,0:T(8,128)(2,1)S(1)}, u32[]{:S(2)}, u32[]{:S(2)}) %collective-permute-start.6) | collective-permute-done | bytes 294944 | tf_op jit(solution)/shard_map/ppermute | solution.py:47
  60.7 7.1 %all-gather.3.cloned.1.call-done = bf16[8,4,96,768]{3,2,1,0:T(8,128)(2,1)} async-done(((bf16[1,4,96,768]{3,2,1,0:T(8,128)(2,1)}), bf16[8,4,96,768]{3,2,1,0:T(8,128)(2,1)}) %all-gather.3.cloned.1.call-update) | async-done | bytes 4718608 | tf_op jit(solution)/shard_map/all_gather | solution.py:52
  67.7 7.0 %slice_bitcast_fusion.2 = (bf16[4,192,8,96]{1,3,0,2:T(8,128)(2,1)S(1)}, bf16[4,192,8,96]{1,3,0,2:T(8,128)(2,1)}, bf16[4,192,8,96]{1,3,0,2:T(8,128)(2,1)}, bf16[4,192,8,96]{1,3,0,2:T(8,128)(2,1)}) fusion(bf16[8,4,96,768]{3,2,1,0:T(8,128)(2,1)} %all-gather.3.cloned.1.call-done), kind=kLoop, calls=%fused_computation.69 | loop fusion | bytes 9437184 | tf_op jit(solution)/shard_map/transpose | solution.py:58
  77.6 3.9 reshape.212
  84.3 2.9 reshape.213
  87.3 3.1 convolution_convert_fusion.3.k_ref
  90.3 4.3 collective-permute-start.3
  110.0 3.8 reshape.211
  115.6 3.9 reshape.214
  122.7 5.4 %collective-permute-done.4.vo_ref = bf16[512,768]{1,0:T(8,128)(2,1)} collective-permute-done((bf16[512,768]{1,0:T(8,128)(2,1)}, bf16[512,768]{1,0:T(8,128)(2,1)}, u32[]{:S(2)}, u32[]{:S(2)}) %collective-permute-start.4) | collective-permute-done | bytes 786464 | tf_op jit(solution)/shard_map/ppermute | solution.py:301
  128.1 18.8 %shard_map.305 = (bf16[512,768]{1,0:T(8,128)(2,1)}, f32[512,768]{1,0:T(8,128)}, f32[12,512,128]{2,1,0:T(8,128)}) custom-call(s32[2]{0:T(128)} %pad_add_fusion.meta_ref, bf16[512,768]{1,0:T(8,128)(2,1)} %add_convert_fusion.3.q_ref, bf16[512,768]{1,0:T(8,128)(2,1)} %convolution_convert_fusion.3.k_ref, bf16[512,768]{1,0:T(8,128)(2,1)} %add_convert_fusion.2.v_ref, ...), custom_call_target="tpu_custom_call" | custom-call | flops 1610612736 | bytes 9437184 | tf_op jit(solution)/shard_map/pallas_call | solution.py:208
  152.1 6.7 %slice_bitcast_fusion = (bf16[4,768,8,96]{1,3,0,2:T(8,128)(2,1)S(1)}, bf16[4,768,8,96]{1,3,0,2:T(8,128)(2,1)}) fusion(bf16[8,4,96,1536]{3,2,1,0:T(8,128)(2,1)} %all-gather.5.cloned.1.call-done), kind=kLoop, calls=%fused_computation.33 | loop fusion | bytes 18874368 | tf_op jit(solution)/shard_map/transpose | solution.py:58
  158.8 6.0 %copy.96 = bf16[4,768,8,96]{1,0,3,2:T(4,128)(2,1)S(1)} copy(bf16[4,768,8,96]{1,3,0,2:T(8,128)(2,1)} %get-tuple-element.116) | data formatting | bytes 9437184 | tf_op jit(solution)/shard_map/transpose | solution.py:58
  165.8 3.6 copy.97
  170.6 18.4 %multiply_convert_fusion = (bf16[512,3072]{1,0:T(8,128)(2,1)S(1)}, f32[512,3072]{1,0:T(8,128)}, f32[512,3072]{1,0:T(8,128)}) fusion(f32[3072]{0:T(1024)S(1)} %copy-done.34, bf16[3072,768]{0,1:T(8,128)(2,1)S(1)} %bitcast.140, f32[512,768]{1,0:T(8,128)S(1)} %get-tuple-element.151, f32[768]{0:T(1024)S(1)} %copy-done.32, f32[768]{0:T(1024)S(1)} %convert_element_type.119, ...), kind=kOutput, calls=%fused_computation.18 | convolution fusion | flops 2521694208 | bytes 22042624 | tf_op jit(solution)/shard_map/dot_general | solution.py:32
  189.0 9.5 %convert_reduce_fusion = (f32[3072]{0:T(1024)}, bf16[512,3072]{1,0:T(8,128)(2,1)S(1)}) fusion(f32[512,3072]{1,0:T(8,128)} %get-tuple-element.114, bf16[512,768]{1,0:T(8,128)(2,1)S(1)} %copy-done.13, bf16[3072,768]{0,1:T(8,128)(2,1)S(1)} %bitcast.138, f32[512,3072]{1,0:T(8,128)} %get-tuple-element.152, f32[3072]{0:T(1024)S(1)} %copy-done.34), kind=kOutput, calls=%fused_computation.17 | convolution fusion | flops 2442654720 | bytes 21258240 | tf_op jit(solution)/shard_map/dot_general | solution.py:32
  198.5 3.9 fusion.74
  202.4 8.3 %fusion.1 = bf16[2,768,3072]{2,1,0:T(8,128)(2,1)} fusion(bf16[1,512,3072]{2,1,0:T(8,128)(2,1)S(1)} %bitcast.158, bf16[1,512,3072]{2,1,0:T(8,128)(2,1)S(1)} %bitcast.159, bf16[1,512,768]{2,1,0:T(8,128)(2,1)S(1)} %bitcast.142, bf16[1,512,768]{2,1,0:T(8,128)(2,1)S(1)} %copy-done.16), kind=kOutput, calls=%fused_computation.4 | convolution fusion | flops 4835770368 | bytes 17301504 | tf_op jit(solution)/shard_map/dot_general | solution.py:314
  223.4 3.0 copy.99
  230.1 3.8 convolution_convert_fusion.1
  233.9 5.1 %collective-permute-done.10 = f32[12,512]{1,0:T(8,128)} collective-permute-done((f32[12,512]{1,0:T(8,128)}, f32[12,512]{1,0:T(8,128)}, u32[]{:S(2)}, u32[]{:S(2)}) %collective-permute-start.10) | collective-permute-done | bytes 24608 | tf_op jit(solution)/shard_map/ppermute | solution.py:303
  241.3 2.9 broadcast_in_dim.41.lser_ref
  246.4 24.1 %shard_map.306 = (bf16[512,768]{1,0:T(8,128)(2,1)}, bf16[512,768]{1,0:T(8,128)(2,1)}, bf16[512,768]{1,0:T(8,128)(2,1)}) custom-call(s32[2]{0:T(128)} %pad_add_fusion.meta_ref, bf16[512,768]{1,0:T(8,128)(2,1)} %add_convert_fusion.3.q_ref, bf16[512,768]{1,0:T(8,128)(2,1)} %convolution_convert_fusion.3.k_ref, bf16[512,768]{1,0:T(8,128)(2,1)} %add_convert_fusion.2.v_ref, ...), custom_call_target="tpu_custom_call" | custom-call | flops 4026531840 | bytes 21233664 | tf_op jit(solution)/shard_map/pallas_call | solution.py:234
  270.5 3.9 convolution_convert_fusion
  300.3 24.7 %psum.7 = f32[9216]{0:T(1024)S(1)} all-reduce(f32[9216]{0:T(1024)} %constant_dynamic-update-slice_fusion), channel_id=1, replica_groups=mesh['dp'=8,'tensor'=4] {'dp'}, use_global_device_ids=true, to_apply=%region_20.21 | all-reduce | flops 9216 | bytes 73728 | tf_op jit(solution)/shard_map/psum | solution.py:368
  329.4 6.9 %add_convert_fusion = bf16[512,768]{1,0:T(8,128)(2,1)} fusion(f32[512,768]{1,0:T(8,128)S(1)} %get-tuple-element.151, bf16[512,3072]{1,0:T(8,128)(2,1)} %copy-done.49, bf16[3072,768]{0,1:T(8,128)(2,1)} %bitcast.139, f32[768]{0:T(1024)S(1)} %copy-done.40), kind=kOutput, calls=%fused_computation.83 | convolution fusion | flops 2417098752 | bytes 10226688 | tf_op jit(solution)/shard_map/dot_general | solution.py:28
  342.9 68.2 %reduce-scatter.5.cloned.1.call-done = bf16[2,96,3072]{2,1,0:T(8,128)(2,1)} async-done(((bf16[2,768,3072]{2,1,0:T(8,128)(2,1)}), bf16[2,96,3072]{2,1,0:T(8,128)(2,1)}) %reduce-scatter.5.cloned.1.call-update) | async-done | bytes 1179664 | tf_op jit(solution)/shard_map/reduce_scatter | solution.py:67
  414.2 3.3 collective-permute-start.17
  425.3 17.6 %collective-permute-done.16 = bf16[96,1536]{1,0:T(8,128)(2,1)S(1)} collective-permute-done((bf16[96,1536]{1,0:T(8,128)(2,1)S(1)}, bf16[96,1536]{1,0:T(8,128)(2,1)S(1)}, u32[]{:S(2)}, u32[]{:S(2)}) %collective-permute-start.16) | collective-permute-done | bytes 294944 | tf_op jit(solution)/shard_map/ppermute | solution.py:80
  (235 shorter events, 119.9 us)
Async XLA Ops:
  7.2 60.6 %all-gather.3.cloned.1.call-start = ((), (), s32[]{:S(2)}) async-start(), calls=%async_computation.2 | async-start | bytes 5308416 | tf_op jit(solution)/shard_map/all_gather | solution.py:52
  9.1 9.4 %collective-permute-start.2 = (bf16[96,768]{1,0:T(8,128)(2,1)S(1)}, bf16[96,768]{1,0:T(8,128)(2,1)S(1)}, u32[]{:S(2)}, u32[]{:S(2)}) collective-permute-start(bf16[96,768]{1,0:T(8,128)(2,1)S(1)} %pad_maximum_fusion.5), channel_id=1, source_target_pairs={{0,3},{1,0},{2,1},{3,2},{4,7},{5,4},{6,5},{7,6},{8,11},{9,8},{10,9... | collective-permute-start | bytes 442376 | tf_op jit(solution)/shard_map/ppermute | solution.py:47
  14.2 12.5 %collective-permute-start.1 = (bf16[96,768]{1,0:T(8,128)(2,1)S(1)}, bf16[96,768]{1,0:T(8,128)(2,1)S(1)}, u32[]{:S(2)}, u32[]{:S(2)}) collective-permute-start(bf16[96,768]{1,0:T(8,128)(2,1)S(1)} %pad_maximum_fusion.5), channel_id=1, source_target_pairs={{0,2},{1,3},{2,0},{3,1},{4,6},{5,7},{6,4},{7,5},{8,10},{9,11},{10,... | collective-permute-start | bytes 442376 | tf_op jit(solution)/shard_map/ppermute | solution.py:47
  14.2 12.5 %collective-permute-start = (bf16[96,768]{1,0:T(8,128)(2,1)S(1)}, bf16[96,768]{1,0:T(8,128)(2,1)S(1)}, u32[]{:S(2)}, u32[]{:S(2)}) collective-permute-start(bf16[96,768]{1,0:T(8,128)(2,1)S(1)} %pad_maximum_fusion.5), channel_id=1, source_target_pairs={{0,1},{1,2},{2,3},{3,0},{4,5},{5,6},{6,7},{7,4},{8,9},{9,10},{10,1... | collective-permute-start | bytes 442376 | tf_op jit(solution)/shard_map/ppermute | solution.py:47
  28.4 123.7 %all-gather.5.cloned.1.call-start = ((), (), s32[]{:S(2)}) async-start(), calls=%async_computation.3 | async-start | bytes 10616832 | tf_op jit(solution)/shard_map/all_gather | solution.py:52
  28.5 8.9 %collective-permute-start.7 = (bf16[96,1536]{1,0:T(8,128)(2,1)S(1)}, bf16[96,1536]{1,0:T(8,128)(2,1)S(1)}, u32[]{:S(2)}, u32[]{:S(2)}) collective-permute-start(bf16[96,1536]{1,0:T(8,128)(2,1)S(1)} %get-tuple-element.141), channel_id=1, source_target_pairs={{0,3},{1,0},{2,1},{3,2},{4,7},{5,4},{6,5},{7,6},{8,11},{9,8},{10,9... | collective-permute-start | bytes 884744 | tf_op jit(solution)/shard_map/ppermute | solution.py:47
  29.9 26.9 %collective-permute-start.6 = (bf16[96,1536]{1,0:T(8,128)(2,1)S(1)}, bf16[96,1536]{1,0:T(8,128)(2,1)S(1)}, u32[]{:S(2)}, u32[]{:S(2)}) collective-permute-start(bf16[96,1536]{1,0:T(8,128)(2,1)S(1)} %get-tuple-element.141), channel_id=1, source_target_pairs={{0,2},{1,3},{2,0},{3,1},{4,6},{5,7},{6,4},{7,5},{8,10},{9,11},{10,... | collective-permute-start | bytes 884744 | tf_op jit(solution)/shard_map/ppermute | solution.py:47
  31.4 25.3 %collective-permute-start.5 = (bf16[96,1536]{1,0:T(8,128)(2,1)S(1)}, bf16[96,1536]{1,0:T(8,128)(2,1)S(1)}, u32[]{:S(2)}, u32[]{:S(2)}) collective-permute-start(bf16[96,1536]{1,0:T(8,128)(2,1)S(1)} %get-tuple-element.141), channel_id=1, source_target_pairs={{0,1},{1,2},{2,3},{3,0},{4,5},{5,6},{6,7},{7,4},{8,9},{9,10},{10,1... | collective-permute-start | bytes 884744 | tf_op jit(solution)/shard_map/ppermute | solution.py:47
  58.8 278.8 %reduce-scatter.3.cloned.1.call-start = ((), (), s32[]{:S(2)}) async-start(), calls=%async_computation.4 | async-start | bytes 5308416 | tf_op jit(solution)/shard_map/reduce_scatter | solution.py:67
  60.7 58.8 %copy-start.23 = (f32[512]{0:T(512)}, f32[512]{0:T(512)S(1)}, u32[]{:S(2)}) copy-start(f32[512]{0:T(512)S(1)} %fusion.51) | copy-start | bytes 6148
  90.3 32.4 %collective-permute-start.3 = (bf16[512,768]{1,0:T(8,128)(2,1)}, bf16[512,768]{1,0:T(8,128)(2,1)}, u32[]{:S(2)}, u32[]{:S(2)}) collective-permute-start(bf16[512,768]{1,0:T(8,128)(2,1)} %convolution_convert_fusion.3.k_ref), channel_id=1, source_target_pairs={{0,1},{2,3},{4,5},{6,7},{8,9},{10,11},{12,13},{14,15},{16,17},{18,... | collective-permute-start | bytes 2359304 | tf_op jit(solution)/shard_map/ppermute | solution.py:301
  96.5 31.6 %collective-permute-start.4 = (bf16[512,768]{1,0:T(8,128)(2,1)}, bf16[512,768]{1,0:T(8,128)(2,1)}, u32[]{:S(2)}, u32[]{:S(2)}) collective-permute-start(bf16[512,768]{1,0:T(8,128)(2,1)} %add_convert_fusion.2.v_ref), channel_id=1, source_target_pairs={{0,1},{2,3},{4,5},{6,7},{8,9},{10,11},{12,13},{14,15},{16,17},{18,... | collective-permute-start | bytes 2359304 | tf_op jit(solution)/shard_map/ppermute | solution.py:301
  121.3 25.7 %copy-start.41 = (f32[768]{0:T(1024)S(1)}, f32[768]{0:T(1024)}, u32[]{:S(2)}) copy-start(f32[768]{0:T(1024)} %convert_element_type.118) | copy-start | bytes 9220
  121.3 112.6 %collective-permute-start.8 = (bf16[512,768]{1,0:T(8,128)(2,1)}, bf16[512,768]{1,0:T(8,128)(2,1)}, u32[]{:S(2)}, u32[]{:S(2)}) collective-permute-start(bf16[512,768]{1,0:T(8,128)(2,1)} %add_convert_fusion.3.q_ref), channel_id=1, source_target_pairs={{1,0},{3,2},{5,4},{7,6},{9,8},{11,10},{13,12},{15,14},{17,16},{19,... | collective-permute-start | bytes 2359304 | tf_op jit(solution)/shard_map/ppermute | solution.py:303
  170.6 18.5 %copy-start.5 = (bf16[96,8,4,768]{3,1,2,0:T(8,128)(2,1)}, bf16[96,8,4,768]{3,1,2,0:T(8,128)(2,1)S(1)}, u32[]{:S(2)}) copy-start(bf16[96,8,4,768]{3,1,2,0:T(8,128)(2,1)S(1)} %copy.117) | copy-start | bytes 14155780
  170.6 18.4 %copy-start.13 = (bf16[512,768]{1,0:T(8,128)(2,1)S(1)}, bf16[512,768]{1,0:T(8,128)(2,1)}, u32[]{:S(2)}) copy-start(bf16[512,768]{1,0:T(8,128)(2,1)} %param.20) | copy-start | bytes 2359300
  216.8 22.5 %collective-permute-start.9 = (bf16[512,768]{1,0:T(8,128)(2,1)}, bf16[512,768]{1,0:T(8,128)(2,1)}, u32[]{:S(2)}, u32[]{:S(2)}) collective-permute-start(bf16[512,768]{1,0:T(8,128)(2,1)} %convolution_convert_fusion.2.do_ref), channel_id=1, source_target_pairs={{1,0},{3,2},{5,4},{7,6},{9,8},{11,10},{13,12},{15,14},{17,16},{19,... | collective-permute-start | bytes 2359304 | tf_op jit(solution)/shard_map/ppermute | solution.py:331
  219.6 19.4 %collective-permute-start.10 = (f32[12,512]{1,0:T(8,128)}, f32[12,512]{1,0:T(8,128)}, u32[]{:S(2)}, u32[]{:S(2)}) collective-permute-start(f32[12,512]{1,0:T(8,128)} %slice_reduce_fusion), channel_id=1, source_target_pairs={{1,0},{3,2},{5,4},{7,6},{9,8},{11,10},{13,12},{15,14},{17,16},{19,... | collective-permute-start | bytes 73736 | tf_op jit(solution)/shard_map/ppermute | solution.py:303
  228.7 10.6 %collective-permute-start.11 = (f32[12,512]{1,0:T(8,128)}, f32[12,512]{1,0:T(8,128)S(1)}, u32[]{:S(2)}, u32[]{:S(2)}) collective-permute-start(f32[12,512]{1,0:T(8,128)} %bitcast.156), channel_id=1, source_target_pairs={{1,0},{3,2},{5,4},{7,6},{9,8},{11,10},{13,12},{15,14},{17,16},{19,... | collective-permute-start | bytes 73736 | tf_op jit(solution)/shard_map/ppermute | solution.py:331
  246.4 24.1 %copy-start.24 = (f32[512]{0:T(512)S(1)}, f32[512]{0:T(512)}, u32[]{:S(2)}) copy-start(f32[512]{0:T(512)} %copy-done.23) | copy-start | bytes 6148
  246.4 24.1 %copy-start.39 = (f32[768]{0:T(1024)S(1)}, f32[768]{0:T(1024)}, u32[]{:S(2)}) copy-start(f32[768]{0:T(1024)} %convert_element_type.111) | copy-start | bytes 9220
  277.2 133.9 %reduce-scatter.5.cloned.1.call-start = ((), (), s32[]{:S(2)}) async-start(), calls=%async_computation.5 | async-start | bytes 10616832 | tf_op jit(solution)/shard_map/reduce_scatter | solution.py:67
  289.2 40.3 %copy-start.40 = (f32[768]{0:T(1024)S(1)}, f32[768]{0:T(1024)}, u32[]{:S(2)}) copy-start(f32[768]{0:T(1024)} %convert_element_type.124) | copy-start | bytes 9220
  325.0 11.4 %collective-permute-start.20 = (f32[9216]{0:T(1024)S(1)}, f32[9216]{0:T(1024)S(1)}, u32[]{:S(2)}, u32[]{:S(2)}) collective-permute-start(f32[9216]{0:T(1024)S(1)} %psum.7), channel_id=1, source_target_pairs={{0,3},{1,0},{2,1},{3,2},{4,7},{5,4},{6,5},{7,6},{8,11},{9,8},{10,9... | collective-permute-start | bytes 110600 | tf_op jit(solution)/shard_map/ppermute | solution.py:371
  326.4 10.0 %collective-permute-start.19 = (f32[9216]{0:T(1024)S(1)}, f32[9216]{0:T(1024)S(1)}, u32[]{:S(2)}, u32[]{:S(2)}) collective-permute-start(f32[9216]{0:T(1024)S(1)} %psum.7), channel_id=1, source_target_pairs={{0,2},{1,3},{2,0},{3,1},{4,6},{5,7},{6,4},{7,5},{8,10},{9,11},{10,... | collective-permute-start | bytes 110600 | tf_op jit(solution)/shard_map/ppermute | solution.py:371
  327.5 8.9 %collective-permute-start.18 = (f32[9216]{0:T(1024)S(1)}, f32[9216]{0:T(1024)S(1)}, u32[]{:S(2)}, u32[]{:S(2)}) collective-permute-start(f32[9216]{0:T(1024)S(1)} %psum.7), channel_id=1, source_target_pairs={{0,1},{1,2},{2,3},{3,0},{4,5},{5,6},{6,7},{7,4},{8,9},{9,10},{10,1... | collective-permute-start | bytes 110600 | tf_op jit(solution)/shard_map/ppermute | solution.py:371
  340.3 77.2 %collective-permute-start.14 = (bf16[96,768]{0,1:T(8,128)(2,1)}, bf16[96,768]{0,1:T(8,128)(2,1)}, u32[]{:S(2)}, u32[]{:S(2)}) collective-permute-start(bf16[96,768]{0,1:T(8,128)(2,1)} %get-tuple-element.128), channel_id=1, source_target_pairs={{0,3},{1,0},{2,1},{3,2},{4,7},{5,4},{6,5},{7,6},{8,11},{9,8},{10,9... | collective-permute-start | bytes 442376 | tf_op jit(solution)/shard_map/ppermute | solution.py:80
  342.2 76.5 %collective-permute-start.13 = (bf16[96,768]{0,1:T(8,128)(2,1)S(1)}, bf16[96,768]{0,1:T(8,128)(2,1)}, u32[]{:S(2)}, u32[]{:S(2)}) collective-permute-start(bf16[96,768]{0,1:T(8,128)(2,1)S(1)} %get-tuple-element.129), channel_id=1, source_target_pairs={{0,2},{1,3},{2,0},{3,1},{4,6},{5,7},{6,4},{7,5},{8,10},{9,11},{10,... | collective-permute-start | bytes 442376 | tf_op jit(solution)/shard_map/ppermute | solution.py:80
  342.3 76.4 %collective-permute-start.12 = (bf16[96,768]{0,1:T(8,128)(2,1)S(1)}, bf16[96,768]{0,1:T(8,128)(2,1)}, u32[]{:S(2)}, u32[]{:S(2)}) collective-permute-start(bf16[96,768]{0,1:T(8,128)(2,1)S(1)} %get-tuple-element.127), channel_id=1, source_target_pairs={{0,1},{1,2},{2,3},{3,0},{4,5},{5,6},{6,7},{7,4},{8,9},{9,10},{10,1... | collective-permute-start | bytes 442376 | tf_op jit(solution)/shard_map/ppermute | solution.py:80
  414.2 11.1 %collective-permute-start.17 = (bf16[96,1536]{1,0:T(8,128)(2,1)}, bf16[96,1536]{1,0:T(8,128)(2,1)S(1)}, u32[]{:S(2)}, u32[]{:S(2)}) collective-permute-start(bf16[96,1536]{1,0:T(8,128)(2,1)} %get-tuple-element.124), channel_id=1, source_target_pairs={{0,3},{1,0},{2,1},{3,2},{4,7},{5,4},{6,5},{7,6},{8,11},{9,8},{10,9... | collective-permute-start | bytes 884744 | tf_op jit(solution)/shard_map/ppermute | solution.py:80
  417.5 25.3 %collective-permute-start.16 = (bf16[96,1536]{1,0:T(8,128)(2,1)S(1)}, bf16[96,1536]{1,0:T(8,128)(2,1)S(1)}, u32[]{:S(2)}, u32[]{:S(2)}) collective-permute-start(bf16[96,1536]{1,0:T(8,128)(2,1)S(1)} %get-tuple-element.123), channel_id=1, source_target_pairs={{0,2},{1,3},{2,0},{3,1},{4,6},{5,7},{6,4},{7,5},{8,10},{9,11},{10,... | collective-permute-start | bytes 884744 | tf_op jit(solution)/shard_map/ppermute | solution.py:80
  417.6 25.3 %collective-permute-start.15 = (bf16[96,1536]{1,0:T(8,128)(2,1)S(1)}, bf16[96,1536]{1,0:T(8,128)(2,1)}, u32[]{:S(2)}, u32[]{:S(2)}) collective-permute-start(bf16[96,1536]{1,0:T(8,128)(2,1)S(1)} %get-tuple-element.122), channel_id=1, source_target_pairs={{0,1},{1,2},{2,3},{3,0},{4,5},{5,6},{6,7},{7,4},{8,9},{9,10},{10,1... | collective-permute-start | bytes 884744 | tf_op jit(solution)/shard_map/ppermute | solution.py:80
  (43 other events, 158.9 us)
Sparse Core Ops, SparseCore 0:
  28.5 39.2 all-gather.2
  69.6 58.6 all-gather.4
  277.3 53.7 reduce-scatter.2
  334.5 76.6 reduce-scatter.4

commit v8 on v6

--- a/solution.py
+++ b/solution.py
@@ -40,7 +40,7 @@
     )
 
 
-def gather_joined(shards, dp, tp):
+def gather_joined(shards, tp):
     r = shards[0].shape[0]
     joined = jnp.concatenate(shards, axis=1)
     pieces = [joined] + [
@@ -49,13 +49,18 @@
     t_index = lax.axis_index("tensor")
     order = (t_index - jnp.arange(tp, dtype=jnp.int32)) % tp
     by_tensor = jnp.take(jnp.stack(pieces), order, axis=0)
-    full = lax.all_gather(by_tensor, "dp", axis=0, tiled=False)
+    strips = []
+    start = 0
+    for piece in shards:
+        c = piece.shape[1]
+        strips.append(by_tensor[:, :, start : start + c].transpose(1, 0, 2).reshape(r, tp * c))
+        start += c
+    full = lax.all_gather(jnp.concatenate(strips, axis=1), "dp", axis=0, tiled=True)
     out = []
     start = 0
     for piece in shards:
-        c = piece.shape[1]
-        block = full[:, :, :, start : start + c]
-        out.append(block.transpose(0, 2, 1, 3).reshape(dp * r, tp * c))
+        c = tp * piece.shape[1]
+        out.append(full[:, start : start + c])
         start += c
     return out
 
@@ -270,7 +275,6 @@
 ):
     f32 = jnp.float32
     bf16 = jnp.bfloat16
-    dp = lax.axis_size("dp")
     tp = lax.axis_size("tensor")
     t_index = lax.axis_index("tensor")
     rows = inputs.shape[0]
@@ -282,10 +286,8 @@
     to_second = [(t, t + 1) for t in range(0, tp, 2)]
     to_first = [(t + 1, t) for t in range(0, tp, 2)]
 
-    full_query, full_key, full_value, out_t = gather_joined([w_query, w_key, w_value, w_out.T], dp, tp)
-    full_out = out_t.T
-    full_up, down_t = gather_joined([w_up, w_down.T], dp, tp)
-    full_down = down_t.T
+    full_query, full_key, full_value, out_t = gather_joined([w_query, w_key, w_value, w_out.T], tp)
+    full_up, down_t = gather_joined([w_up, w_down.T], tp)
     width = full_query.shape[1]
     heads = width // HEAD
 
@@ -304,14 +306,14 @@
     attended, o_full, lse_wide = attention_forward(meta, queries, key_rows, value_rows, k_oth, v_oth)
     q_rcv, lse_rcv = lax.ppermute((queries, lse_wide[:, :, 0]), "tensor", to_first)
 
-    middle = in_rows + dot_right(attended, full_out) + b_out.astype(f32)
+    middle = in_rows + dot_back(attended, out_t) + b_out.astype(f32)
     normed_two = layer_norm(middle, gain_second, shift_second).astype(bf16)
     pre_act = dot_right(normed_two, full_up) + b_up.astype(f32)
     activated = gelu_exact(pre_act).astype(bf16)
-    result = (middle + dot_right(activated, full_down) + b_down.astype(f32)).astype(bf16)
+    result = (middle + dot_back(activated, down_t) + b_down.astype(f32)).astype(bf16)
 
     grad_result = cotangent.astype(f32)
-    grad_act = dot_back(cotangent, full_down)
+    grad_act = dot_right(cotangent, down_t)
     grad_pre = jax.vjp(gelu_exact, pre_act)[1](grad_act)[0].astype(bf16)
     ffn_grad = lax.dot_general(
         jnp.stack([normed_two, cotangent]),
@@ -327,7 +329,7 @@
     norm_two_back = jax.vjp(layer_norm, middle, gain_second, shift_second)[1](grad_norm_two)
     grad_middle = grad_result + norm_two_back[0]
     grad_attn_rows = grad_middle.astype(bf16)
-    grad_attended = dot_back(grad_attn_rows, full_out).astype(bf16)
+    grad_attended = dot_right(grad_attn_rows, out_t).astype(bf16)
 
     delta = jnp.sum((grad_attended.astype(f32) * o_full).reshape(rows, heads, HEAD), axis=-1).T
     do_rcv, delta_rcv = lax.ppermute((grad_attended, delta), "tensor", to_first)

time: 460 us -> 423 us (0.920)
  local copies, waits for them, and re-layouts: 90.3 us -> 29.9 us
  waiting for transfers between devices: 140 us -> 174 us
  other arithmetic: 33.9 us -> 20.8 us
  matrix products: 69.5 us -> 75.3 us
    transpose x8 -> x0, local copies, waits for them, and re-layouts: 33.6 us -> none  [gather_joined(): out.append(block.transpose(0, 2, 1, 3).reshape(dp * r, tp * c))]
    ppermute x2, waiting for transfers between devices: 5.4 us -> 22.8 us  [layer(): k_oth, v_oth = lax.ppermute((key_rows, value_rows), 'tensor', to_second)]
    reshape x4 -> x6, local copies, waits for them, and re-layouts: 14.5 us -> 0.65 us  [gather_joined(): by_tensor[:, :, start:start + c].transpose(1, 0, 2).reshape(r, tp * c)]
    unnamed x114 -> x79, local copies, waits for them, and re-layouts: 19.2 us -> 9.08 us
    reduce_scatter x2, waiting for transfers between devices: 68.3 us -> 75.9 us  [scatter_rows(): lax.psum_scatter(grad.astype(LINK), 'dp', scatter_dimension=axis, tiled=T...]
    ppermute x6, waiting for transfers between devices: 33.9 us -> 39 us  [gather_joined(): lax.ppermute(joined, 'tensor', [(i, (i + step) % tp) for i in range(tp)])]
  transfers between devices with their start and end apart: 25 -> 25, of which waited for: 11 -> 13; matrix products, arithmetic and copies ran while one was open for 38% -> 24% of each run, Pallas kernels for 4% -> 4%
where the time goes in v8:
time: 423 us; the launch traced here: 417 us
  waiting for transfers between devices  174 us (41%)
  matrix products  75.3 us (18%)
  Pallas kernels  42.4 us (10%)
  starting transfers between devices  36.3 us (9%)
  local copies, waits for them, and re-layouts  29.9 us (7%)
  blocking collectives  23.9 us (6%)
  other arithmetic  20.8 us (5%)
  between operations  14.9 us (4%)
    reduce_scatter x2, waiting for transfers between devices, scatter_rows(): lax.psum_scatter(grad.astype(LINK), 'dp', scatter_dimension=axis, tiled=T...  75.9 us
    ppermute x6, waiting for transfers between devices, gather_joined(): lax.ppermute(joined, 'tensor', [(i, (i + step) % tp) for i in range(tp)])  39 us
    dot_general x6, matrix products, dot_right(): return jnp.dot(first_op, second_op, preferred_element_type=jnp.float32)  37 us
    pallas_call x1, Pallas kernels, attention_backward(): pl.pallas_call(attn_bwd_kernel, out_shape=tuple((jax.ShapeDtypeStruct(q.s...  24 us
    psum x1, blocking collectives, layer(): joined = lax.psum(jnp.concatenate(vectors), 'dp')  23.9 us
    ppermute x2, waiting for transfers between devices, layer(): k_oth, v_oth = lax.ppermute((key_rows, value_rows), 'tensor', to_second)  22.8 us
    dot_general x6, matrix products, dot_back(): lax.dot_general(first_op, second_op, (((1,), (1,)), ((), ())), preferred_...  22.4 us
    ppermute x6, waiting for transfers between devices, sum_over_tensor(): lax.ppermute(sent, 'tensor', [(i, (i + step) % tp) for i in range(tp)])  19.9 us
  transfers between devices with their start and end apart: 25, of which 13 were waited for; matrix products, arithmetic and copies ran while one was open for 24% of the time, Pallas kernels for 4%

profile of v8, /device:TPU:0, one launch (start us, length us, event | category | flops | bytes accessed | tf_op | source)
XLA Modules:
  0.0 417.2 jit_solution(1859420220219955956)
XLA Ops:
  10.8 5.1 %collective-permute-start.2 = (bf16[96,768]{0,1:T(8,128)(2,1)S(1)}, bf16[96,768]{0,1:T(8,128)(2,1)S(1)}, u32[]{:S(2)}, u32[]{:S(2)}) collective-permute-start(bf16[96,768]{0,1:T(8,128)(2,1)S(1)} %get-tuple-element.125), channel_id=1, source_target_pairs={{0,3},{1,0},{2,1},{3,2},{4,7},{5,4},{6,5},{7,6},{8,11},{9,8},{10,9... | collective-permute-start | bytes 442376 | tf_op jit(solution)/shard_map/ppermute | solution.py:47
  17.0 4.3 %collective-permute-done.2 = bf16[96,768]{0,1:T(8,128)(2,1)S(1)} collective-permute-done((bf16[96,768]{0,1:T(8,128)(2,1)S(1)}, bf16[96,768]{0,1:T(8,128)(2,1)S(1)}, u32[]{:S(2)}, u32[]{:S(2)}) %collective-permute-start.2) | collective-permute-done | bytes 147488 | tf_op jit(solution)/shard_map/ppermute | solution.py:47
  21.3 11.4 %collective-permute-done.1 = bf16[96,768]{0,1:T(8,128)(2,1)S(1)} collective-permute-done((bf16[96,768]{0,1:T(8,128)(2,1)S(1)}, bf16[96,768]{0,1:T(8,128)(2,1)S(1)}, u32[]{:S(2)}, u32[]{:S(2)}) %collective-permute-start.1) | collective-permute-done | bytes 147488 | tf_op jit(solution)/shard_map/ppermute | solution.py:47
  35.8 2.6 collective-permute-start.6
  40.3 3.4 collective-permute-done.7
  43.6 20.0 %collective-permute-done.6 = bf16[96,1536]{1,0:T(8,128)(2,1)S(1)} collective-permute-done((bf16[96,1536]{1,0:T(8,128)(2,1)S(1)}, bf16[96,1536]{1,0:T(8,128)(2,1)S(1)}, u32[]{:S(2)}, u32[]{:S(2)}) %collective-permute-start.6) | collective-permute-done | bytes 294944 | tf_op jit(solution)/shard_map/ppermute | solution.py:47
  66.9 7.7 %all-gather.3.cloned.1.call-done = bf16[768,3072]{1,0:T(8,128)(2,1)} async-done(((bf16[96,3072]{1,0:T(8,128)(2,1)}), bf16[768,3072]{1,0:T(8,128)(2,1)}) %all-gather.3.cloned.1.call-update) | async-done | bytes 4718608 | tf_op jit(solution)/shard_map/all_gather | solution.py:58
  76.9 3.6 collective-permute-start.3
  86.8 3.1 add_convert_fusion.3.q_ref
  91.7 6.7 %collective-permute-done.3.ko_ref = bf16[512,768]{1,0:T(8,128)(2,1)S(1)} collective-permute-done((bf16[512,768]{1,0:T(8,128)(2,1)S(1)}, bf16[512,768]{1,0:T(8,128)(2,1)S(1)}, u32[]{:S(2)}, u32[]{:S(2)}) %collective-permute-start.3) | collective-permute-done | bytes 786464 | tf_op jit(solution)/shard_map/ppermute | solution.py:305
  98.4 16.1 %collective-permute-done.4.vo_ref = bf16[512,768]{1,0:T(8,128)(2,1)} collective-permute-done((bf16[512,768]{1,0:T(8,128)(2,1)S(1)}, bf16[512,768]{1,0:T(8,128)(2,1)}, u32[]{:S(2)}, u32[]{:S(2)}) %collective-permute-start.4) | collective-permute-done | bytes 786464 | tf_op jit(solution)/shard_map/ppermute | solution.py:305
  114.5 18.4 %shard_map.305 = (bf16[512,768]{1,0:T(8,128)(2,1)}, f32[512,768]{1,0:T(8,128)}, f32[12,512,128]{2,1,0:T(8,128)}) custom-call(s32[2]{0:T(128)} %pad_add_fusion.meta_ref, bf16[512,768]{1,0:T(8,128)(2,1)} %add_convert_fusion.3.q_ref, bf16[512,768]{1,0:T(8,128)(2,1)} %copy-done.8, bf16[512,768]{1,0:T(8,128)(2,1)} %copy-done.10, bf16[512,768]{1,0:T(8,128)(2,1)} %copy-done.9, ...), custom_call_target="tpu_custom_call" | custom-call | flops 1610612736 | bytes 9437184 | tf_op jit(solution)/shard_map/pallas_call | solution.py:213
  133.0 2.4 fusion.99
  136.9 19.1 %multiply_convert_fusion = (bf16[512,3072]{1,0:T(8,128)(2,1)S(1)}, f32[512,3072]{1,0:T(8,128)S(1)}, f32[512,3072]{1,0:T(8,128)}) fusion(f32[3072]{0:T(1024)S(1)} %convert_element_type.122, bf16[768,6144]{1,0:T(8,128)(2,1)} %all-gather.5.cloned.1.call-done, f32[512,768]{1,0:T(8,128)S(1)} %get-tuple-element.135, f32[768]{0:T(1024)S(1)} %convert_element_type.120, ...), kind=kOutput, calls=%fused_computation.18 | convolution fusion | flops 2521694208 | bytes 22042624 | tf_op jit(solution)/shard_map/dot_general | solution.py:28
  156.1 8.2 %convert_reduce_fusion = (f32[3072]{0:T(1024)S(1)}, bf16[512,3072]{1,0:T(8,128)(2,1)S(1)}) fusion(f32[512,3072]{1,0:T(8,128)S(1)} %get-tuple-element.96, bf16[512,768]{1,0:T(8,128)(2,1)S(1)} %copy-done.11, bf16[768,6144]{1,0:T(8,128)(2,1)S(1)} %copy-done.27, f32[512,3072]{1,0:T(8,128)} %get-tuple-element.136, f32[3072]{0:T(1024)S(1)} %convert_element_type.122), kind=kOutput, calls=%fused_computation.17 | convolution fusion | flops 2442654720 | bytes 21258240 | tf_op jit(solution)/shard_map/dot_general | solution.py:28
  165.9 8.2 %fusion.1 = bf16[2,768,3072]{2,1,0:T(8,128)(2,1)} fusion(bf16[1,512,3072]{2,1,0:T(8,128)(2,1)S(1)} %bitcast.131, bf16[1,512,3072]{2,1,0:T(8,128)(2,1)S(1)} %bitcast.132, bf16[1,512,768]{2,1,0:T(8,128)(2,1)S(1)} %bitcast.112, bf16[1,512,768]{2,1,0:T(8,128)(2,1)S(1)} %copy-done.15), kind=kOutput, calls=%fused_computation.4 | convolution fusion | flops 4835770368 | bytes 17301504 | tf_op jit(solution)/shard_map/dot_general | solution.py:318
  174.1 5.9 %fusion.21 = f32[512,768]{1,0:T(8,128)S(1)} fusion(bf16[512,3072]{1,0:T(8,128)(2,1)} %copy-done.31, bf16[768,6144]{1,0:T(8,128)(2,1)} %all-gather.5.cloned.1.call-done), kind=kOutput, calls=%fused_computation.38 | convolution fusion | flops 2415919104 | bytes 9437184 | tf_op jit(solution)/shard_map/dot_general | solution.py:32
  189.1 3.0 copy.76
  195.0 3.8 convolution_convert_fusion.1
  198.8 7.5 %collective-permute-done.10 = f32[12,512]{1,0:T(8,128)S(1)} collective-permute-done((f32[12,512]{1,0:T(8,128)S(1)}, f32[12,512]{1,0:T(8,128)S(1)}, u32[]{:S(2)}, u32[]{:S(2)}) %collective-permute-start.10) | collective-permute-done | bytes 24608 | tf_op jit(solution)/shard_map/ppermute | solution.py:307
  206.6 2.3 broadcast_in_dim.40.dl_ref
  213.2 24.0 %shard_map.306 = (bf16[512,768]{1,0:T(8,128)(2,1)}, bf16[512,768]{1,0:T(8,128)(2,1)}, bf16[512,768]{1,0:T(8,128)(2,1)}) custom-call(s32[2]{0:T(128)} %pad_add_fusion.meta_ref, bf16[512,768]{1,0:T(8,128)(2,1)} %add_convert_fusion.3.q_ref, bf16[512,768]{1,0:T(8,128)(2,1)} %copy-done.8, bf16[512,768]{1,0:T(8,128)(2,1)} %copy-done.10, ...), custom_call_target="tpu_custom_call" | custom-call | flops 4026531840 | bytes 21233664 | tf_op jit(solution)/shard_map/pallas_call | solution.py:239
  237.2 3.9 convolution_convert_fusion
  241.1 2.8 pad_maximum_fusion
  250.8 2.6 fusion.92
  257.3 23.9 %psum.7 = f32[9216]{0:T(1024)S(1)} all-reduce(f32[9216]{0:T(1024)S(1)} %constant_dynamic-update-slice_fusion), channel_id=1, replica_groups=mesh['dp'=8,'tensor'=4] {'dp'}, use_global_device_ids=true, to_apply=%region_20.21 | all-reduce | flops 9216 | bytes 73728 | tf_op jit(solution)/shard_map/psum | solution.py:372
  286.0 7.2 %add_convert_fusion = bf16[512,768]{1,0:T(8,128)(2,1)} fusion(f32[512,768]{1,0:T(8,128)S(1)} %get-tuple-element.135, bf16[512,3072]{1,0:T(8,128)(2,1)} %copy-done.30, bf16[768,6144]{1,0:T(8,128)(2,1)} %all-gather.5.cloned.1.call-done, f32[768]{0:T(1024)S(1)} %convert_element_type.124), kind=kOutput, calls=%fused_computation.85 | convolution fusion | flops 2417098752 | bytes 10226688 | tf_op jit(solution)/shard_map/dot_general | solution.py:32
  294.4 3.1 reduce-scatter.3.cloned.1.call-done
  300.4 3.3 collective-permute-start.14
  304.8 72.8 %reduce-scatter.5.cloned.1.call-done = bf16[2,96,3072]{2,1,0:T(8,128)(2,1)} async-done(((bf16[2,768,3072]{2,1,0:T(8,128)(2,1)}), bf16[2,96,3072]{2,1,0:T(8,128)(2,1)}) %reduce-scatter.5.cloned.1.call-update) | async-done | bytes 1179664 | tf_op jit(solution)/shard_map/reduce_scatter | solution.py:72
  380.0 3.4 collective-permute-start.17
  390.8 17.7 %collective-permute-done.16 = bf16[96,1536]{1,0:T(8,128)(2,1)S(1)} collective-permute-done((bf16[96,1536]{1,0:T(8,128)(2,1)S(1)}, bf16[96,1536]{1,0:T(8,128)(2,1)S(1)}, u32[]{:S(2)}, u32[]{:S(2)}) %collective-permute-start.16) | collective-permute-done | bytes 294944 | tf_op jit(solution)/shard_map/ppermute | solution.py:85
  (196 shorter events, 75.0 us)
Async XLA Ops:
  7.2 67.5 %all-gather.3.cloned.1.call-start = ((), (), s32[]{:S(2)}) async-start(), calls=%async_computation.2 | async-start | bytes 5308416 | tf_op jit(solution)/shard_map/all_gather | solution.py:58
  10.8 10.5 %collective-permute-start.2 = (bf16[96,768]{0,1:T(8,128)(2,1)S(1)}, bf16[96,768]{0,1:T(8,128)(2,1)S(1)}, u32[]{:S(2)}, u32[]{:S(2)}) collective-permute-start(bf16[96,768]{0,1:T(8,128)(2,1)S(1)} %get-tuple-element.125), channel_id=1, source_target_pairs={{0,3},{1,0},{2,1},{3,2},{4,7},{5,4},{6,5},{7,6},{8,11},{9,8},{10,9... | collective-permute-start | bytes 442376 | tf_op jit(solution)/shard_map/ppermute | solution.py:47
  16.0 16.7 %collective-permute-start.1 = (bf16[96,768]{0,1:T(8,128)(2,1)S(1)}, bf16[96,768]{0,1:T(8,128)(2,1)S(1)}, u32[]{:S(2)}, u32[]{:S(2)}) collective-permute-start(bf16[96,768]{0,1:T(8,128)(2,1)S(1)} %get-tuple-element.125), channel_id=1, source_target_pairs={{0,2},{1,3},{2,0},{3,1},{4,6},{5,7},{6,4},{7,5},{8,10},{9,11},{10,... | collective-permute-start | bytes 442376 | tf_op jit(solution)/shard_map/ppermute | solution.py:47
  16.0 16.7 %collective-permute-start = (bf16[96,768]{0,1:T(8,128)(2,1)S(1)}, bf16[96,768]{0,1:T(8,128)(2,1)S(1)}, u32[]{:S(2)}, u32[]{:S(2)}) collective-permute-start(bf16[96,768]{0,1:T(8,128)(2,1)S(1)} %get-tuple-element.125), channel_id=1, source_target_pairs={{0,1},{1,2},{2,3},{3,0},{4,5},{5,6},{6,7},{7,4},{8,9},{9,10},{10,1... | collective-permute-start | bytes 442376 | tf_op jit(solution)/shard_map/ppermute | solution.py:47
  35.3 101.7 %all-gather.5.cloned.1.call-start = ((), (), s32[]{:S(2)}) async-start(), calls=%async_computation.3 | async-start | bytes 10616832 | tf_op jit(solution)/shard_map/all_gather | solution.py:58
  35.4 8.2 %collective-permute-start.7 = (bf16[96,1536]{1,0:T(8,128)(2,1)S(1)}, bf16[96,1536]{1,0:T(8,128)(2,1)S(1)}, u32[]{:S(2)}, u32[]{:S(2)}) collective-permute-start(bf16[96,1536]{1,0:T(8,128)(2,1)S(1)} %get-tuple-element.123), channel_id=1, source_target_pairs={{0,3},{1,0},{2,1},{3,2},{4,7},{5,4},{6,5},{7,6},{8,11},{9,8},{10,9... | collective-permute-start | bytes 884744 | tf_op jit(solution)/shard_map/ppermute | solution.py:47
  35.8 27.9 %collective-permute-start.6 = (bf16[96,1536]{1,0:T(8,128)(2,1)S(1)}, bf16[96,1536]{1,0:T(8,128)(2,1)S(1)}, u32[]{:S(2)}, u32[]{:S(2)}) collective-permute-start(bf16[96,1536]{1,0:T(8,128)(2,1)S(1)} %get-tuple-element.123), channel_id=1, source_target_pairs={{0,2},{1,3},{2,0},{3,1},{4,6},{5,7},{6,4},{7,5},{8,10},{9,11},{10,... | collective-permute-start | bytes 884744 | tf_op jit(solution)/shard_map/ppermute | solution.py:47
  38.3 25.3 %collective-permute-start.5 = (bf16[96,1536]{1,0:T(8,128)(2,1)S(1)}, bf16[96,1536]{1,0:T(8,128)(2,1)S(1)}, u32[]{:S(2)}, u32[]{:S(2)}) collective-permute-start(bf16[96,1536]{1,0:T(8,128)(2,1)S(1)} %get-tuple-element.123), channel_id=1, source_target_pairs={{0,1},{1,2},{2,3},{3,0},{4,5},{5,6},{6,7},{7,4},{8,9},{9,10},{10,1... | collective-permute-start | bytes 884744 | tf_op jit(solution)/shard_map/ppermute | solution.py:47
  66.0 231.5 %reduce-scatter.3.cloned.1.call-start = ((), (), s32[]{:S(2)}) async-start(), calls=%async_computation.4 | async-start | bytes 5308416 | tf_op jit(solution)/shard_map/reduce_scatter | solution.py:72
  76.9 8.1 %copy-start.25 = (bf16[768]{0:T(1024)(128)(2,1)S(1)}, bf16[768]{0:T(1024)(128)(2,1)}, u32[]{:S(2)}) copy-start(bf16[768]{0:T(1024)(128)(2,1)} %param.34) | copy-start | bytes 4612
  76.9 8.1 %copy-start.29 = (s32[2]{0:T(128)S(1)}, s32[2]{0:T(128)}, u32[]{:S(2)}) copy-start(s32[2]{0:T(128)} %param.19) | copy-start | bytes 28
  76.9 21.4 %collective-permute-start.3 = (bf16[512,768]{1,0:T(8,128)(2,1)S(1)}, bf16[512,768]{1,0:T(8,128)(2,1)S(1)}, u32[]{:S(2)}, u32[]{:S(2)}) collective-permute-start(bf16[512,768]{1,0:T(8,128)(2,1)S(1)} %convolution_convert_fusion.3.k_ref), channel_id=1, source_target_pairs={{0,1},{2,3},{4,5},{6,7},{8,9},{10,11},{12,13},{14,15},{16,17},{18,... | collective-permute-start | bytes 2359304 | tf_op jit(solution)/shard_map/ppermute | solution.py:305
  82.7 31.8 %collective-permute-start.4 = (bf16[512,768]{1,0:T(8,128)(2,1)S(1)}, bf16[512,768]{1,0:T(8,128)(2,1)}, u32[]{:S(2)}, u32[]{:S(2)}) collective-permute-start(bf16[512,768]{1,0:T(8,128)(2,1)S(1)} %add_convert_fusion.2.v_ref), channel_id=1, source_target_pairs={{0,1},{2,3},{4,5},{6,7},{8,9},{10,11},{12,13},{14,15},{16,17},{18,... | collective-permute-start | bytes 2359304 | tf_op jit(solution)/shard_map/ppermute | solution.py:305
  89.9 108.9 %collective-permute-start.8 = (bf16[512,768]{1,0:T(8,128)(2,1)}, bf16[512,768]{1,0:T(8,128)(2,1)}, u32[]{:S(2)}, u32[]{:S(2)}) collective-permute-start(bf16[512,768]{1,0:T(8,128)(2,1)} %add_convert_fusion.3.q_ref), channel_id=1, source_target_pairs={{1,0},{3,2},{5,4},{7,6},{9,8},{11,10},{13,12},{15,14},{17,16},{19,... | collective-permute-start | bytes 2359304 | tf_op jit(solution)/shard_map/ppermute | solution.py:307
  98.4 16.1 %copy-start.9 = (bf16[512,768]{1,0:T(8,128)(2,1)}, bf16[512,768]{1,0:T(8,128)(2,1)S(1)}, u32[]{:S(2)}) copy-start(bf16[512,768]{1,0:T(8,128)(2,1)S(1)} %collective-permute-done.3.ko_ref) | copy-start | bytes 2359300
  136.9 19.1 %copy-start.11 = (bf16[512,768]{1,0:T(8,128)(2,1)S(1)}, bf16[512,768]{1,0:T(8,128)(2,1)}, u32[]{:S(2)}) copy-start(bf16[512,768]{1,0:T(8,128)(2,1)} %param.20) | copy-start | bytes 2359300
  136.9 19.1 %copy-start.27 = (bf16[768,6144]{1,0:T(8,128)(2,1)S(1)}, bf16[768,6144]{1,0:T(8,128)(2,1)}, u32[]{:S(2)}) copy-start(bf16[768,6144]{1,0:T(8,128)(2,1)} %all-gather.5.cloned.1.call-done) | copy-start | bytes 28311556
  156.1 8.2 %copy-start.30 = (bf16[512,3072]{1,0:T(8,128)(2,1)}, bf16[512,3072]{1,0:T(8,128)(2,1)S(1)}, u32[]{:S(2)}) copy-start(bf16[512,3072]{1,0:T(8,128)(2,1)S(1)} %get-tuple-element.95) | copy-start | bytes 9437188
  156.1 9.8 %copy-start.15 = (bf16[1,512,768]{2,1,0:T(8,128)(2,1)S(1)}, bf16[1,512,768]{2,1,0:T(8,128)(2,1)}, u32[]{:S(2)}) copy-start(bf16[1,512,768]{2,1,0:T(8,128)(2,1)} %fusion.86) | copy-start | bytes 2359300
  184.2 22.4 %collective-permute-start.9 = (bf16[512,768]{1,0:T(8,128)(2,1)S(1)}, bf16[512,768]{1,0:T(8,128)(2,1)}, u32[]{:S(2)}, u32[]{:S(2)}) collective-permute-start(bf16[512,768]{1,0:T(8,128)(2,1)S(1)} %convolution_convert_fusion.2.do_ref), channel_id=1, source_target_pairs={{1,0},{3,2},{5,4},{7,6},{9,8},{11,10},{13,12},{15,14},{17,16},{19,... | collective-permute-start | bytes 2359304 | tf_op jit(solution)/shard_map/ppermute | solution.py:335
  186.4 19.9 %collective-permute-start.10 = (f32[12,512]{1,0:T(8,128)S(1)}, f32[12,512]{1,0:T(8,128)S(1)}, u32[]{:S(2)}, u32[]{:S(2)}) collective-permute-start(f32[12,512]{1,0:T(8,128)S(1)} %slice_reduce_fusion), channel_id=1, source_target_pairs={{1,0},{3,2},{5,4},{7,6},{9,8},{11,10},{13,12},{15,14},{17,16},{19,... | collective-permute-start | bytes 73736 | tf_op jit(solution)/shard_map/ppermute | solution.py:307
  193.7 12.9 %collective-permute-start.11 = (f32[12,512]{1,0:T(8,128)S(1)}, f32[12,512]{1,0:T(8,128)S(1)}, u32[]{:S(2)}, u32[]{:S(2)}) collective-permute-start(f32[12,512]{1,0:T(8,128)S(1)} %bitcast.128), channel_id=1, source_target_pairs={{1,0},{3,2},{5,4},{7,6},{9,8},{11,10},{13,12},{15,14},{17,16},{19,... | collective-permute-start | bytes 73736 | tf_op jit(solution)/shard_map/ppermute | solution.py:335
  244.0 133.6 %reduce-scatter.5.cloned.1.call-start = ((), (), s32[]{:S(2)}) async-start(), calls=%async_computation.5 | async-start | bytes 10616832 | tf_op jit(solution)/shard_map/reduce_scatter | solution.py:72
  281.3 11.9 %collective-permute-start.20 = (f32[9216]{0:T(1024)S(1)}, f32[9216]{0:T(1024)S(1)}, u32[]{:S(2)}, u32[]{:S(2)}) collective-permute-start(f32[9216]{0:T(1024)S(1)} %psum.7), channel_id=1, source_target_pairs={{0,3},{1,0},{2,1},{3,2},{4,7},{5,4},{6,5},{7,6},{8,11},{9,8},{10,9... | collective-permute-start | bytes 110600 | tf_op jit(solution)/shard_map/ppermute | solution.py:375
  282.5 10.7 %collective-permute-start.19 = (f32[9216]{0:T(1024)S(1)}, f32[9216]{0:T(1024)S(1)}, u32[]{:S(2)}, u32[]{:S(2)}) collective-permute-start(f32[9216]{0:T(1024)S(1)} %psum.7), channel_id=1, source_target_pairs={{0,2},{1,3},{2,0},{3,1},{4,6},{5,7},{6,4},{7,5},{8,10},{9,11},{10,... | collective-permute-start | bytes 110600 | tf_op jit(solution)/shard_map/ppermute | solution.py:375
  283.8 9.4 %collective-permute-start.18 = (f32[9216]{0:T(1024)S(1)}, f32[9216]{0:T(1024)S(1)}, u32[]{:S(2)}, u32[]{:S(2)}) collective-permute-start(f32[9216]{0:T(1024)S(1)} %psum.7), channel_id=1, source_target_pairs={{0,1},{1,2},{2,3},{3,0},{4,5},{5,6},{6,7},{7,4},{8,9},{9,10},{10,1... | collective-permute-start | bytes 110600 | tf_op jit(solution)/shard_map/ppermute | solution.py:375
  300.4 83.0 %collective-permute-start.14 = (bf16[96,768]{0,1:T(8,128)(2,1)}, bf16[96,768]{0,1:T(8,128)(2,1)}, u32[]{:S(2)}, u32[]{:S(2)}) collective-permute-start(bf16[96,768]{0,1:T(8,128)(2,1)} %get-tuple-element.106), channel_id=1, source_target_pairs={{0,3},{1,0},{2,1},{3,2},{4,7},{5,4},{6,5},{7,6},{8,11},{9,8},{10,9... | collective-permute-start | bytes 442376 | tf_op jit(solution)/shard_map/ppermute | solution.py:85
  303.7 80.8 %collective-permute-start.13 = (bf16[96,768]{0,1:T(8,128)(2,1)}, bf16[96,768]{0,1:T(8,128)(2,1)}, u32[]{:S(2)}, u32[]{:S(2)}) collective-permute-start(bf16[96,768]{0,1:T(8,128)(2,1)} %get-tuple-element.107), channel_id=1, source_target_pairs={{0,2},{1,3},{2,0},{3,1},{4,6},{5,7},{6,4},{7,5},{8,10},{9,11},{10,... | collective-permute-start | bytes 442376 | tf_op jit(solution)/shard_map/ppermute | solution.py:85
  303.7 80.8 %collective-permute-start.12 = (bf16[96,768]{0,1:T(8,128)(2,1)}, bf16[96,768]{0,1:T(8,128)(2,1)}, u32[]{:S(2)}, u32[]{:S(2)}) collective-permute-start(bf16[96,768]{0,1:T(8,128)(2,1)} %get-tuple-element.105), channel_id=1, source_target_pairs={{0,1},{1,2},{2,3},{3,0},{4,5},{5,6},{6,7},{7,4},{8,9},{9,10},{10,1... | collective-permute-start | bytes 442376 | tf_op jit(solution)/shard_map/ppermute | solution.py:85
  380.0 10.8 %collective-permute-start.17 = (bf16[96,1536]{1,0:T(8,128)(2,1)S(1)}, bf16[96,1536]{1,0:T(8,128)(2,1)S(1)}, u32[]{:S(2)}, u32[]{:S(2)}) collective-permute-start(bf16[96,1536]{1,0:T(8,128)(2,1)S(1)} %get-tuple-element.100), channel_id=1, source_target_pairs={{0,3},{1,0},{2,1},{3,2},{4,7},{5,4},{6,5},{7,6},{8,11},{9,8},{10,9... | collective-permute-start | bytes 884744 | tf_op jit(solution)/shard_map/ppermute | solution.py:85
  383.4 25.1 %collective-permute-start.16 = (bf16[96,1536]{1,0:T(8,128)(2,1)S(1)}, bf16[96,1536]{1,0:T(8,128)(2,1)S(1)}, u32[]{:S(2)}, u32[]{:S(2)}) collective-permute-start(bf16[96,1536]{1,0:T(8,128)(2,1)S(1)} %get-tuple-element.99), channel_id=1, source_target_pairs={{0,2},{1,3},{2,0},{3,1},{4,6},{5,7},{6,4},{7,5},{8,10},{9,11},{10,... | collective-permute-start | bytes 884744 | tf_op jit(solution)/shard_map/ppermute | solution.py:85
  383.4 25.1 %collective-permute-start.15 = (bf16[96,1536]{1,0:T(8,128)(2,1)S(1)}, bf16[96,1536]{1,0:T(8,128)(2,1)}, u32[]{:S(2)}, u32[]{:S(2)}) collective-permute-start(bf16[96,1536]{1,0:T(8,128)(2,1)S(1)} %get-tuple-element.98), channel_id=1, source_target_pairs={{0,1},{1,2},{2,3},{3,0},{4,5},{5,6},{6,7},{7,4},{8,9},{9,10},{10,1... | collective-permute-start | bytes 884744 | tf_op jit(solution)/shard_map/ppermute | solution.py:85
  (25 other events, 81.3 us)
Sparse Core Ops, SparseCore 0:
  35.4 39.2 all-gather.2
  76.5 58.6 all-gather.4
  244.1 53.4 reduce-scatter.2
  300.9 76.6 reduce-scatter.4

commit v9 on v8

--- a/solution.py
+++ b/solution.py
@@ -283,7 +283,6 @@
     half = t_index % pieces
     seq_here = (t_index * rows) // SEQ_LEN
     prefix_len = lax.dynamic_index_in_dim(prefix, seq_here, keepdims=False)
-    to_second = [(t, t + 1) for t in range(0, tp, 2)]
     to_first = [(t + 1, t) for t in range(0, tp, 2)]
 
     full_query, full_key, full_value, out_t = gather_joined([w_query, w_key, w_value, w_out.T], tp)
@@ -298,13 +297,17 @@
 
     in_rows = inputs.astype(f32)
     normed_one = layer_norm(in_rows, gain_first, shift_first).astype(bf16)
+    swap = [(t, t ^ 1) for t in range(tp)]
+    normed_oth = lax.ppermute(normed_one, "tensor", swap)
     key_rows = dot_right(normed_one, full_key).astype(bf16)
     value_rows = (dot_right(normed_one, full_value) + b_value.astype(f32)).astype(bf16)
     queries = (dot_right(normed_one, full_query) + b_query.astype(f32)).astype(bf16)
     meta = jnp.stack([half, prefix_len]).astype(jnp.int32)
-    k_oth, v_oth = lax.ppermute((key_rows, value_rows), "tensor", to_second)
+    k_oth = dot_right(normed_oth, full_key).astype(bf16)
+    v_oth = (dot_right(normed_oth, full_value) + b_value.astype(f32)).astype(bf16)
+    q_rcv = (dot_right(normed_oth, full_query) + b_query.astype(f32)).astype(bf16)
     attended, o_full, lse_wide = attention_forward(meta, queries, key_rows, value_rows, k_oth, v_oth)
-    q_rcv, lse_rcv = lax.ppermute((queries, lse_wide[:, :, 0]), "tensor", to_first)
+    lse_rcv = lax.ppermute(lse_wide[:, :, 0], "tensor", to_first)
 
     middle = in_rows + dot_back(attended, out_t) + b_out.astype(f32)
     normed_two = layer_norm(middle, gain_second, shift_second).astype(bf16)
@@ -322,7 +325,6 @@
         preferred_element_type=f32,
     )
     grad_norm_two = dot_back(grad_pre, full_up)
-    ffn_grad, grad_norm_two = lax.optimization_barrier((ffn_grad, grad_norm_two))
     ffn_rows = scatter_rows(ffn_grad, axis=1)
     up_rows = ffn_rows[0]
     down_rows = ffn_rows[1]

time: 423 us -> 409 us (0.967)
  starting transfers between devices: 36.3 us -> 26.6 us
  waiting for transfers between devices: 174 us -> 167 us
    all_gather x2, waiting for transfers between devices: 7.72 us -> 24.8 us  [gather_joined(): lax.all_gather(jnp.concatenate(strips, axis=1), 'dp', axis=0, tiled=True)]
    ppermute x4 -> x2, waiting for transfers between devices: 30.3 us -> 14.9 us  [the longest x1 7.96 us: layer(): normed_oth = lax.ppermute(normed_one, 'tensor', swap)]
    reduce_scatter x2, waiting for transfers between devices: 75.9 us -> 67.5 us  [scatter_rows(): lax.psum_scatter(grad.astype(LINK), 'dp', scatter_dimension=axis, tiled=T...]
    ppermute x4 -> x2, starting transfers between devices: 8.87 us -> 1.36 us  [the longest x1 1.29 us: layer(): lse_rcv = lax.ppermute(lse_wide[:, :, 0], 'tensor', to_first)]
    dot_general x6 -> x9, matrix products: 37 us -> 41.9 us  [dot_right(): return jnp.dot(first_op, second_op, preferred_element_type=jnp.float32)]
    unnamed x79 -> x77, local copies, waits for them, and re-layouts: 9.08 us -> 7.12 us
  transfers between devices with their start and end apart: 25 -> 23, of which waited for: 13 -> 12; matrix products, arithmetic and copies ran while one was open for 24% -> 17% of each run, Pallas kernels for 4% -> 5%
where the time goes in v9:
time: 409 us; the launch traced here: 403 us
  waiting for transfers between devices  167 us (41%)
  matrix products  78.3 us (19%)
  Pallas kernels  43 us (11%)
  local copies, waits for them, and re-layouts  27.9 us (7%)
  starting transfers between devices  26.6 us (7%)
  blocking collectives  24.8 us (6%)
  other arithmetic  20.8 us (5%)
  between operations  14.8 us (4%)
    reduce_scatter x2, waiting for transfers between devices, scatter_rows(): lax.psum_scatter(grad.astype(LINK), 'dp', scatter_dimension=axis, tiled=T...  67.5 us
    dot_general x9, matrix products, dot_right(): return jnp.dot(first_op, second_op, preferred_element_type=jnp.float32)  41.9 us
    ppermute x6, waiting for transfers between devices, gather_joined(): lax.ppermute(joined, 'tensor', [(i, (i + step) % tp) for i in range(tp)])  39 us
    all_gather x2, waiting for transfers between devices, gather_joined(): lax.all_gather(jnp.concatenate(strips, axis=1), 'dp', axis=0, tiled=True)  24.8 us
    psum x1, blocking collectives, layer(): joined = lax.psum(jnp.concatenate(vectors), 'dp')  24.8 us
    pallas_call x1, Pallas kernels, attention_backward(): pl.pallas_call(attn_bwd_kernel, out_shape=tuple((jax.ShapeDtypeStruct(q.s...  24.1 us
    ppermute x6, waiting for transfers between devices, sum_over_tensor(): lax.ppermute(sent, 'tensor', [(i, (i + step) % tp) for i in range(tp)])  20 us
    dot_general x6, matrix products, dot_back(): lax.dot_general(first_op, second_op, (((1,), (1,)), ((), ())), preferred_...  19.5 us
  transfers between devices with their start and end apart: 23, of which 12 were waited for; matrix products, arithmetic and copies ran while one was open for 17% of the time, Pallas kernels for 5%

profile of v9, /device:TPU:0, one launch (start us, length us, event | category | flops | bytes accessed | tf_op | source)
XLA Modules:
  0.0 402.7 jit_solution(9251390319962706553)
XLA Ops:
  10.8 5.1 %collective-permute-start.2 = (bf16[96,768]{0,1:T(8,128)(2,1)S(1)}, bf16[96,768]{0,1:T(8,128)(2,1)S(1)}, u32[]{:S(2)}, u32[]{:S(2)}) collective-permute-start(bf16[96,768]{0,1:T(8,128)(2,1)S(1)} %get-tuple-element.122), channel_id=1, source_target_pairs={{0,3},{1,0},{2,1},{3,2},{4,7},{5,4},{6,5},{7,6},{8,11},{9,8},{10,9... | collective-permute-start | bytes 442376 | tf_op jit(solution)/shard_map/ppermute | solution.py:47
  17.0 4.3 %collective-permute-done.2 = bf16[96,768]{0,1:T(8,128)(2,1)S(1)} collective-permute-done((bf16[96,768]{0,1:T(8,128)(2,1)S(1)}, bf16[96,768]{0,1:T(8,128)(2,1)S(1)}, u32[]{:S(2)}, u32[]{:S(2)}) %collective-permute-start.2) | collective-permute-done | bytes 147488 | tf_op jit(solution)/shard_map/ppermute | solution.py:47
  21.3 11.4 %collective-permute-done.1 = bf16[96,768]{0,1:T(8,128)(2,1)S(1)} collective-permute-done((bf16[96,768]{0,1:T(8,128)(2,1)S(1)}, bf16[96,768]{0,1:T(8,128)(2,1)S(1)}, u32[]{:S(2)}, u32[]{:S(2)}) %collective-permute-start.1) | collective-permute-done | bytes 147488 | tf_op jit(solution)/shard_map/ppermute | solution.py:47
  35.8 2.6 collective-permute-start.5
  40.3 3.4 collective-permute-done.6
  43.6 20.0 %collective-permute-done.5 = bf16[96,1536]{1,0:T(8,128)(2,1)S(1)} collective-permute-done((bf16[96,1536]{1,0:T(8,128)(2,1)S(1)}, bf16[96,1536]{1,0:T(8,128)(2,1)S(1)}, u32[]{:S(2)}, u32[]{:S(2)}) %collective-permute-start.5) | collective-permute-done | bytes 294944 | tf_op jit(solution)/shard_map/ppermute | solution.py:47
  69.4 5.3 %all-gather.3.cloned.1.call-done = bf16[768,3072]{1,0:T(8,128)(2,1)} async-done(((bf16[96,3072]{1,0:T(8,128)(2,1)}), bf16[768,3072]{1,0:T(8,128)(2,1)}) %all-gather.3.cloned.1.call-update) | async-done | bytes 4718608 | tf_op jit(solution)/shard_map/all_gather | solution.py:58
  74.7 3.1 convolution_convert_fusion.5.k_ref
  77.7 8.0 %collective-permute-done.3 = bf16[512,768]{1,0:T(8,128)(2,1)S(1)} collective-permute-done((bf16[512,768]{1,0:T(8,128)(2,1)S(1)}, bf16[512,768]{1,0:T(8,128)(2,1)S(1)}, u32[]{:S(2)}, u32[]{:S(2)}) %collective-permute-start.3) | collective-permute-done | bytes 786464 | tf_op jit(solution)/shard_map/ppermute | solution.py:301
  85.7 3.3 convolution_convert_fusion.4.ko_ref
  94.1 18.9 %shard_map.305 = (bf16[512,768]{1,0:T(8,128)(2,1)}, f32[512,768]{1,0:T(8,128)}, f32[12,512,128]{2,1,0:T(8,128)}) custom-call(s32[2]{0:T(128)} %pad_add_fusion.meta_ref, bf16[512,768]{1,0:T(8,128)(2,1)} %add_convert_fusion.5.q_ref, bf16[512,768]{1,0:T(8,128)(2,1)} %convolution_convert_fusion.5.k_ref, bf16[512,768]{1,0:T(8,128)(2,1)} %add_convert_fusion.4.v_ref, ...), custom_call_target="tpu_custom_call" | custom-call | flops 1610612736 | bytes 9437184 | tf_op jit(solution)/shard_map/pallas_call | solution.py:213
  113.0 2.4 fusion.97
  115.8 19.5 %all-gather.5.cloned.1.call-done = bf16[768,6144]{1,0:T(8,128)(2,1)} async-done(((bf16[96,6144]{1,0:T(8,128)(2,1)}), bf16[768,6144]{1,0:T(8,128)(2,1)}) %all-gather.5.cloned.1.call-update) | async-done | bytes 9437200 | tf_op jit(solution)/shard_map/all_gather | solution.py:58
  135.3 18.7 %multiply_convert_fusion = (bf16[512,3072]{1,0:T(8,128)(2,1)}, f32[512,3072]{1,0:T(8,128)S(1)}, f32[512,3072]{1,0:T(8,128)S(1)}) fusion(f32[3072]{0:T(1024)S(1)} %convert_element_type.135, bf16[768,6144]{1,0:T(8,128)(2,1)} %all-gather.5.cloned.1.call-done, f32[512,768]{1,0:T(8,128)S(1)} %get-tuple-element.132, f32[768]{0:T(1024)S(1)} %convert_element_type.133, ...), kind=kOutput, calls=%fused_computation.18 | convolution fusion | flops 2521694208 | bytes 22042624 | tf_op jit(solution)/shard_map/dot_general | solution.py:28
  154.0 5.3 %convert_reduce_fusion = (f32[3072]{0:T(1024)S(1)}, bf16[512,3072]{1,0:T(8,128)(2,1)S(1)}) fusion(f32[512,3072]{1,0:T(8,128)S(1)} %get-tuple-element.92, bf16[512,768]{1,0:T(8,128)(2,1)S(1)} %copy-done.4, bf16[768,6144]{1,0:T(8,128)(2,1)S(1)} %copy-done.25, f32[512,3072]{1,0:T(8,128)S(1)} %get-tuple-element.133, f32[3072]{0:T(1024)S(1)} %convert_element_type.135), kind=kOutput, calls=%fused_computation.17 | convolution fusion | flops 2442654720 | bytes 21258240 | tf_op jit(solution)/shard_map/dot_general | solution.py:28
  159.3 3.0 multiply_reduce_fusion
  162.3 3.1 fusion.91
  165.5 3.4 convert_multiply_fusion
  172.4 3.0 add_convert_fusion.qr_ref
  175.4 3.0 copy.75
  181.3 3.3 convolution_convert_fusion.2
  184.6 6.9 %collective-permute-done.8 = f32[12,512]{1,0:T(8,128)S(1)} collective-permute-done((f32[12,512]{1,0:T(8,128)S(1)}, f32[12,512]{1,0:T(8,128)S(1)}, u32[]{:S(2)}, u32[]{:S(2)}) %collective-permute-start.8) | collective-permute-done | bytes 24608 | tf_op jit(solution)/shard_map/ppermute | solution.py:310
  198.4 24.1 %shard_map.306 = (bf16[512,768]{1,0:T(8,128)(2,1)}, bf16[512,768]{1,0:T(8,128)(2,1)}, bf16[512,768]{1,0:T(8,128)(2,1)}) custom-call(s32[2]{0:T(128)} %pad_add_fusion.meta_ref, bf16[512,768]{1,0:T(8,128)(2,1)} %add_convert_fusion.5.q_ref, bf16[512,768]{1,0:T(8,128)(2,1)} %convolution_convert_fusion.5.k_ref, bf16[512,768]{1,0:T(8,128)(2,1)} %add_convert_fusion.4.v_ref, ...), custom_call_target="tpu_custom_call" | custom-call | flops 4026531840 | bytes 21233664 | tf_op jit(solution)/shard_map/pallas_call | solution.py:239
  222.6 3.7 convolution_convert_fusion.1
  226.3 2.9 pad_maximum_fusion
  230.3 9.9 %convolution_convert_fusion = bf16[2,768,3072]{2,1,0:T(8,128)(2,1)} fusion(bf16[1,512,3072]{2,1,0:T(8,128)(2,1)} %bitcast.138, bf16[1,512,3072]{2,1,0:T(8,128)(2,1)} %bitcast.139, bf16[1,512,768]{2,1,0:T(8,128)(2,1)S(1)} %bitcast.117, bf16[1,512,768]{2,1,0:T(8,128)(2,1)} %get-tuple-element.94), kind=kOutput, calls=%fused_computation.3 | convolution fusion | flops 4840488960 | bytes 17301504 | tf_op jit(solution)/shard_map/dot_general | solution.py:321
  247.1 2.4 fusion.90
  252.4 24.8 %psum.7 = f32[9216]{0:T(1024)S(1)} all-reduce(f32[9216]{0:T(1024)S(1)} %constant_dynamic-update-slice_fusion), channel_id=1, replica_groups=mesh['dp'=8,'tensor'=4] {'dp'}, use_global_device_ids=true, to_apply=%region_20.21 | all-reduce | flops 9216 | bytes 73728 | tf_op jit(solution)/shard_map/psum | solution.py:374
  281.5 7.3 %add_convert_fusion.1 = bf16[512,768]{1,0:T(8,128)(2,1)} fusion(f32[512,768]{1,0:T(8,128)} %copy-done.2, bf16[512,3072]{1,0:T(8,128)(2,1)} %get-tuple-element.91, bf16[768,6144]{1,0:T(8,128)(2,1)} %all-gather.5.cloned.1.call-done, f32[768]{0:T(1024)S(1)} %convert_element_type.137), kind=kOutput, calls=%fused_computation.86 | convolution fusion | flops 2417098752 | bytes 10226688 | tf_op jit(solution)/shard_map/dot_general | solution.py:32
  295.6 67.5 %reduce-scatter.5.cloned.1.call-done = bf16[2,96,3072]{2,1,0:T(8,128)(2,1)} async-done(((bf16[2,768,3072]{2,1,0:T(8,128)(2,1)}), bf16[2,96,3072]{2,1,0:T(8,128)(2,1)}) %reduce-scatter.5.cloned.1.call-update) | async-done | bytes 1179664 | tf_op jit(solution)/shard_map/reduce_scatter | solution.py:72
  365.5 3.4 collective-permute-start.15
  376.3 17.7 %collective-permute-done.14 = bf16[96,1536]{1,0:T(8,128)(2,1)S(1)} collective-permute-done((bf16[96,1536]{1,0:T(8,128)(2,1)S(1)}, bf16[96,1536]{1,0:T(8,128)(2,1)S(1)}, u32[]{:S(2)}, u32[]{:S(2)}) %collective-permute-start.14) | collective-permute-done | bytes 294944 | tf_op jit(solution)/shard_map/ppermute | solution.py:85
  (191 shorter events, 67.3 us)
Async XLA Ops:
  7.2 67.5 %all-gather.3.cloned.1.call-start = ((), (), s32[]{:S(2)}) async-start(), calls=%async_computation.2 | async-start | bytes 5308416 | tf_op jit(solution)/shard_map/all_gather | solution.py:58
  10.8 10.5 %collective-permute-start.2 = (bf16[96,768]{0,1:T(8,128)(2,1)S(1)}, bf16[96,768]{0,1:T(8,128)(2,1)S(1)}, u32[]{:S(2)}, u32[]{:S(2)}) collective-permute-start(bf16[96,768]{0,1:T(8,128)(2,1)S(1)} %get-tuple-element.122), channel_id=1, source_target_pairs={{0,3},{1,0},{2,1},{3,2},{4,7},{5,4},{6,5},{7,6},{8,11},{9,8},{10,9... | collective-permute-start | bytes 442376 | tf_op jit(solution)/shard_map/ppermute | solution.py:47
  16.0 16.7 %collective-permute-start.1 = (bf16[96,768]{0,1:T(8,128)(2,1)S(1)}, bf16[96,768]{0,1:T(8,128)(2,1)S(1)}, u32[]{:S(2)}, u32[]{:S(2)}) collective-permute-start(bf16[96,768]{0,1:T(8,128)(2,1)S(1)} %get-tuple-element.122), channel_id=1, source_target_pairs={{0,2},{1,3},{2,0},{3,1},{4,6},{5,7},{6,4},{7,5},{8,10},{9,11},{10,... | collective-permute-start | bytes 442376 | tf_op jit(solution)/shard_map/ppermute | solution.py:47
  16.0 16.7 %collective-permute-start = (bf16[96,768]{0,1:T(8,128)(2,1)S(1)}, bf16[96,768]{0,1:T(8,128)(2,1)S(1)}, u32[]{:S(2)}, u32[]{:S(2)}) collective-permute-start(bf16[96,768]{0,1:T(8,128)(2,1)S(1)} %get-tuple-element.122), channel_id=1, source_target_pairs={{0,1},{1,2},{2,3},{3,0},{4,5},{5,6},{6,7},{7,4},{8,9},{9,10},{10,1... | collective-permute-start | bytes 442376 | tf_op jit(solution)/shard_map/ppermute | solution.py:47
  35.3 100.0 %all-gather.5.cloned.1.call-start = ((), (), s32[]{:S(2)}) async-start(), calls=%async_computation.3 | async-start | bytes 10616832 | tf_op jit(solution)/shard_map/all_gather | solution.py:58
  35.4 8.2 %collective-permute-start.6 = (bf16[96,1536]{1,0:T(8,128)(2,1)S(1)}, bf16[96,1536]{1,0:T(8,128)(2,1)S(1)}, u32[]{:S(2)}, u32[]{:S(2)}) collective-permute-start(bf16[96,1536]{1,0:T(8,128)(2,1)S(1)} %get-tuple-element.120), channel_id=1, source_target_pairs={{0,3},{1,0},{2,1},{3,2},{4,7},{5,4},{6,5},{7,6},{8,11},{9,8},{10,9... | collective-permute-start | bytes 884744 | tf_op jit(solution)/shard_map/ppermute | solution.py:47
  35.8 27.9 %collective-permute-start.5 = (bf16[96,1536]{1,0:T(8,128)(2,1)S(1)}, bf16[96,1536]{1,0:T(8,128)(2,1)S(1)}, u32[]{:S(2)}, u32[]{:S(2)}) collective-permute-start(bf16[96,1536]{1,0:T(8,128)(2,1)S(1)} %get-tuple-element.120), channel_id=1, source_target_pairs={{0,2},{1,3},{2,0},{3,1},{4,6},{5,7},{6,4},{7,5},{8,10},{9,11},{10,... | collective-permute-start | bytes 884744 | tf_op jit(solution)/shard_map/ppermute | solution.py:47
  38.3 25.3 %collective-permute-start.4 = (bf16[96,1536]{1,0:T(8,128)(2,1)S(1)}, bf16[96,1536]{1,0:T(8,128)(2,1)S(1)}, u32[]{:S(2)}, u32[]{:S(2)}) collective-permute-start(bf16[96,1536]{1,0:T(8,128)(2,1)S(1)} %get-tuple-element.120), channel_id=1, source_target_pairs={{0,1},{1,2},{2,3},{3,0},{4,5},{5,6},{6,7},{7,4},{8,9},{9,10},{10,1... | collective-permute-start | bytes 884744 | tf_op jit(solution)/shard_map/ppermute | solution.py:47
  66.0 224.1 %reduce-scatter.3.cloned.1.call-start = ((), (), s32[]{:S(2)}) async-start(), calls=%async_computation.4 | async-start | bytes 5308416 | tf_op jit(solution)/shard_map/reduce_scatter | solution.py:72
  67.3 25.1 %copy-start.11 = (bf16[512,768]{1,0:T(8,128)(2,1)}, bf16[512,768]{1,0:T(8,128)(2,1)S(1)}, u32[]{:S(2)}) copy-start(bf16[512,768]{1,0:T(8,128)(2,1)S(1)} %fusion.38) | copy-start | bytes 2359300
  67.3 18.4 %collective-permute-start.3 = (bf16[512,768]{1,0:T(8,128)(2,1)S(1)}, bf16[512,768]{1,0:T(8,128)(2,1)S(1)}, u32[]{:S(2)}, u32[]{:S(2)}) collective-permute-start(bf16[512,768]{1,0:T(8,128)(2,1)S(1)} %fusion.38), channel_id=1, source_target_pairs={{0,1},{1,0},{2,3},{3,2},{4,5},{5,4},{6,7},{7,6},{8,9},{9,8},{10,11... | collective-permute-start | bytes 2359304 | tf_op jit(solution)/shard_map/ppermute | solution.py:301
  74.7 14.4 %copy-start.10 = (bf16[768,3072]{1,0:T(8,128)(2,1)S(1)}, bf16[768,3072]{1,0:T(8,128)(2,1)}, u32[]{:S(2)}) copy-start(bf16[768,3072]{1,0:T(8,128)(2,1)} %all-gather.3.cloned.1.call-done) | copy-start | bytes 14155780
  85.7 5.1 %copy-start.27 = (bf16[512,768]{1,0:T(8,128)(2,1)}, bf16[512,768]{1,0:T(8,128)(2,1)S(1)}, u32[]{:S(2)}) copy-start(bf16[512,768]{1,0:T(8,128)(2,1)S(1)} %collective-permute-done.3) | copy-start | bytes 2359300
  115.4 43.9 %copy-start.2 = (f32[512,768]{1,0:T(8,128)}, f32[512,768]{1,0:T(8,128)S(1)}, u32[]{:S(2)}) copy-start(f32[512,768]{1,0:T(8,128)S(1)} %get-tuple-element.132) | copy-start | bytes 4718596
  115.7 38.2 %copy-start.4 = (bf16[512,768]{1,0:T(8,128)(2,1)S(1)}, bf16[512,768]{1,0:T(8,128)(2,1)}, u32[]{:S(2)}) copy-start(bf16[512,768]{1,0:T(8,128)(2,1)} %param.20) | copy-start | bytes 2359300
  135.3 18.7 %copy-start.25 = (bf16[768,6144]{1,0:T(8,128)(2,1)S(1)}, bf16[768,6144]{1,0:T(8,128)(2,1)}, u32[]{:S(2)}) copy-start(bf16[768,6144]{1,0:T(8,128)(2,1)} %all-gather.5.cloned.1.call-done) | copy-start | bytes 28311556
  165.4 4.7 %copy-start.1 = (f32[12,512,128]{2,1,0:T(8,128)S(1)}, f32[12,512,128]{2,1,0:T(8,128)}, u32[]{:S(2)}) copy-start(f32[12,512,128]{2,1,0:T(8,128)} %get-tuple-element.24.lse_ref) | copy-start | bytes 9437188
  168.9 23.0 %collective-permute-start.7 = (bf16[512,768]{1,0:T(8,128)(2,1)S(1)}, bf16[512,768]{1,0:T(8,128)(2,1)}, u32[]{:S(2)}, u32[]{:S(2)}) collective-permute-start(bf16[512,768]{1,0:T(8,128)(2,1)S(1)} %get-tuple-element.136.do_ref), channel_id=1, source_target_pairs={{1,0},{3,2},{5,4},{7,6},{9,8},{11,10},{13,12},{15,14},{17,16},{19,... | collective-permute-start | bytes 2359304 | tf_op jit(solution)/shard_map/ppermute | solution.py:337
  171.1 20.4 %collective-permute-start.8 = (f32[12,512]{1,0:T(8,128)S(1)}, f32[12,512]{1,0:T(8,128)S(1)}, u32[]{:S(2)}, u32[]{:S(2)}) collective-permute-start(f32[12,512]{1,0:T(8,128)S(1)} %slice_reduce_fusion), channel_id=1, source_target_pairs={{1,0},{3,2},{5,4},{7,6},{9,8},{11,10},{13,12},{15,14},{17,16},{19,... | collective-permute-start | bytes 73736 | tf_op jit(solution)/shard_map/ppermute | solution.py:310
  180.0 11.9 %collective-permute-start.9 = (f32[12,512]{1,0:T(8,128)S(1)}, f32[12,512]{1,0:T(8,128)S(1)}, u32[]{:S(2)}, u32[]{:S(2)}) collective-permute-start(f32[12,512]{1,0:T(8,128)S(1)} %bitcast.135), channel_id=1, source_target_pairs={{1,0},{3,2},{5,4},{7,6},{9,8},{11,10},{13,12},{15,14},{17,16},{19,... | collective-permute-start | bytes 73736 | tf_op jit(solution)/shard_map/ppermute | solution.py:337
  198.4 24.1 %copy-start.12 = (bf16[512,768]{1,0:T(8,128)(2,1)S(1)}, bf16[512,768]{1,0:T(8,128)(2,1)}, u32[]{:S(2)}) copy-start(bf16[512,768]{1,0:T(8,128)(2,1)} %copy-done.11) | copy-start | bytes 2359300
  222.6 3.8 copy-start.9
  229.2 133.9 %reduce-scatter.5.cloned.1.call-start = ((), (), s32[]{:S(2)}) async-start(), calls=%async_computation.5 | async-start | bytes 10616832 | tf_op jit(solution)/shard_map/reduce_scatter | solution.py:72
  277.2 11.7 %collective-permute-start.18 = (f32[9216]{0:T(1024)S(1)}, f32[9216]{0:T(1024)S(1)}, u32[]{:S(2)}, u32[]{:S(2)}) collective-permute-start(f32[9216]{0:T(1024)S(1)} %psum.7), channel_id=1, source_target_pairs={{0,3},{1,0},{2,1},{3,2},{4,7},{5,4},{6,5},{7,6},{8,11},{9,8},{10,9... | collective-permute-start | bytes 110600 | tf_op jit(solution)/shard_map/ppermute | solution.py:377
  278.2 10.6 %collective-permute-start.17 = (f32[9216]{0:T(1024)S(1)}, f32[9216]{0:T(1024)S(1)}, u32[]{:S(2)}, u32[]{:S(2)}) collective-permute-start(f32[9216]{0:T(1024)S(1)} %psum.7), channel_id=1, source_target_pairs={{0,2},{1,3},{2,0},{3,1},{4,6},{5,7},{6,4},{7,5},{8,10},{9,11},{10,... | collective-permute-start | bytes 110600 | tf_op jit(solution)/shard_map/ppermute | solution.py:377
  279.6 9.3 %collective-permute-start.16 = (f32[9216]{0:T(1024)S(1)}, f32[9216]{0:T(1024)S(1)}, u32[]{:S(2)}, u32[]{:S(2)}) collective-permute-start(f32[9216]{0:T(1024)S(1)} %psum.7), channel_id=1, source_target_pairs={{0,1},{1,2},{2,3},{3,0},{4,5},{5,6},{6,7},{7,4},{8,9},{9,10},{10,1... | collective-permute-start | bytes 110600 | tf_op jit(solution)/shard_map/ppermute | solution.py:377
  293.0 75.9 %collective-permute-start.12 = (bf16[96,768]{0,1:T(8,128)(2,1)}, bf16[96,768]{0,1:T(8,128)(2,1)}, u32[]{:S(2)}, u32[]{:S(2)}) collective-permute-start(bf16[96,768]{0,1:T(8,128)(2,1)} %get-tuple-element.103), channel_id=1, source_target_pairs={{0,3},{1,0},{2,1},{3,2},{4,7},{5,4},{6,5},{7,6},{8,11},{9,8},{10,9... | collective-permute-start | bytes 442376 | tf_op jit(solution)/shard_map/ppermute | solution.py:85
  294.9 75.1 %collective-permute-start.11 = (bf16[96,768]{0,1:T(8,128)(2,1)}, bf16[96,768]{0,1:T(8,128)(2,1)}, u32[]{:S(2)}, u32[]{:S(2)}) collective-permute-start(bf16[96,768]{0,1:T(8,128)(2,1)} %get-tuple-element.104), channel_id=1, source_target_pairs={{0,2},{1,3},{2,0},{3,1},{4,6},{5,7},{6,4},{7,5},{8,10},{9,11},{10,... | collective-permute-start | bytes 442376 | tf_op jit(solution)/shard_map/ppermute | solution.py:85
  294.9 75.1 %collective-permute-start.10 = (bf16[96,768]{0,1:T(8,128)(2,1)}, bf16[96,768]{0,1:T(8,128)(2,1)}, u32[]{:S(2)}, u32[]{:S(2)}) collective-permute-start(bf16[96,768]{0,1:T(8,128)(2,1)} %get-tuple-element.102), channel_id=1, source_target_pairs={{0,1},{1,2},{2,3},{3,0},{4,5},{5,6},{6,7},{7,4},{8,9},{9,10},{10,1... | collective-permute-start | bytes 442376 | tf_op jit(solution)/shard_map/ppermute | solution.py:85
  365.5 10.8 %collective-permute-start.15 = (bf16[96,1536]{1,0:T(8,128)(2,1)S(1)}, bf16[96,1536]{1,0:T(8,128)(2,1)S(1)}, u32[]{:S(2)}, u32[]{:S(2)}) collective-permute-start(bf16[96,1536]{1,0:T(8,128)(2,1)S(1)} %get-tuple-element.97), channel_id=1, source_target_pairs={{0,3},{1,0},{2,1},{3,2},{4,7},{5,4},{6,5},{7,6},{8,11},{9,8},{10,9... | collective-permute-start | bytes 884744 | tf_op jit(solution)/shard_map/ppermute | solution.py:85
  368.9 25.1 %collective-permute-start.14 = (bf16[96,1536]{1,0:T(8,128)(2,1)S(1)}, bf16[96,1536]{1,0:T(8,128)(2,1)S(1)}, u32[]{:S(2)}, u32[]{:S(2)}) collective-permute-start(bf16[96,1536]{1,0:T(8,128)(2,1)S(1)} %get-tuple-element.96), channel_id=1, source_target_pairs={{0,2},{1,3},{2,0},{3,1},{4,6},{5,7},{6,4},{7,5},{8,10},{9,11},{10,... | collective-permute-start | bytes 884744 | tf_op jit(solution)/shard_map/ppermute | solution.py:85
  368.9 25.1 %collective-permute-start.13 = (bf16[96,1536]{1,0:T(8,128)(2,1)S(1)}, bf16[96,1536]{1,0:T(8,128)(2,1)}, u32[]{:S(2)}, u32[]{:S(2)}) collective-permute-start(bf16[96,1536]{1,0:T(8,128)(2,1)S(1)} %get-tuple-element.95), channel_id=1, source_target_pairs={{0,1},{1,2},{2,3},{3,0},{4,5},{5,6},{6,7},{7,4},{8,9},{9,10},{10,1... | collective-permute-start | bytes 884744 | tf_op jit(solution)/shard_map/ppermute | solution.py:85
  (22 other events, 36.7 us)
Sparse Core Ops, SparseCore 0:
  35.4 39.2 all-gather.2
  76.5 58.6 all-gather.4
  229.3 53.6 reduce-scatter.2
  286.4 76.6 reduce-scatter.4

commit v10 on v9

--- a/solution.py
+++ b/solution.py
@@ -307,6 +307,7 @@
     v_oth = (dot_right(normed_oth, full_value) + b_value.astype(f32)).astype(bf16)
     q_rcv = (dot_right(normed_oth, full_query) + b_query.astype(f32)).astype(bf16)
     attended, o_full, lse_wide = attention_forward(meta, queries, key_rows, value_rows, k_oth, v_oth)
+    q_rcv, attended = lax.optimization_barrier((q_rcv, attended))
     lse_rcv = lax.ppermute(lse_wide[:, :, 0], "tensor", to_first)
 
     middle = in_rows + dot_back(attended, out_t) + b_out.astype(f32)
@@ -372,9 +373,14 @@
         norm_two_back[2],
     ]
     joined = lax.psum(jnp.concatenate(vectors), "dp")
-    total = joined
-    for step in range(1, tp):
-        total = total + lax.ppermute(joined, "tensor", [(i, (i + step) % tp) for i in range(tp)])
+    pieces = [joined] + [
+        lax.ppermute(joined, "tensor", [(i, (i + step) % tp) for i in range(tp)]) for step in range(1, tp)
+    ]
+    t_index = lax.axis_index("tensor")
+    by_source = jnp.take(jnp.stack(pieces), (t_index - jnp.arange(tp, dtype=jnp.int32)) % tp, axis=0)
+    total = by_source[0]
+    for source in range(1, tp):
+        total = total + by_source[source]
     vector_sums = []
     start = 0
     for v in vectors:

time: 409 us -> 409 us (level)
  transfers between devices with their start and end apart: 23 -> 23, of which waited for: 12 -> 12; matrix products, arithmetic and copies ran while one was open for 17% -> 18% of each run, Pallas kernels for 5% -> 5%
where the time goes in v10:
time: 409 us; the launch traced here: 403 us
  waiting for transfers between devices  166 us (41%)
  matrix products  77.9 us (19%)
  Pallas kernels  43 us (11%)
  local copies, waits for them, and re-layouts  28.7 us (7%)
  starting transfers between devices  26.4 us (6%)
  blocking collectives  24.6 us (6%)
  other arithmetic  21.2 us (5%)
  between operations  14.8 us (4%)
    reduce_scatter x2, waiting for transfers between devices, scatter_rows(): lax.psum_scatter(grad.astype(LINK), 'dp', scatter_dimension=axis, tiled=T...  66.6 us
    dot_general x9, matrix products, dot_right(): return jnp.dot(first_op, second_op, preferred_element_type=jnp.float32)  41.8 us
    ppermute x6, waiting for transfers between devices, gather_joined(): lax.ppermute(joined, 'tensor', [(i, (i + step) % tp) for i in range(tp)])  39 us
    psum x1, blocking collectives, layer(): joined = lax.psum(jnp.concatenate(vectors), 'dp')  24.6 us
    pallas_call x1, Pallas kernels, attention_backward(): pl.pallas_call(attn_bwd_kernel, out_shape=tuple((jax.ShapeDtypeStruct(q.s...  24.1 us
    all_gather x2, waiting for transfers between devices, gather_joined(): lax.all_gather(jnp.concatenate(strips, axis=1), 'dp', axis=0, tiled=True)  22.2 us
    ppermute x6, waiting for transfers between devices, sum_over_tensor(): lax.ppermute(sent, 'tensor', [(i, (i + step) % tp) for i in range(tp)])  19.9 us
    dot_general x6, matrix products, dot_back(): lax.dot_general(first_op, second_op, (((1,), (1,)), ((), ())), preferred_...  19.2 us
  transfers between devices with their start and end apart: 23, of which 12 were waited for; matrix products, arithmetic and copies ran while one was open for 18% of the time, Pallas kernels for 5%

profile of v10, /device:TPU:0, one launch (start us, length us, event | category | flops | bytes accessed | tf_op | source)
XLA Modules:
  0.0 402.7 jit_solution(8182909340002161779)
XLA Ops:
  10.8 5.1 %collective-permute-start.3 = (bf16[96,768]{0,1:T(8,128)(2,1)S(1)}, bf16[96,768]{0,1:T(8,128)(2,1)S(1)}, u32[]{:S(2)}, u32[]{:S(2)}) collective-permute-start(bf16[96,768]{0,1:T(8,128)(2,1)S(1)} %get-tuple-element.134), channel_id=1, source_target_pairs={{0,3},{1,0},{2,1},{3,2},{4,7},{5,4},{6,5},{7,6},{8,11},{9,8},{10,9... | collective-permute-start | bytes 442376 | tf_op jit(solution)/shard_map/ppermute | solution.py:47
  17.0 4.3 %collective-permute-done.3 = bf16[96,768]{0,1:T(8,128)(2,1)S(1)} collective-permute-done((bf16[96,768]{0,1:T(8,128)(2,1)S(1)}, bf16[96,768]{0,1:T(8,128)(2,1)S(1)}, u32[]{:S(2)}, u32[]{:S(2)}) %collective-permute-start.3) | collective-permute-done | bytes 147488 | tf_op jit(solution)/shard_map/ppermute | solution.py:47
  21.3 11.4 %collective-permute-done.2 = bf16[96,768]{0,1:T(8,128)(2,1)S(1)} collective-permute-done((bf16[96,768]{0,1:T(8,128)(2,1)S(1)}, bf16[96,768]{0,1:T(8,128)(2,1)S(1)}, u32[]{:S(2)}, u32[]{:S(2)}) %collective-permute-start.2) | collective-permute-done | bytes 147488 | tf_op jit(solution)/shard_map/ppermute | solution.py:47
  35.8 2.6 collective-permute-start.5
  40.3 3.4 collective-permute-done.6
  43.6 20.0 %collective-permute-done.5 = bf16[96,1536]{1,0:T(8,128)(2,1)S(1)} collective-permute-done((bf16[96,1536]{1,0:T(8,128)(2,1)S(1)}, bf16[96,1536]{1,0:T(8,128)(2,1)S(1)}, u32[]{:S(2)}, u32[]{:S(2)}) %collective-permute-start.5) | collective-permute-done | bytes 294944 | tf_op jit(solution)/shard_map/ppermute | solution.py:47
  69.4 5.3 %all-gather.3.cloned.1.call-done = bf16[768,3072]{1,0:T(8,128)(2,1)} async-done(((bf16[96,3072]{1,0:T(8,128)(2,1)}), bf16[768,3072]{1,0:T(8,128)(2,1)}) %all-gather.3.cloned.1.call-update) | async-done | bytes 4718608 | tf_op jit(solution)/shard_map/all_gather | solution.py:58
  74.7 3.1 convolution_convert_fusion.5.k_ref
  77.8 7.9 %collective-permute-done = bf16[512,768]{1,0:T(8,128)(2,1)S(1)} collective-permute-done((bf16[512,768]{1,0:T(8,128)(2,1)S(1)}, bf16[512,768]{1,0:T(8,128)(2,1)S(1)}, u32[]{:S(2)}, u32[]{:S(2)}) %collective-permute-start) | collective-permute-done | bytes 786464 | tf_op jit(solution)/shard_map/ppermute | solution.py:301
  85.7 3.2 convolution_convert_fusion.4.ko_ref
  93.9 18.9 %shard_map.305 = (bf16[512,768]{1,0:T(8,128)(2,1)}, f32[512,768]{1,0:T(8,128)}, f32[12,512,128]{2,1,0:T(8,128)}) custom-call(s32[2]{0:T(128)} %pad_add_fusion.meta_ref, bf16[512,768]{1,0:T(8,128)(2,1)} %add_convert_fusion.4.q_ref, bf16[512,768]{1,0:T(8,128)(2,1)} %convolution_convert_fusion.5.k_ref, bf16[512,768]{1,0:T(8,128)(2,1)} %add_convert_fusion.3.v_ref, ...), custom_call_target="tpu_custom_call" | custom-call | flops 1610612736 | bytes 9437184 | tf_op jit(solution)/shard_map/pallas_call | solution.py:213
  112.8 3.1 add_convert_fusion.5.qr_ref
  118.4 16.9 %all-gather.5.cloned.1.call-done = bf16[768,6144]{1,0:T(8,128)(2,1)} async-done(((bf16[96,6144]{1,0:T(8,128)(2,1)}), bf16[768,6144]{1,0:T(8,128)(2,1)}) %all-gather.5.cloned.1.call-update) | async-done | bytes 9437200 | tf_op jit(solution)/shard_map/all_gather | solution.py:58
  135.3 18.7 %multiply_convert_fusion = (bf16[512,3072]{1,0:T(8,128)(2,1)}, f32[512,3072]{1,0:T(8,128)S(1)}, f32[512,3072]{1,0:T(8,128)S(1)}) fusion(f32[3072]{0:T(1024)S(1)} %convert_element_type.136, bf16[768,6144]{1,0:T(8,128)(2,1)} %all-gather.5.cloned.1.call-done, f32[512,768]{1,0:T(8,128)S(1)} %get-tuple-element.136, f32[768]{0:T(1024)S(1)} %convert_element_type.134, ...), kind=kOutput, calls=%fused_computation.19 | convolution fusion | flops 2521694208 | bytes 22042624 | tf_op jit(solution)/shard_map/dot_general | solution.py:28
  154.0 5.3 %convert_reduce_fusion = (f32[3072]{0:T(1024)S(1)}, bf16[512,3072]{1,0:T(8,128)(2,1)S(1)}) fusion(f32[512,3072]{1,0:T(8,128)S(1)} %get-tuple-element.104, bf16[512,768]{1,0:T(8,128)(2,1)S(1)} %copy-done.4, bf16[768,6144]{1,0:T(8,128)(2,1)S(1)} %copy-done.25, f32[512,3072]{1,0:T(8,128)S(1)} %get-tuple-element.137, f32[3072]{0:T(1024)S(1)} %convert_element_type.136), kind=kOutput, calls=%fused_computation.18 | convolution fusion | flops 2442654720 | bytes 21258240 | tf_op jit(solution)/shard_map/dot_general | solution.py:28
  159.3 3.0 multiply_reduce_fusion
  162.3 3.2 fusion.91
  165.5 3.4 convert_multiply_fusion
  172.4 3.1 copy.75
  178.4 3.3 convolution_convert_fusion.2
  181.7 9.9 %collective-permute-done.8 = f32[12,512]{1,0:T(8,128)S(1)} collective-permute-done((f32[12,512]{1,0:T(8,128)S(1)}, f32[12,512]{1,0:T(8,128)S(1)}, u32[]{:S(2)}, u32[]{:S(2)}) %collective-permute-start.8) | collective-permute-done | bytes 24608 | tf_op jit(solution)/shard_map/ppermute | solution.py:311
  198.4 24.1 %shard_map.306 = (bf16[512,768]{1,0:T(8,128)(2,1)}, bf16[512,768]{1,0:T(8,128)(2,1)}, bf16[512,768]{1,0:T(8,128)(2,1)}) custom-call(s32[2]{0:T(128)} %pad_add_fusion.meta_ref, bf16[512,768]{1,0:T(8,128)(2,1)} %add_convert_fusion.4.q_ref, bf16[512,768]{1,0:T(8,128)(2,1)} %convolution_convert_fusion.5.k_ref, bf16[512,768]{1,0:T(8,128)(2,1)} %add_convert_fusion.3.v_ref, ...), custom_call_target="tpu_custom_call" | custom-call | flops 4026531840 | bytes 21233664 | tf_op jit(solution)/shard_map/pallas_call | solution.py:239
  222.5 3.7 convolution_convert_fusion.1
  226.3 2.9 pad_maximum_fusion
  230.3 9.9 %convolution_convert_fusion = bf16[2,768,3072]{2,1,0:T(8,128)(2,1)} fusion(bf16[1,512,3072]{2,1,0:T(8,128)(2,1)} %bitcast.148, bf16[1,512,3072]{2,1,0:T(8,128)(2,1)} %bitcast.149, bf16[1,512,768]{2,1,0:T(8,128)(2,1)S(1)} %bitcast.122, bf16[1,512,768]{2,1,0:T(8,128)(2,1)} %get-tuple-element.106), kind=kOutput, calls=%fused_computation.4 | convolution fusion | flops 4840488960 | bytes 17301504 | tf_op jit(solution)/shard_map/dot_general | solution.py:322
  247.1 2.4 fusion.90
  252.4 24.6 %psum.7 = f32[9216]{0:T(1024)S(1)} all-reduce(f32[9216]{0:T(1024)S(1)} %constant_dynamic-update-slice_fusion), channel_id=1, replica_groups=mesh['dp'=8,'tensor'=4] {'dp'}, use_global_device_ids=true, to_apply=%region_20.21 | all-reduce | flops 9216 | bytes 73728 | tf_op jit(solution)/shard_map/psum | solution.py:375
  281.5 7.3 %add_convert_fusion = bf16[512,768]{1,0:T(8,128)(2,1)} fusion(f32[512,768]{1,0:T(8,128)} %copy-done.2, bf16[512,3072]{1,0:T(8,128)(2,1)} %get-tuple-element.103, bf16[768,6144]{1,0:T(8,128)(2,1)} %all-gather.5.cloned.1.call-done, f32[768]{0:T(1024)S(1)} %convert_element_type.138), kind=kOutput, calls=%fused_computation.86 | convolution fusion | flops 2417098752 | bytes 10226688 | tf_op jit(solution)/shard_map/dot_general | solution.py:32
  296.4 66.6 %reduce-scatter.5.cloned.1.call-done = bf16[2,96,3072]{2,1,0:T(8,128)(2,1)} async-done(((bf16[2,768,3072]{2,1,0:T(8,128)(2,1)}), bf16[2,96,3072]{2,1,0:T(8,128)(2,1)}) %reduce-scatter.5.cloned.1.call-update) | async-done | bytes 1179664 | tf_op jit(solution)/shard_map/reduce_scatter | solution.py:72
  365.4 3.4 collective-permute-start.15
  374.0 2.2 collective-permute-done.15
  376.3 17.7 %collective-permute-done.14 = bf16[96,1536]{1,0:T(8,128)(2,1)S(1)} collective-permute-done((bf16[96,1536]{1,0:T(8,128)(2,1)S(1)}, bf16[96,1536]{1,0:T(8,128)(2,1)S(1)}, u32[]{:S(2)}, u32[]{:S(2)}) %collective-permute-start.14) | collective-permute-done | bytes 294944 | tf_op jit(solution)/shard_map/ppermute | solution.py:85
  (192 shorter events, 68.1 us)
Async XLA Ops:
  7.2 67.5 %all-gather.3.cloned.1.call-start = ((), (), s32[]{:S(2)}) async-start(), calls=%async_computation.2 | async-start | bytes 5308416 | tf_op jit(solution)/shard_map/all_gather | solution.py:58
  10.8 10.5 %collective-permute-start.3 = (bf16[96,768]{0,1:T(8,128)(2,1)S(1)}, bf16[96,768]{0,1:T(8,128)(2,1)S(1)}, u32[]{:S(2)}, u32[]{:S(2)}) collective-permute-start(bf16[96,768]{0,1:T(8,128)(2,1)S(1)} %get-tuple-element.134), channel_id=1, source_target_pairs={{0,3},{1,0},{2,1},{3,2},{4,7},{5,4},{6,5},{7,6},{8,11},{9,8},{10,9... | collective-permute-start | bytes 442376 | tf_op jit(solution)/shard_map/ppermute | solution.py:47
  16.0 16.7 %collective-permute-start.2 = (bf16[96,768]{0,1:T(8,128)(2,1)S(1)}, bf16[96,768]{0,1:T(8,128)(2,1)S(1)}, u32[]{:S(2)}, u32[]{:S(2)}) collective-permute-start(bf16[96,768]{0,1:T(8,128)(2,1)S(1)} %get-tuple-element.134), channel_id=1, source_target_pairs={{0,2},{1,3},{2,0},{3,1},{4,6},{5,7},{6,4},{7,5},{8,10},{9,11},{10,... | collective-permute-start | bytes 442376 | tf_op jit(solution)/shard_map/ppermute | solution.py:47
  16.0 16.7 %collective-permute-start.1 = (bf16[96,768]{0,1:T(8,128)(2,1)S(1)}, bf16[96,768]{0,1:T(8,128)(2,1)S(1)}, u32[]{:S(2)}, u32[]{:S(2)}) collective-permute-start(bf16[96,768]{0,1:T(8,128)(2,1)S(1)} %get-tuple-element.134), channel_id=1, source_target_pairs={{0,1},{1,2},{2,3},{3,0},{4,5},{5,6},{6,7},{7,4},{8,9},{9,10},{10,1... | collective-permute-start | bytes 442376 | tf_op jit(solution)/shard_map/ppermute | solution.py:47
  35.3 100.0 %all-gather.5.cloned.1.call-start = ((), (), s32[]{:S(2)}) async-start(), calls=%async_computation.3 | async-start | bytes 10616832 | tf_op jit(solution)/shard_map/all_gather | solution.py:58
  35.4 8.2 %collective-permute-start.6 = (bf16[96,1536]{1,0:T(8,128)(2,1)S(1)}, bf16[96,1536]{1,0:T(8,128)(2,1)S(1)}, u32[]{:S(2)}, u32[]{:S(2)}) collective-permute-start(bf16[96,1536]{1,0:T(8,128)(2,1)S(1)} %get-tuple-element.132), channel_id=1, source_target_pairs={{0,3},{1,0},{2,1},{3,2},{4,7},{5,4},{6,5},{7,6},{8,11},{9,8},{10,9... | collective-permute-start | bytes 884744 | tf_op jit(solution)/shard_map/ppermute | solution.py:47
  35.8 27.9 %collective-permute-start.5 = (bf16[96,1536]{1,0:T(8,128)(2,1)S(1)}, bf16[96,1536]{1,0:T(8,128)(2,1)S(1)}, u32[]{:S(2)}, u32[]{:S(2)}) collective-permute-start(bf16[96,1536]{1,0:T(8,128)(2,1)S(1)} %get-tuple-element.132), channel_id=1, source_target_pairs={{0,2},{1,3},{2,0},{3,1},{4,6},{5,7},{6,4},{7,5},{8,10},{9,11},{10,... | collective-permute-start | bytes 884744 | tf_op jit(solution)/shard_map/ppermute | solution.py:47
  38.3 25.3 %collective-permute-start.4 = (bf16[96,1536]{1,0:T(8,128)(2,1)S(1)}, bf16[96,1536]{1,0:T(8,128)(2,1)S(1)}, u32[]{:S(2)}, u32[]{:S(2)}) collective-permute-start(bf16[96,1536]{1,0:T(8,128)(2,1)S(1)} %get-tuple-element.132), channel_id=1, source_target_pairs={{0,1},{1,2},{2,3},{3,0},{4,5},{5,6},{6,7},{7,4},{8,9},{9,10},{10,1... | collective-permute-start | bytes 884744 | tf_op jit(solution)/shard_map/ppermute | solution.py:47
  66.0 225.1 %reduce-scatter.3.cloned.1.call-start = ((), (), s32[]{:S(2)}) async-start(), calls=%async_computation.4 | async-start | bytes 5308416 | tf_op jit(solution)/shard_map/reduce_scatter | solution.py:72
  67.3 24.9 %copy-start.11 = (bf16[512,768]{1,0:T(8,128)(2,1)}, bf16[512,768]{1,0:T(8,128)(2,1)S(1)}, u32[]{:S(2)}) copy-start(bf16[512,768]{1,0:T(8,128)(2,1)S(1)} %fusion.38) | copy-start | bytes 2359300
  67.3 18.4 %collective-permute-start = (bf16[512,768]{1,0:T(8,128)(2,1)S(1)}, bf16[512,768]{1,0:T(8,128)(2,1)S(1)}, u32[]{:S(2)}, u32[]{:S(2)}) collective-permute-start(bf16[512,768]{1,0:T(8,128)(2,1)S(1)} %fusion.38), channel_id=1, source_target_pairs={{0,1},{1,0},{2,3},{3,2},{4,5},{5,4},{6,7},{7,6},{8,9},{9,8},{10,11... | collective-permute-start | bytes 2359304 | tf_op jit(solution)/shard_map/ppermute | solution.py:301
  74.7 14.2 %copy-start.10 = (bf16[768,3072]{1,0:T(8,128)(2,1)S(1)}, bf16[768,3072]{1,0:T(8,128)(2,1)}, u32[]{:S(2)}) copy-start(bf16[768,3072]{1,0:T(8,128)(2,1)} %all-gather.3.cloned.1.call-done) | copy-start | bytes 14155780
  118.0 41.3 %copy-start.2 = (f32[512,768]{1,0:T(8,128)}, f32[512,768]{1,0:T(8,128)S(1)}, u32[]{:S(2)}) copy-start(f32[512,768]{1,0:T(8,128)S(1)} %get-tuple-element.136) | copy-start | bytes 4718596
  118.3 35.7 %copy-start.4 = (bf16[512,768]{1,0:T(8,128)(2,1)S(1)}, bf16[512,768]{1,0:T(8,128)(2,1)}, u32[]{:S(2)}) copy-start(bf16[512,768]{1,0:T(8,128)(2,1)} %param.20) | copy-start | bytes 2359300
  135.3 18.7 %copy-start.25 = (bf16[768,6144]{1,0:T(8,128)(2,1)S(1)}, bf16[768,6144]{1,0:T(8,128)(2,1)}, u32[]{:S(2)}) copy-start(bf16[768,6144]{1,0:T(8,128)(2,1)} %all-gather.5.cloned.1.call-done) | copy-start | bytes 28311556
  162.3 3.2 copy-start.5
  165.5 4.7 %copy-start.1 = (f32[12,512,128]{2,1,0:T(8,128)S(1)}, f32[12,512,128]{2,1,0:T(8,128)}, u32[]{:S(2)}) copy-start(f32[12,512,128]{2,1,0:T(8,128)} %get-tuple-element.27.lse_ref) | copy-start | bytes 9437188
  168.9 23.0 %collective-permute-start.7 = (bf16[512,768]{1,0:T(8,128)(2,1)S(1)}, bf16[512,768]{1,0:T(8,128)(2,1)}, u32[]{:S(2)}, u32[]{:S(2)}) collective-permute-start(bf16[512,768]{1,0:T(8,128)(2,1)S(1)} %get-tuple-element.140.do_ref), channel_id=1, source_target_pairs={{1,0},{3,2},{5,4},{7,6},{9,8},{11,10},{13,12},{15,14},{17,16},{19,... | collective-permute-start | bytes 2359304 | tf_op jit(solution)/shard_map/ppermute | solution.py:338
  171.1 20.5 %collective-permute-start.8 = (f32[12,512]{1,0:T(8,128)S(1)}, f32[12,512]{1,0:T(8,128)S(1)}, u32[]{:S(2)}, u32[]{:S(2)}) collective-permute-start(f32[12,512]{1,0:T(8,128)S(1)} %slice_reduce_fusion), channel_id=1, source_target_pairs={{1,0},{3,2},{5,4},{7,6},{9,8},{11,10},{13,12},{15,14},{17,16},{19,... | collective-permute-start | bytes 73736 | tf_op jit(solution)/shard_map/ppermute | solution.py:311
  177.1 14.8 %collective-permute-start.9 = (f32[12,512]{1,0:T(8,128)S(1)}, f32[12,512]{1,0:T(8,128)S(1)}, u32[]{:S(2)}, u32[]{:S(2)}) collective-permute-start(f32[12,512]{1,0:T(8,128)S(1)} %bitcast.141), channel_id=1, source_target_pairs={{1,0},{3,2},{5,4},{7,6},{9,8},{11,10},{13,12},{15,14},{17,16},{19,... | collective-permute-start | bytes 73736 | tf_op jit(solution)/shard_map/ppermute | solution.py:338
  198.4 24.1 %copy-start.12 = (bf16[512,768]{1,0:T(8,128)(2,1)S(1)}, bf16[512,768]{1,0:T(8,128)(2,1)}, u32[]{:S(2)}) copy-start(bf16[512,768]{1,0:T(8,128)(2,1)} %copy-done.11) | copy-start | bytes 2359300
  222.5 3.8 copy-start.9
  229.2 133.9 %reduce-scatter.5.cloned.1.call-start = ((), (), s32[]{:S(2)}) async-start(), calls=%async_computation.5 | async-start | bytes 10616832 | tf_op jit(solution)/shard_map/reduce_scatter | solution.py:72
  276.9 11.9 %collective-permute-start.18 = (f32[9216]{0:T(1024)S(1)}, f32[9216]{0:T(1024)S(1)}, u32[]{:S(2)}, u32[]{:S(2)}) collective-permute-start(f32[9216]{0:T(1024)S(1)} %psum.7), channel_id=1, source_target_pairs={{0,3},{1,0},{2,1},{3,2},{4,7},{5,4},{6,5},{7,6},{8,11},{9,8},{10,9... | collective-permute-start | bytes 110600 | tf_op jit(solution)/shard_map/ppermute | solution.py:377
  278.2 10.6 %collective-permute-start.17 = (f32[9216]{0:T(1024)S(1)}, f32[9216]{0:T(1024)S(1)}, u32[]{:S(2)}, u32[]{:S(2)}) collective-permute-start(f32[9216]{0:T(1024)S(1)} %psum.7), channel_id=1, source_target_pairs={{0,2},{1,3},{2,0},{3,1},{4,6},{5,7},{6,4},{7,5},{8,10},{9,11},{10,... | collective-permute-start | bytes 110600 | tf_op jit(solution)/shard_map/ppermute | solution.py:377
  279.6 9.3 %collective-permute-start.16 = (f32[9216]{0:T(1024)S(1)}, f32[9216]{0:T(1024)S(1)}, u32[]{:S(2)}, u32[]{:S(2)}) collective-permute-start(f32[9216]{0:T(1024)S(1)} %psum.7), channel_id=1, source_target_pairs={{0,1},{1,2},{2,3},{3,0},{4,5},{5,6},{6,7},{7,4},{8,9},{9,10},{10,1... | collective-permute-start | bytes 110600 | tf_op jit(solution)/shard_map/ppermute | solution.py:377
  294.2 74.6 %collective-permute-start.12 = (bf16[96,768]{0,1:T(8,128)(2,1)}, bf16[96,768]{0,1:T(8,128)(2,1)}, u32[]{:S(2)}, u32[]{:S(2)}) collective-permute-start(bf16[96,768]{0,1:T(8,128)(2,1)} %get-tuple-element.115), channel_id=1, source_target_pairs={{0,3},{1,0},{2,1},{3,2},{4,7},{5,4},{6,5},{7,6},{8,11},{9,8},{10,9... | collective-permute-start | bytes 442376 | tf_op jit(solution)/shard_map/ppermute | solution.py:85
  295.8 74.1 %collective-permute-start.11 = (bf16[96,768]{0,1:T(8,128)(2,1)}, bf16[96,768]{0,1:T(8,128)(2,1)}, u32[]{:S(2)}, u32[]{:S(2)}) collective-permute-start(bf16[96,768]{0,1:T(8,128)(2,1)} %get-tuple-element.116), channel_id=1, source_target_pairs={{0,2},{1,3},{2,0},{3,1},{4,6},{5,7},{6,4},{7,5},{8,10},{9,11},{10,... | collective-permute-start | bytes 442376 | tf_op jit(solution)/shard_map/ppermute | solution.py:85
  295.9 74.1 %collective-permute-start.10 = (bf16[96,768]{0,1:T(8,128)(2,1)}, bf16[96,768]{0,1:T(8,128)(2,1)}, u32[]{:S(2)}, u32[]{:S(2)}) collective-permute-start(bf16[96,768]{0,1:T(8,128)(2,1)} %get-tuple-element.114), channel_id=1, source_target_pairs={{0,1},{1,2},{2,3},{3,0},{4,5},{5,6},{6,7},{7,4},{8,9},{9,10},{10,1... | collective-permute-start | bytes 442376 | tf_op jit(solution)/shard_map/ppermute | solution.py:85
  365.4 10.8 %collective-permute-start.15 = (bf16[96,1536]{1,0:T(8,128)(2,1)S(1)}, bf16[96,1536]{1,0:T(8,128)(2,1)S(1)}, u32[]{:S(2)}, u32[]{:S(2)}) collective-permute-start(bf16[96,1536]{1,0:T(8,128)(2,1)S(1)} %get-tuple-element.109), channel_id=1, source_target_pairs={{0,3},{1,0},{2,1},{3,2},{4,7},{5,4},{6,5},{7,6},{8,11},{9,8},{10,9... | collective-permute-start | bytes 884744 | tf_op jit(solution)/shard_map/ppermute | solution.py:85
  368.8 25.1 %collective-permute-start.14 = (bf16[96,1536]{1,0:T(8,128)(2,1)S(1)}, bf16[96,1536]{1,0:T(8,128)(2,1)S(1)}, u32[]{:S(2)}, u32[]{:S(2)}) collective-permute-start(bf16[96,1536]{1,0:T(8,128)(2,1)S(1)} %get-tuple-element.108), channel_id=1, source_target_pairs={{0,2},{1,3},{2,0},{3,1},{4,6},{5,7},{6,4},{7,5},{8,10},{9,11},{10,... | collective-permute-start | bytes 884744 | tf_op jit(solution)/shard_map/ppermute | solution.py:85
  368.8 25.1 %collective-permute-start.13 = (bf16[96,1536]{1,0:T(8,128)(2,1)S(1)}, bf16[96,1536]{1,0:T(8,128)(2,1)}, u32[]{:S(2)}, u32[]{:S(2)}) collective-permute-start(bf16[96,1536]{1,0:T(8,128)(2,1)S(1)} %get-tuple-element.107), channel_id=1, source_target_pairs={{0,1},{1,2},{2,3},{3,0},{4,5},{5,6},{6,7},{7,4},{8,9},{9,10},{10,1... | collective-permute-start | bytes 884744 | tf_op jit(solution)/shard_map/ppermute | solution.py:85
  (21 other events, 34.4 us)
Sparse Core Ops, SparseCore 0:
  35.4 39.2 all-gather.2
  76.5 58.6 all-gather.4
  229.3 53.6 reduce-scatter.2
  286.4 76.6 reduce-scatter.4
